TPU v7x, 256 devices: a whole 4x4x8 slice. The times are simulated.
256 devices in a mesh: blk: 8 (over y, x_hi), grp: 32 (over x_lo, z, core).
Axes of the slice: x: 4 (x_hi: 2, x_lo: 2; x = x_hi * 2 + x_lo), y: 4, z: 8, core: 2. Of those that a mesh axis runs over, the one named last changes fastest.
Arguments:
- position: float32 [3, 65536], P(None, ('blk', 'grp'))
- velocity: float32 [3, 65536], P(None, ('blk', 'grp')), may hold values from -3 to 3
- accel_old: float32 [3, 65536], P(None, ('blk', 'grp')), may hold values from -5 to 5
- jerk_old: float32 [3, 65536], P(None, ('blk', 'grp')), may hold values from -5 to 5
- elapsed: float32 [65536], P(('blk', 'grp')), may hold values from 0.01 to 0.1
- masses: float32 [65536], P(('blk', 'grp'))
- active_stars: int32 [8192], P(('blk', 'grp')), may hold values from 0 to 255, as said below
- neighbour_list: int32 [256, 64], P(('blk', 'grp')), may hold values from 0 to 63, as said below
- neighbour_count: int32 [256], P(('blk', 'grp')), may hold values from 1 to 64, as said below
Outputs:
- regular: float32 [6, 8192], P(None, ('blk', 'grp'))
- irregular: float32 [6, 8192], P(None, ('blk', 'grp'))
- correction: float32 [6, 8192], P(None, ('blk', 'grp'))
Inputs may be any that keep to these rules, and one draw needn't show every extreme that they name: `active_stars`: the 32 entries of one device are distinct local indices of that device's stars, all inside one block of 128 of them. `neighbour_list`: row r lists neighbour blocks for the active stars of device r, numbered within r's group (2 blocks a device, devices in grp order). Its first neighbour_count[r] entries are distinct and ascending, at most 2 of them from one device, and include the block that holds r's active stars; later entries mean nothing. `neighbour_count`: in every group along blk some device lists 2 blocks of every device of its group.
All inputs are finite; a program needn't handle non-finite values.
Results may differ from a plain program's by a relative error of at most 0.0003.
Values sent between devices are 32-bit elements; how exact they have to be, the bound alone decides.
No kernel may reach another device: no remote copies, remote signals or barrier semaphores. Data moves between devices by JAX's collectives and lax.ppermute only.
A program may use at most 64 MiB of HBM per device.

v0:
```python
import jax
import jax.numpy as jnp
from jax import lax
from jax.sharding import PartitionSpec as P

BLOCK = 128


soften_sq = 0.0001


def shifted(block, axis, distance):
    devices = range(lax.axis_size(axis))
    route = [((i - distance) % len(devices), i) for i in devices]
    return lax.ppermute(block, axis, route)


def pair_sums(targets, sources, weight):
    gap_x = sources[0][None, :] - targets[0][:, None]
    gap_y = sources[1][None, :] - targets[1][:, None]
    gap_z = sources[2][None, :] - targets[2][:, None]
    rel_x = sources[3][None, :] - targets[3][:, None]
    rel_y = sources[4][None, :] - targets[4][:, None]
    rel_z = sources[5][None, :] - targets[5][:, None]
    dist_sq = gap_x * gap_x + gap_y * gap_y + gap_z * gap_z + soften_sq
    inverse = lax.rsqrt(dist_sq)
    scaled = weight * (inverse * inverse * inverse)
    radial = 3.0 * (gap_x * rel_x + gap_y * rel_y + gap_z * rel_z) / dist_sq
    term_list = [
        gap_x,
        gap_y,
        gap_z,
        rel_x - radial * gap_x,
        rel_y - radial * gap_y,
        rel_z - radial * gap_z,
    ]
    return jnp.stack([jnp.sum(scaled * term, axis=1) for term in term_list])


def per_device(
    position,
    velocity,
    accel_old,
    jerk_old,
    elapsed,
    masses,
    active_stars,
    neighbour_list,
    neighbour_count,
):
    moved_pos = position + elapsed * (
        velocity + elapsed * (0.5 * accel_old + elapsed * jerk_old / 6.0)
    )
    turned = velocity + elapsed * (accel_old + 0.5 * elapsed * jerk_old)
    sources = jnp.concatenate([moved_pos, turned], axis=0)
    own_set = jnp.take(sources, active_stars, axis=1)
    act_dev = active_stars.shape[0]
    res_dev = position.shape[1]
    blk_dev = res_dev // BLOCK
    group_set = lax.all_gather(own_set, "grp", axis=1, tiled=True)
    all_lists, all_counts = (
        lax.all_gather(neighbour_list, "grp", axis=0, tiled=True),
        lax.all_gather(neighbour_count, "grp", axis=0, tiled=True),
    )
    blk_size = lax.axis_size("blk")
    my_index = lax.axis_index("grp")
    slot_total = all_lists.shape[1]
    in_list = jnp.arange(slot_total)[None, :] < all_counts[:, None]
    my_blocks = my_index * blk_dev + jnp.arange(blk_dev)
    listed = jnp.any(
        in_list[:, :, None] & (all_lists[:, :, None] == my_blocks[None, None, :]), axis=1
    )
    keep_home = 1.0 - listed.astype(jnp.float32)
    keep_all = jnp.ones_like(keep_home)
    set_size = group_set.shape[1]
    piece_rows = min(512, set_size)
    piece_count = set_size // piece_rows
    owners_piece = piece_rows // act_dev
    blk_here = lax.axis_index("blk")
    moving = group_set
    partial_terms = jnp.zeros((6, blk_size * set_size), jnp.float32)
    for step in range(blk_size):
        target_pieces = moving.reshape(6, piece_count, piece_rows).transpose(1, 0, 2)
        keep_pieces = (keep_home if step == 0 else keep_all).reshape(
            piece_count, owners_piece, blk_dev
        )

        def one_piece(items):
            target_piece, keep_piece = items
            weight = (
                jnp.repeat(jnp.repeat(keep_piece, act_dev, axis=0), BLOCK, axis=1) * masses[None, :]
            )
            return pair_sums(target_piece, sources, weight)

        sums = lax.map(one_piece, (target_pieces, keep_pieces))
        contribution = sums.transpose(1, 0, 2).reshape(6, set_size)
        anchor = (blk_here - step) % blk_size
        partial_terms = lax.dynamic_update_slice_in_dim(
            partial_terms, contribution, anchor * set_size, 1
        )
        if step + 1 < blk_size:
            moving = shifted(moving, "blk", 1)
    regular = lax.psum_scatter(partial_terms, ("blk", "grp"), scatter_dimension=1, tiled=True)
    block_data = jnp.concatenate([sources, masses[None, :]], axis=0).reshape(7, blk_dev, BLOCK)
    own_list = neighbour_list[0]
    own_live = jnp.arange(slot_total) < neighbour_count[0]
    everyone = lax.all_gather(block_data, "grp", axis=1, tiled=True)
    picked = jnp.take(everyone, own_list, axis=1)
    near_src = picked[:6].reshape(6, -1)
    near_mass = (picked[6] * own_live[:, None].astype(jnp.float32)).reshape(1, -1)
    irregular = pair_sums(own_set, near_src, near_mass)
    accel_now = regular[:3] + irregular[:3]
    jerk_now = regular[3:] + irregular[3:]
    step_time = jnp.take(elapsed, active_stars)
    start_accel = jnp.take(accel_old, active_stars, axis=1)
    start_jerk = jnp.take(jerk_old, active_stars, axis=1)
    change = start_accel - accel_now
    snap_term = -6.0 * change - step_time * (4.0 * start_jerk + 2.0 * jerk_now)
    crackle_term = 12.0 * change + 6.0 * step_time * (start_jerk + jerk_now)
    return (regular, irregular, jnp.concatenate([snap_term, crackle_term], axis=0))


def solution(mesh):
    in_specs = (
        P(None, ("blk", "grp")),
        P(None, ("blk", "grp")),
        P(None, ("blk", "grp")),
        P(None, ("blk", "grp")),
        P(("blk", "grp")),
        P(("blk", "grp")),
        P(("blk", "grp")),
        P(("blk", "grp"), None),
        P(("blk", "grp")),
    )
    out_specs = (P(None, ("blk", "grp")), P(None, ("blk", "grp")), P(None, ("blk", "grp")))
    return jax.shard_map(
        per_device, mesh=mesh, in_specs=in_specs, out_specs=out_specs, check_vma=False
    )
```

profile of v0, /device:TPU:32, one launch (start us, length us, event | category | flops | bytes accessed | tf_op | source)
XLA Modules:
  0.0 1507.0 jit_solution(7764682181993999072)
XLA Ops:
  7.2 0.7 broadcast_multiply_fusion
  7.9 0.8 multiply_add_fusion
  8.7 0.1 copy.277
  8.8 0.7 compare_select_fusion.2
  9.5 1.4 gather_fusion.2
  10.9 0.6 gather_fusion
  11.5 0.7 broadcast_multiply_fusion.1
  12.3 34.4 %all-gather.1 = f32[32,32,6]{1,2,0:T(8,128)S(1)} all-gather(f32[1,32,6]{1,2,0:T(8,128)S(1)} %copy.278), channel_id=1, replica_groups=mesh['blk'=8,'grp'=32] {'grp'}, dimensions={0}, use_global_device_ids=true | all-gather | bytes 25344 | tf_op jit(solution)/shard_map/all_gather | solution.py:60
  46.9 2.8 collective-permute-start
  49.7 0.7 fusion.159
  50.3 0.7 compare_and_fusion
  51.0 0.3 slice_reduce_fusion.1
  51.3 0.7 pad_maximum_fusion.1
  52.0 34.2 %all_gather.15 = f32[7,64,128]{2,0,1:T(8,128)S(1)} all-gather(f32[7,2,128]{2,0,1:T(8,128)S(1)} %pad_maximum_fusion.1), channel_id=1, replica_groups=mesh['blk'=8,'grp'=32] {'grp'}, dimensions={1}, use_global_device_ids=true | all-gather | bytes 236544 | tf_op jit(solution)/shard_map/all_gather | solution.py:107
  86.1 0.6 gather_fusion.1
  86.8 0.1 select_bitcast_fusion
  86.9 0.2 fusion.176
  87.8 1.3 dynamic-slice
  89.0 0.8 dynamic-update-slice
  89.8 13.4 all-reduce
  103.3 31.7 %all-gather = s32[32,1,64]{2,1,0:T(1,128)S(1)} all-gather(s32[1,1,64]{2,1,0:T(1,128)} %bitcast.860), channel_id=1, replica_groups=mesh['blk'=8,'grp'=32] {'grp'}, dimensions={0}, use_global_device_ids=true | all-gather | bytes 8448 | tf_op jit(solution)/shard_map/all_gather | solution.py:62
  135.0 0.2 and_reduce_fusion
  135.3 4.8 while.80
  135.5 2.1 fusion.194
  137.9 2.1 fusion.194
  140.4 0.1 copy.290
  140.5 0.1 copy.292
  140.6 0.6 gather_fusion.3
  141.3 0.6 gather_fusion.4
  142.0 4.5 while.81
  142.1 2.1 fusion.196
  144.3 2.1 fusion.196
  146.5 1.9 collective-permute-start.1
  148.4 5.7 collective-permute-done.1
  154.2 4.5 while.82
  154.2 2.1 fusion.198
  156.5 2.1 fusion.198
  158.8 7.5 collective-permute-done.2
  166.3 4.5 while.83
  166.4 2.1 fusion.200
  168.6 2.1 fusion.200
  170.9 7.5 collective-permute-done.3
  178.5 4.5 while.84
  178.5 2.1 fusion.202
  180.8 2.1 fusion.202
  183.0 0.3 collective-permute-start.4
  183.3 7.5 collective-permute-done.4
  190.8 4.5 while.85
  190.9 2.1 fusion.204
  193.1 2.1 fusion.204
  195.4 7.5 collective-permute-done.5
  203.0 4.5 while.86
  203.0 2.1 fusion.206
  205.3 2.1 fusion.206
  207.6 7.5 collective-permute-done.6
  215.1 4.5 while.87
  215.2 2.1 fusion.208
  217.4 2.1 fusion.208
  219.6 2.6 copy.294
  222.3 2.0 fusion.141
  224.3 0.6 stack.199
  224.9 1273.8 %reduce-scatter.4.cloned.1.call-done = f32[32,6]{1,0:T(8,128)} async-done(((f32[8192,6]{1,0:T(8,128)}), f32[32,6]{1,0:T(8,128)}) %reduce-scatter.4.cloned.1.call-update) | async-done | bytes 784
  1498.7 0.8 copy.295
  1499.6 0.6 pad_maximum_fusion.2
  (126 shorter events, 3.0 us)
Async XLA Ops:
  7.2 133.2 %copy-start.1 = (f32[3,256]{1,0:T(4,128)S(1)}, f32[3,256]{1,0:T(4,128)}, u32[]{:S(2)}) copy-start(f32[3,256]{1,0:T(4,128)} %param.29) | copy-start | bytes 9220
  7.2 133.3 %copy-start.2 = (f32[3,256]{1,0:T(4,128)S(1)}, f32[3,256]{1,0:T(4,128)}, u32[]{:S(2)}) copy-start(f32[3,256]{1,0:T(4,128)} %param.30) | copy-start | bytes 9220
  7.2 1491.6 %reduce-scatter.4.cloned.1.call-start = ((), (), s32[]{:S(2)}) async-start(), calls=%async_computation.1 | async-start | bytes 4210688
  46.9 95.1 %collective-permute-start = (f32[6,1024]{1,0:T(8,128)S(1)}, f32[6,1024]{1,0:T(8,128)S(1)}, u32[]{:S(2)}, u32[]{:S(2)}) collective-permute-start(f32[6,1024]{1,0:T(8,128)S(1)} %bitcast.677), channel_id=1, source_target_pairs={{224,0},{0,32},{32,64},{64,96},{96,128},{128,160},{160,192},{192,2... | collective-permute-start | bytes 73736 | tf_op jit(solution)/shard_map/ppermute | solution.py:15
  146.5 7.6 collective-permute-start.1
  158.7 7.6 collective-permute-start.2
  170.8 7.6 collective-permute-start.3
  183.0 7.8 collective-permute-start.4
  195.3 7.6 collective-permute-start.5
  207.5 7.6 collective-permute-start.6
  1499.5 0.6 copy-start
Sparse Core Ops, SparseCore 0:
  222.4 1276.2 reduce-scatter.3
where the time goes:
time: 1510 us
  waiting for transfers between devices  1320 us (87%)
  blocking collectives  114 us (8%)
  other arithmetic  42.1 us (3%)
  between operations  15.2 us (1%)
    unnamed x2, waiting for transfers between devices  1270 us
    ppermute x7, waiting for transfers between devices, shifted(): return lax.ppermute(block, axis, route)  43.2 us
    reduce_sum x17, other arithmetic, pair_sums(): return jnp.stack([jnp.sum(scaled * term, axis=1) for term in term_list])  36.1 us
    all_gather x1, blocking collectives, per_device(): group_set = lax.all_gather(own_set, 'grp', axis=1, tiled=True)  34.4 us
    all_gather x1, blocking collectives, per_device(): everyone = lax.all_gather(block_data, 'grp', axis=1, tiled=True)  34.2 us
    all_gather x1, blocking collectives, per_device(): lax.all_gather(neighbour_list, 'grp', axis=0, tiled=True)  31.7 us
  transfers between devices with their start and end apart: 8, of which 7 were waited for; matrix products, arithmetic and copies ran while one was open for 1% of the time, Pallas kernels for 0%

commit v1 on v0

v1 whole, which is shorter than its diff:
```python
import jax
import jax.numpy as jnp
from jax import lax
from jax.sharding import PartitionSpec as P

BLOCK = 128


soften_sq = 0.0001


def pair_sums(targets, sources, weight):
    gap_x = sources[0][None, :] - targets[0][:, None]
    gap_y = sources[1][None, :] - targets[1][:, None]
    gap_z = sources[2][None, :] - targets[2][:, None]
    rel_x = sources[3][None, :] - targets[3][:, None]
    rel_y = sources[4][None, :] - targets[4][:, None]
    rel_z = sources[5][None, :] - targets[5][:, None]
    dist_sq = gap_x * gap_x + gap_y * gap_y + gap_z * gap_z + soften_sq
    inverse = lax.rsqrt(dist_sq)
    scaled = weight * (inverse * inverse * inverse)
    radial = 3.0 * (gap_x * rel_x + gap_y * rel_y + gap_z * rel_z) / dist_sq
    term_list = [
        gap_x,
        gap_y,
        gap_z,
        rel_x - radial * gap_x,
        rel_y - radial * gap_y,
        rel_z - radial * gap_z,
    ]
    return jnp.stack([jnp.sum(scaled * term, axis=1) for term in term_list])


def per_device(
    position,
    velocity,
    accel_old,
    jerk_old,
    elapsed,
    masses,
    active_stars,
    neighbour_list,
    neighbour_count,
):
    moved_pos = position + elapsed * (
        velocity + elapsed * (0.5 * accel_old + elapsed * jerk_old / 6.0)
    )
    turned = velocity + elapsed * (accel_old + 0.5 * elapsed * jerk_old)
    sources = jnp.concatenate([moved_pos, turned], axis=0)
    own_set = jnp.take(sources, active_stars, axis=1)
    act_dev = active_stars.shape[0]
    block_data = jnp.concatenate([sources, masses[None, :]], axis=0)
    group = lax.all_gather(block_data, "grp", axis=1, tiled=True)
    group_src = group[:6]
    group_mass = group[6]
    targets = lax.all_gather(own_set, "blk", axis=1, tiled=True)
    blk_size = lax.axis_size("blk")
    blk_here = lax.axis_index("blk")
    block_total = group_src.shape[1] // BLOCK
    slot_total = neighbour_list.shape[1]
    own_live = jnp.arange(slot_total) < neighbour_count[0]
    near = jnp.any(
        own_live[:, None]
        & (neighbour_list[0][:, None] == jnp.arange(block_total)[None, :]),
        axis=0,
    ).astype(jnp.float32)
    owner_rows = jnp.arange(blk_size)
    keep = jnp.where((owner_rows == blk_here)[:, None], 1.0 - near[None, :], 1.0)
    target_pieces = targets.reshape(6, blk_size, act_dev).transpose(1, 0, 2)

    def one_piece(items):
        target_piece, keep_piece = items
        weight = jnp.repeat(keep_piece, BLOCK)[None, :] * group_mass[None, :]
        return pair_sums(target_piece, group_src, weight)

    sums = lax.map(one_piece, (target_pieces, keep))
    partial_terms = sums.transpose(1, 0, 2).reshape(6, blk_size * act_dev)
    regular = lax.psum_scatter(partial_terms, "blk", scatter_dimension=1, tiled=True)
    near_mass = (jnp.repeat(near, BLOCK) * group_mass)[None, :]
    irregular = pair_sums(own_set, group_src, near_mass)
    accel_now = regular[:3] + irregular[:3]
    jerk_now = regular[3:] + irregular[3:]
    step_time = jnp.take(elapsed, active_stars)
    start_accel = jnp.take(accel_old, active_stars, axis=1)
    start_jerk = jnp.take(jerk_old, active_stars, axis=1)
    change = start_accel - accel_now
    snap_term = -6.0 * change - step_time * (4.0 * start_jerk + 2.0 * jerk_now)
    crackle_term = 12.0 * change + 6.0 * step_time * (start_jerk + jerk_now)
    return (regular, irregular, jnp.concatenate([snap_term, crackle_term], axis=0))


def solution(mesh):
    in_specs = (
        P(None, ("blk", "grp")),
        P(None, ("blk", "grp")),
        P(None, ("blk", "grp")),
        P(None, ("blk", "grp")),
        P(("blk", "grp")),
        P(("blk", "grp")),
        P(("blk", "grp")),
        P(("blk", "grp"), None),
        P(("blk", "grp")),
    )
    out_specs = (P(None, ("blk", "grp")), P(None, ("blk", "grp")), P(None, ("blk", "grp")))
    return jax.shard_map(
        per_device, mesh=mesh, in_specs=in_specs, out_specs=out_specs, check_vma=False
    )
```

time: 1510 us -> 184 us (0.12)
  waiting for transfers between devices: 1320 us -> 69.3 us
  blocking collectives: 114 us -> 69.5 us
  other arithmetic: 42.1 us -> 20.4 us
    unnamed x2, waiting for transfers between devices: 1270 us -> 69.3 us
    ppermute x7 -> x0, waiting for transfers between devices: 43.2 us -> none  [shifted(): return lax.ppermute(block, axis, route)]
    all_gather x3 -> x2, blocking collectives: 100 us -> 69.5 us  [the longest x1 34.8 us: per_device(): group = lax.all_gather(block_data, 'grp', axis=1, tiled=True)]
    reduce_sum x17 -> x9, other arithmetic: 36.1 us -> 18 us  [pair_sums(): return jnp.stack([jnp.sum(scaled * term, axis=1) for term in term_list])]
  transfers between devices with their start and end apart: 8 -> 1, of which waited for: 7 -> 1; matrix products, arithmetic and copies ran while one was open for 1% -> 2% of each run, Pallas kernels for 0% -> 0%
where the time goes in v1:
time: 184 us
  blocking collectives  69.5 us (38%)
  waiting for transfers between devices  69.3 us (38%)
  other arithmetic  20.4 us (11%)
  between operations  14.9 us (8%)
  local copies, waits for them, and re-layouts  9.81 us (5%)
    unnamed x2, waiting for transfers between devices  69.3 us
    all_gather x1, blocking collectives, per_device(): group = lax.all_gather(block_data, 'grp', axis=1, tiled=True)  34.8 us
    all_gather x1, blocking collectives, per_device(): targets = lax.all_gather(own_set, 'blk', axis=1, tiled=True)  34.6 us
    reduce_sum x9, other arithmetic, pair_sums(): return jnp.stack([jnp.sum(scaled * term, axis=1) for term in term_list])  18 us
    unnamed x22, local copies, waits for them, and re-layouts  4.44 us
  transfers between devices with their start and end apart: 1, of which 1 were waited for; matrix products, arithmetic and copies ran while one was open for 2% of the time, Pallas kernels for 0%

profile of v1, /device:TPU:32, one launch (start us, length us, event | category | flops | bytes accessed | tf_op | source)
XLA Modules:
  0.0 184.2 jit_solution(8976956344711509726)
XLA Ops:
  7.2 0.0 reduce-scatter.4.cloned.1.call-start
  7.2 0.0 copy-start.5
  7.9 0.0 copy-start.4
  7.9 0.0 copy-start.3
  7.9 0.8 fusion.42
  8.7 0.0 copy-start.2
  8.7 0.0 copy-start
  8.7 0.7 copy-done
  9.5 0.0 copy-start.7
  9.5 0.1 copy.108
  9.6 0.5 copy-done.7
  10.1 0.7 gather_fusion.1
  10.8 0.6 gather_fusion
  11.4 0.0 copy-start.6
  11.4 0.7 copy-done.6
  12.1 34.8 %all_gather.6 = f32[7,8192]{1,0:T(8,128)S(1)} all-gather(f32[7,256]{1,0:T(8,128)S(1)} %pad_maximum_fusion), channel_id=1, replica_groups=mesh['blk'=8,'grp'=32] {'grp'}, dimensions={1}, use_global_device_ids=true | all-gather | bytes 236544 | tf_op jit(solution)/shard_map/all_gather | solution.py:53
  46.9 0.1 select_bitcast_fusion.1
  47.0 0.1 copy.109
  47.1 34.6 %all-gather = f32[8,32,6]{1,2,0:T(8,128)S(1)} all-gather(f32[1,32,6]{1,2,0:T(8,128)S(1)} %copy.109), channel_id=1, replica_groups=mesh['blk'=8,'grp'=32] {'blk'}, dimensions={0}, use_global_device_ids=true | all-gather | bytes 6912 | tf_op jit(solution)/shard_map/all_gather | solution.py:56
  81.7 0.1 reshape.131
  81.8 0.1 reshape.91
  81.9 0.1 broadcast_in_dim.83
  82.0 0.2 fusion.50
  82.2 0.1 broadcast_select_fusion
  82.2 18.5 %while.10 = (s32[]{:T(128)}, f32[8,6,32]{2,1,0:T(8,128)S(1)}, f32[8,64]{1,0:T(8,128)S(1)}, f32[1,8192]{1,0:T(1,128)S(1)}, f32[6,8192]{1,0:T(8,128)S(1)}, /*index...) while((s32[]{:T(128)}, f32[8,6,32]{2,1,0:T(8,128)S(1)}, ...), condition=%wide.region_8.9_spmd, body=%wide.region_1.8_spmd.sunk | while | flops 10493767 | bytes 701913 | solution.py:76
  82.2 0.1 fusion.56
  82.4 0.1 bitcast_multiply_fusion.3
  82.5 2.0 %fusion.58 = (f32[32]{0:T(128)S(1)}, f32[32]{0:T(128)S(1)}, f32[32]{0:T(128)S(1)}, f32[32]{0:T(128)S(1)}, f32[32]{0:T(128)S(1)}, /*index=5*/f32[32]{0:T(128)S(1)}) fusion(f32[32]{0:T(128)S(1)} %get-tuple-element.206, f32[8192]{0:T(1024)S(1)} %bitcast.131, f32[32]{0:T(128)S(1)} %get-tuple-element.208, f32[8192]{0:T(1024)S(1)} %bitcast.133, ...), kind=kLoop, calls=%fused_computation.25.clone.1 | loop fusion | flops 10485568 | bytes 230912 | tf_op jit(solution)/shard_map/while/body/eval_jaxpr/reduce_sum | solution.py:31
  84.6 0.1 fusion.56
  84.7 0.1 bitcast_multiply_fusion.3
  84.8 2.0 %fusion.58 = (f32[32]{0:T(128)S(1)}, f32[32]{0:T(128)S(1)}, f32[32]{0:T(128)S(1)}, f32[32]{0:T(128)S(1)}, f32[32]{0:T(128)S(1)}, /*index=5*/f32[32]{0:T(128)S(1)}) fusion(f32[32]{0:T(128)S(1)} %get-tuple-element.206, f32[8192]{0:T(1024)S(1)} %bitcast.131, f32[32]{0:T(128)S(1)} %get-tuple-element.208, f32[8192]{0:T(1024)S(1)} %bitcast.133, ...), kind=kLoop, calls=%fused_computation.25.clone.1 | loop fusion | flops 10485568 | bytes 230912 | tf_op jit(solution)/shard_map/while/body/eval_jaxpr/reduce_sum | solution.py:31
  86.9 0.1 fusion.56
  87.0 0.1 bitcast_multiply_fusion.3
  87.1 2.0 %fusion.58 = (f32[32]{0:T(128)S(1)}, f32[32]{0:T(128)S(1)}, f32[32]{0:T(128)S(1)}, f32[32]{0:T(128)S(1)}, f32[32]{0:T(128)S(1)}, /*index=5*/f32[32]{0:T(128)S(1)}) fusion(f32[32]{0:T(128)S(1)} %get-tuple-element.206, f32[8192]{0:T(1024)S(1)} %bitcast.131, f32[32]{0:T(128)S(1)} %get-tuple-element.208, f32[8192]{0:T(1024)S(1)} %bitcast.133, ...), kind=kLoop, calls=%fused_computation.25.clone.1 | loop fusion | flops 10485568 | bytes 230912 | tf_op jit(solution)/shard_map/while/body/eval_jaxpr/reduce_sum | solution.py:31
  89.2 0.1 fusion.56
  89.4 0.1 bitcast_multiply_fusion.3
  89.4 2.0 %fusion.58 = (f32[32]{0:T(128)S(1)}, f32[32]{0:T(128)S(1)}, f32[32]{0:T(128)S(1)}, f32[32]{0:T(128)S(1)}, f32[32]{0:T(128)S(1)}, /*index=5*/f32[32]{0:T(128)S(1)}) fusion(f32[32]{0:T(128)S(1)} %get-tuple-element.206, f32[8192]{0:T(1024)S(1)} %bitcast.131, f32[32]{0:T(128)S(1)} %get-tuple-element.208, f32[8192]{0:T(1024)S(1)} %bitcast.133, ...), kind=kLoop, calls=%fused_computation.25.clone.1 | loop fusion | flops 10485568 | bytes 230912 | tf_op jit(solution)/shard_map/while/body/eval_jaxpr/reduce_sum | solution.py:31
  91.5 0.1 fusion.56
  91.7 0.1 bitcast_multiply_fusion.3
  91.8 2.0 %fusion.58 = (f32[32]{0:T(128)S(1)}, f32[32]{0:T(128)S(1)}, f32[32]{0:T(128)S(1)}, f32[32]{0:T(128)S(1)}, f32[32]{0:T(128)S(1)}, /*index=5*/f32[32]{0:T(128)S(1)}) fusion(f32[32]{0:T(128)S(1)} %get-tuple-element.206, f32[8192]{0:T(1024)S(1)} %bitcast.131, f32[32]{0:T(128)S(1)} %get-tuple-element.208, f32[8192]{0:T(1024)S(1)} %bitcast.133, ...), kind=kLoop, calls=%fused_computation.25.clone.1 | loop fusion | flops 10485568 | bytes 230912 | tf_op jit(solution)/shard_map/while/body/eval_jaxpr/reduce_sum | solution.py:31
  93.8 0.1 fusion.56
  94.0 0.1 bitcast_multiply_fusion.3
  94.1 2.0 %fusion.58 = (f32[32]{0:T(128)S(1)}, f32[32]{0:T(128)S(1)}, f32[32]{0:T(128)S(1)}, f32[32]{0:T(128)S(1)}, f32[32]{0:T(128)S(1)}, /*index=5*/f32[32]{0:T(128)S(1)}) fusion(f32[32]{0:T(128)S(1)} %get-tuple-element.206, f32[8192]{0:T(1024)S(1)} %bitcast.131, f32[32]{0:T(128)S(1)} %get-tuple-element.208, f32[8192]{0:T(1024)S(1)} %bitcast.133, ...), kind=kLoop, calls=%fused_computation.25.clone.1 | loop fusion | flops 10485568 | bytes 230912 | tf_op jit(solution)/shard_map/while/body/eval_jaxpr/reduce_sum | solution.py:31
  96.2 0.1 fusion.56
  96.3 0.1 bitcast_multiply_fusion.3
  96.4 2.0 %fusion.58 = (f32[32]{0:T(128)S(1)}, f32[32]{0:T(128)S(1)}, f32[32]{0:T(128)S(1)}, f32[32]{0:T(128)S(1)}, f32[32]{0:T(128)S(1)}, /*index=5*/f32[32]{0:T(128)S(1)}) fusion(f32[32]{0:T(128)S(1)} %get-tuple-element.206, f32[8192]{0:T(1024)S(1)} %bitcast.131, f32[32]{0:T(128)S(1)} %get-tuple-element.208, f32[8192]{0:T(1024)S(1)} %bitcast.133, ...), kind=kLoop, calls=%fused_computation.25.clone.1 | loop fusion | flops 10485568 | bytes 230912 | tf_op jit(solution)/shard_map/while/body/eval_jaxpr/reduce_sum | solution.py:31
  98.5 0.1 fusion.56
  98.6 0.1 bitcast_multiply_fusion.3
  98.7 2.0 %fusion.58 = (f32[32]{0:T(128)S(1)}, f32[32]{0:T(128)S(1)}, f32[32]{0:T(128)S(1)}, f32[32]{0:T(128)S(1)}, f32[32]{0:T(128)S(1)}, /*index=5*/f32[32]{0:T(128)S(1)}) fusion(f32[32]{0:T(128)S(1)} %get-tuple-element.206, f32[8192]{0:T(1024)S(1)} %bitcast.131, f32[32]{0:T(128)S(1)} %get-tuple-element.208, f32[8192]{0:T(1024)S(1)} %bitcast.133, ...), kind=kLoop, calls=%fused_computation.25.clone.1 | loop fusion | flops 10485568 | bytes 230912 | tf_op jit(solution)/shard_map/while/body/eval_jaxpr/reduce_sum | solution.py:31
  100.8 0.8 copy.119
  101.5 0.0 reduce-scatter.4.cloned.1.call-update
  101.6 0.3 slice_reduce_fusion.1
  101.8 2.0 %fusion.29 = (f32[32]{0:T(128)S(1)}, f32[32]{0:T(128)S(1)}, f32[32]{0:T(128)S(1)}, f32[32]{0:T(128)S(1)}, f32[32]{0:T(128)S(1)}, /*index=5*/f32[32]{0:T(128)S(1)}) fusion(f32[32]{0:T(128)S(1)} %get-tuple-element.111, f32[8192]{0:T(1024)S(1)} %bitcast.141, f32[32]{0:T(128)S(1)} %get-tuple-element.108, f32[8192]{0:T(1024)S(1)} %bitcast.143, ...), kind=kLoop, calls=%fused_computation.74 | loop fusion | flops 10485568 | bytes 230912 | tf_op jit(solution)/shard_map/reduce_sum | solution.py:31
  103.8 0.1 copy.113
  104.0 0.1 copy.115
  104.1 0.6 gather_fusion.2
  104.7 0.1 copy.114
  104.8 0.6 gather_fusion.3
  105.3 0.1 copy.116
  105.4 0.6 stack.52
  106.0 69.3 %reduce-scatter.4.cloned.1.call-done = f32[32,6]{1,0:T(8,128)} async-done(((f32[256,6]{1,0:T(8,128)}), f32[32,6]{1,0:T(8,128)}) %reduce-scatter.4.cloned.1.call-update) | async-done | bytes 784
  175.3 0.8 copy.118
  176.1 0.6 copy-done.1
  176.7 0.6 pad_maximum_fusion.2
  (52 shorter events, 0.6 us)
Async XLA Ops:
  7.2 168.2 %reduce-scatter.4.cloned.1.call-start = ((), (), s32[]{:S(2)}) async-start(), calls=%async_computation.1 | async-start | bytes 147456
  7.2 2.2 %copy-start.5 = (f32[3,256]{1,0:T(4,128)S(1)}, f32[3,256]{1,0:T(4,128)}, u32[]{:S(2)}) copy-start(f32[3,256]{1,0:T(4,128)} %param.14) | copy-start | bytes 9220
  7.9 1.5 copy-start.4
  7.9 1.5 copy-start.3
  8.7 0.7 copy-start.2
  8.7 0.7 copy-start
  9.5 0.7 copy-start.7
  11.4 0.7 copy-start.6
  176.1 0.6 copy-start.1
Sparse Core Ops, SparseCore 0:
  101.7 73.6 reduce-scatter.3

commit v2 on v1

--- a/solution.py
+++ b/solution.py
@@ -7,6 +7,45 @@
 
 
 soften_sq = 0.0001
+
+
+def exchange(block, axis, bit):
+    size = lax.axis_size(axis)
+    return lax.ppermute(block, axis, [(i, i ^ bit) for i in range(size)])
+
+
+def gather_doubling(block, axis):
+    me = lax.axis_index(axis)
+    bit = 1
+    while bit < lax.axis_size(axis):
+        got = exchange(block, axis, bit)
+        upper = (me // bit) % 2 == 1
+        block = jnp.where(
+            upper, jnp.concatenate([got, block], 1), jnp.concatenate([block, got], 1)
+        )
+        bit *= 2
+    return block
+
+
+def reduce_halving(block, axis):
+    me = lax.axis_index(axis)
+    bit = lax.axis_size(axis) // 2
+    while bit >= 1:
+        width = block.shape[1] // 2
+        low, high = block[:, :width], block[:, width:]
+        upper = (me // bit) % 2 == 1
+        keep = jnp.where(upper, high, low)
+        send = jnp.where(upper, low, high)
+        block = keep + exchange(send, axis, bit)
+        bit //= 2
+    return block
+
+
+def gather_all_to_all(block, axis):
+    size = lax.axis_size(axis)
+    spread = jnp.broadcast_to(block[:, None, :], (block.shape[0], size, block.shape[1]))
+    got = lax.all_to_all(spread, axis, 1, 1, tiled=True)
+    return got.reshape(block.shape[0], size * block.shape[1])
 
 
 def pair_sums(targets, sources, weight):
@@ -50,10 +89,10 @@
     own_set = jnp.take(sources, active_stars, axis=1)
     act_dev = active_stars.shape[0]
     block_data = jnp.concatenate([sources, masses[None, :]], axis=0)
-    group = lax.all_gather(block_data, "grp", axis=1, tiled=True)
+    group = gather_all_to_all(block_data, "grp")
     group_src = group[:6]
     group_mass = group[6]
-    targets = lax.all_gather(own_set, "blk", axis=1, tiled=True)
+    targets = gather_doubling(own_set, "blk")
     blk_size = lax.axis_size("blk")
     blk_here = lax.axis_index("blk")
     block_total = group_src.shape[1] // BLOCK
@@ -75,7 +114,7 @@
 
     sums = lax.map(one_piece, (target_pieces, keep))
     partial_terms = sums.transpose(1, 0, 2).reshape(6, blk_size * act_dev)
-    regular = lax.psum_scatter(partial_terms, "blk", scatter_dimension=1, tiled=True)
+    regular = reduce_halving(partial_terms, "blk")
     near_mass = (jnp.repeat(near, BLOCK) * group_mass)[None, :]
     irregular = pair_sums(own_set, group_src, near_mass)
     accel_now = regular[:3] + irregular[:3]

time: 184 us -> 65.8 us (0.36)
  blocking collectives: 69.5 us -> 0 us
  waiting for transfers between devices: 69.3 us -> 7.43 us
  starting transfers between devices: 0.04 us -> 23.9 us
  between operations: 14.9 us -> 1.46 us
    all_gather x2 -> x0, blocking collectives: 69.5 us -> none  [the longest x1 34.8 us: per_device(): group = lax.all_gather(block_data, 'grp', axis=1, tiled=True)]
    unnamed x2 -> x0, waiting for transfers between devices: 69.3 us -> none
    ppermute x0 -> x6, starting transfers between devices: none -> 14.3 us  [exchange(): return lax.ppermute(block, axis, [(i, i ^ bit) for i in range(size)])]
    all_to_all x0 -> x1, starting transfers between devices: none -> 9.66 us  [gather_all_to_all(): got = lax.all_to_all(spread, axis, 1, 1, tiled=True)]
    ppermute x0 -> x6, waiting for transfers between devices: none -> 7.42 us  [exchange(): return lax.ppermute(block, axis, [(i, i ^ bit) for i in range(size)])]
    unnamed x22 -> x16, local copies, waits for them, and re-layouts: 4.44 us -> 3.64 us
  transfers between devices with their start and end apart: 1 -> 7, of which waited for: 1 -> 4; matrix products, arithmetic and copies ran while one was open for 2% -> 11% of each run, Pallas kernels for 0% -> 0%
where the time goes in v2:
time: 65.8 us; the launch traced here: 65.1 us
  starting transfers between devices  23.9 us (36%)
  other arithmetic  21.6 us (33%)
  local copies, waits for them, and re-layouts  10.3 us (16%)
  waiting for transfers between devices  7.43 us (11%)
  between operations  1.46 us (2%)
    reduce_sum x9, other arithmetic, pair_sums(): return jnp.stack([jnp.sum(scaled * term, axis=1) for term in term_list])  17.9 us
    ppermute x6, starting transfers between devices, exchange(): return lax.ppermute(block, axis, [(i, i ^ bit) for i in range(size)])  14.3 us
    all_to_all x1, starting transfers between devices, gather_all_to_all(): got = lax.all_to_all(spread, axis, 1, 1, tiled=True)  9.66 us
    ppermute x6, waiting for transfers between devices, exchange(): return lax.ppermute(block, axis, [(i, i ^ bit) for i in range(size)])  7.42 us
    unnamed x16, local copies, waits for them, and re-layouts  3.64 us
  transfers between devices with their start and end apart: 7, of which 4 were waited for; matrix products, arithmetic and copies ran while one was open for 11% of the time, Pallas kernels for 0%

profile of v2, /device:TPU:32, one launch (start us, length us, event | category | flops | bytes accessed | tf_op | source)
XLA Modules:
  0.0 65.1 jit_solution(6454936929841591038)
XLA Ops:
  0.6 0.7 %broadcast_multiply_fusion = f32[256]{0:T(256)S(1)} fusion(f32[256]{0:T(256)} %param.17), kind=kLoop, calls=%fused_computation.129 | loop fusion | flops 256 | bytes 2048 | tf_op jit(solution)/shard_map/mul | solution.py:87
  1.4 0.7 %multiply_add_fusion.1 = (f32[3,256]{1,0:T(4,128)S(1)}, f32[3,256]{1,0:T(4,128)S(1)}) fusion(f32[3,256]{1,0:T(4,128)} %param.13, f32[3,256]{1,0:T(4,128)} %param.14, f32[3,256]{1,0:T(4,128)} %param.16, f32[3,256]{1,0:T(4,128)} %param.15, f32[256]{0:T(256)S(1)} %copy-done, f32[256]{0:T(256)S(1)} %broadcast_multiply_fusion), kind=kLoop, calls=%fused_computation.112 | loop fusion | flops 9216 | bytes 20480 | tf_op jit(solution)/shard_map/add | solution.py:84
  2.1 0.7 %copy-done.4 = f32[256]{0:T(256)S(1)} copy-done((f32[256]{0:T(256)S(1)}, f32[256]{0:T(256)}, u32[]{:S(2)}) %copy-start.4) | copy-done | bytes 1048
  2.8 0.7 %broadcast_in_dim.90 = f32[7,32,256]{2,0,1:T(8,128)} broadcast(f32[7,256]{1,0:T(8,128)S(1)} %pad_maximum_fusion), dimensions={0,2} | broadcast | bytes 236544 | tf_op jit(solution)/shard_map/broadcast_in_dim | solution.py:46
  3.5 9.7 %all-to-all-start = ((f32[7,32,256]{2,0,1:T(8,128)}), f32[7,32,256]{2,0,1:T(8,128)S(1)}, u32[]{:S(2)}, u32[]{:S(2)}) async-start(f32[7,32,256]{2,0,1:T(8,128)} %broadcast_in_dim.90), calls=%async_computation | async-start | bytes 524288 | tf_op jit(solution)/shard_map/all_to_all | solution.py:47
  13.2 0.1 copy.97
  13.4 0.5 copy-done.5
  13.9 0.7 %gather_fusion.1 = f32[32]{0:T(128)S(1)} fusion(f32[256]{0:T(256)S(1)} %copy-done, s32[1024]{0:T(1024)S(1)} %pad_clamp_fusion), kind=kCustom, calls=%fused_computation.3 | custom fusion | bytes 384 | tf_op jit(solution)/shard_map/jit(_take)/gather | solution.py:122
  14.6 0.6 gather_fusion
  15.3 2.8 %collective-permute-start = (f32[6,32]{0,1:T(8,128)S(1)}, f32[6,32]{0,1:T(8,128)S(1)}, u32[]{:S(2)}, u32[]{:S(2)}) collective-permute-start(f32[6,32]{0,1:T(8,128)S(1)} %bitcast_select_fusion.1), channel_id=1, source_target_pairs={{0,32},{32,0},{64,96},{96,64},{128,160},{160,128},{192,224},{224,1... | collective-permute-start | bytes 2312 | tf_op jit(solution)/shard_map/ppermute | solution.py:14
  18.8 0.6 copy-done.6
  19.4 0.1 fusion.42
  19.5 0.1 broadcast_select_fusion
  19.6 0.1 copy.99
  19.7 0.1 copy.103
  19.8 0.8 %collective-permute-done = f32[6,32]{0,1:T(8,128)S(1)} collective-permute-done((f32[6,32]{0,1:T(8,128)S(1)}, f32[6,32]{0,1:T(8,128)S(1)}, u32[]{:S(2)}, u32[]{:S(2)}) %collective-permute-start) | collective-permute-done | bytes 800 | tf_op jit(solution)/shard_map/ppermute | solution.py:14
  20.6 0.1 copy.98
  20.7 0.1 maximum_select_fusion.3
  20.7 1.6 %collective-permute-start.1 = (f32[6,64]{1,0:T(8,128)S(1)}, f32[6,64]{1,0:T(8,128)S(1)}, u32[]{:S(2)}, u32[]{:S(2)}) collective-permute-start(f32[6,64]{1,0:T(8,128)S(1)} %maximum_select_fusion.3), channel_id=1, source_target_pairs={{0,64},{32,96},{64,0},{96,32},{128,192},{160,224},{192,128},{224,1... | collective-permute-start | bytes 4616 | tf_op jit(solution)/shard_map/ppermute | solution.py:14
  22.3 0.1 copy.102
  22.4 1.9 %collective-permute-done.1 = f32[6,64]{1,0:T(8,128)S(1)} collective-permute-done((f32[6,64]{1,0:T(8,128)S(1)}, f32[6,64]{1,0:T(8,128)S(1)}, u32[]{:S(2)}, u32[]{:S(2)}) %collective-permute-start.1) | collective-permute-done | bytes 1568 | tf_op jit(solution)/shard_map/ppermute | solution.py:14
  24.4 0.1 maximum_select_fusion.4
  24.5 3.2 %collective-permute-start.2 = (f32[6,128]{1,0:T(8,128)S(1)}, f32[6,128]{1,0:T(8,128)S(1)}, u32[]{:S(2)}, u32[]{:S(2)}) collective-permute-start(f32[6,128]{1,0:T(8,128)S(1)} %maximum_select_fusion.4), channel_id=1, source_target_pairs={{0,128},{32,160},{64,192},{96,224},{128,0},{160,32},{192,64},{224,... | collective-permute-start | bytes 9224 | tf_op jit(solution)/shard_map/ppermute | solution.py:14
  27.7 0.1 concatenate.57
  27.8 1.8 %collective-permute-done.2 = f32[6,128]{1,0:T(8,128)S(1)} collective-permute-done((f32[6,128]{1,0:T(8,128)S(1)}, f32[6,128]{1,0:T(8,128)S(1)}, u32[]{:S(2)}, u32[]{:S(2)}) %collective-permute-start.2) | collective-permute-done | bytes 3104 | tf_op jit(solution)/shard_map/ppermute | solution.py:14
  29.6 0.1 concatenate.56
  29.7 0.2 fusion.51
  29.9 18.5 %while.10 = (s32[]{:T(128)}, f32[8,6,32]{2,1,0:T(8,128)S(1)}, f32[8,64]{1,0:T(8,128)S(1)}, f32[1,8192]{1,0:T(1,128)S(1)}, f32[6,8192]{1,0:T(8,128)S(1)}, /*index...) while((s32[]{:T(128)}, f32[8,6,32]{2,1,0:T(8,128)S(1)}, ...), condition=%wide.region_8.9_spmd, body=%wide.region_1.8_spmd.sunk | while | flops 10493767 | bytes 701913 | solution.py:115
  29.9 0.1 fusion.57
  30.1 2.0 %fusion.59 = (f32[32]{0:T(128)S(1)}, f32[32]{0:T(128)S(1)}, f32[32]{0:T(128)S(1)}, f32[32]{0:T(128)S(1)}, f32[32]{0:T(128)S(1)}, /*index=5*/f32[32]{0:T(128)S(1)}) fusion(f32[32]{0:T(128)S(1)} %get-tuple-element.188, f32[8192]{0:T(1024)S(1)} %bitcast.132, f32[32]{0:T(128)S(1)} %get-tuple-element.190, f32[8192]{0:T(1024)S(1)} %bitcast.134, ...), kind=kLoop, calls=%fused_computation.25.clone.1 | loop fusion | flops 10485568 | bytes 230912 | tf_op jit(solution)/shard_map/while/body/eval_jaxpr/reduce_sum | solution.py:70
  32.2 0.1 fusion.57
  32.5 2.0 %fusion.59 = (f32[32]{0:T(128)S(1)}, f32[32]{0:T(128)S(1)}, f32[32]{0:T(128)S(1)}, f32[32]{0:T(128)S(1)}, f32[32]{0:T(128)S(1)}, /*index=5*/f32[32]{0:T(128)S(1)}) fusion(f32[32]{0:T(128)S(1)} %get-tuple-element.188, f32[8192]{0:T(1024)S(1)} %bitcast.132, f32[32]{0:T(128)S(1)} %get-tuple-element.190, f32[8192]{0:T(1024)S(1)} %bitcast.134, ...), kind=kLoop, calls=%fused_computation.25.clone.1 | loop fusion | flops 10485568 | bytes 230912 | tf_op jit(solution)/shard_map/while/body/eval_jaxpr/reduce_sum | solution.py:70
  34.5 0.1 fusion.57
  34.8 2.0 %fusion.59 = (f32[32]{0:T(128)S(1)}, f32[32]{0:T(128)S(1)}, f32[32]{0:T(128)S(1)}, f32[32]{0:T(128)S(1)}, f32[32]{0:T(128)S(1)}, /*index=5*/f32[32]{0:T(128)S(1)}) fusion(f32[32]{0:T(128)S(1)} %get-tuple-element.188, f32[8192]{0:T(1024)S(1)} %bitcast.132, f32[32]{0:T(128)S(1)} %get-tuple-element.190, f32[8192]{0:T(1024)S(1)} %bitcast.134, ...), kind=kLoop, calls=%fused_computation.25.clone.1 | loop fusion | flops 10485568 | bytes 230912 | tf_op jit(solution)/shard_map/while/body/eval_jaxpr/reduce_sum | solution.py:70
  36.9 0.1 fusion.57
  37.0 0.1 bitcast_multiply_fusion.4
  37.1 2.0 %fusion.59 = (f32[32]{0:T(128)S(1)}, f32[32]{0:T(128)S(1)}, f32[32]{0:T(128)S(1)}, f32[32]{0:T(128)S(1)}, f32[32]{0:T(128)S(1)}, /*index=5*/f32[32]{0:T(128)S(1)}) fusion(f32[32]{0:T(128)S(1)} %get-tuple-element.188, f32[8192]{0:T(1024)S(1)} %bitcast.132, f32[32]{0:T(128)S(1)} %get-tuple-element.190, f32[8192]{0:T(1024)S(1)} %bitcast.134, ...), kind=kLoop, calls=%fused_computation.25.clone.1 | loop fusion | flops 10485568 | bytes 230912 | tf_op jit(solution)/shard_map/while/body/eval_jaxpr/reduce_sum | solution.py:70
  39.2 0.1 fusion.57
  39.4 2.0 %fusion.59 = (f32[32]{0:T(128)S(1)}, f32[32]{0:T(128)S(1)}, f32[32]{0:T(128)S(1)}, f32[32]{0:T(128)S(1)}, f32[32]{0:T(128)S(1)}, /*index=5*/f32[32]{0:T(128)S(1)}) fusion(f32[32]{0:T(128)S(1)} %get-tuple-element.188, f32[8192]{0:T(1024)S(1)} %bitcast.132, f32[32]{0:T(128)S(1)} %get-tuple-element.190, f32[8192]{0:T(1024)S(1)} %bitcast.134, ...), kind=kLoop, calls=%fused_computation.25.clone.1 | loop fusion | flops 10485568 | bytes 230912 | tf_op jit(solution)/shard_map/while/body/eval_jaxpr/reduce_sum | solution.py:70
  41.5 0.1 fusion.57
  41.7 2.0 %fusion.59 = (f32[32]{0:T(128)S(1)}, f32[32]{0:T(128)S(1)}, f32[32]{0:T(128)S(1)}, f32[32]{0:T(128)S(1)}, f32[32]{0:T(128)S(1)}, /*index=5*/f32[32]{0:T(128)S(1)}) fusion(f32[32]{0:T(128)S(1)} %get-tuple-element.188, f32[8192]{0:T(1024)S(1)} %bitcast.132, f32[32]{0:T(128)S(1)} %get-tuple-element.190, f32[8192]{0:T(1024)S(1)} %bitcast.134, ...), kind=kLoop, calls=%fused_computation.25.clone.1 | loop fusion | flops 10485568 | bytes 230912 | tf_op jit(solution)/shard_map/while/body/eval_jaxpr/reduce_sum | solution.py:70
  43.8 0.1 fusion.57
  44.0 2.0 %fusion.59 = (f32[32]{0:T(128)S(1)}, f32[32]{0:T(128)S(1)}, f32[32]{0:T(128)S(1)}, f32[32]{0:T(128)S(1)}, f32[32]{0:T(128)S(1)}, /*index=5*/f32[32]{0:T(128)S(1)}) fusion(f32[32]{0:T(128)S(1)} %get-tuple-element.188, f32[8192]{0:T(1024)S(1)} %bitcast.132, f32[32]{0:T(128)S(1)} %get-tuple-element.190, f32[8192]{0:T(1024)S(1)} %bitcast.134, ...), kind=kLoop, calls=%fused_computation.25.clone.1 | loop fusion | flops 10485568 | bytes 230912 | tf_op jit(solution)/shard_map/while/body/eval_jaxpr/reduce_sum | solution.py:70
  46.1 0.1 fusion.57
  46.4 2.0 %fusion.59 = (f32[32]{0:T(128)S(1)}, f32[32]{0:T(128)S(1)}, f32[32]{0:T(128)S(1)}, f32[32]{0:T(128)S(1)}, f32[32]{0:T(128)S(1)}, /*index=5*/f32[32]{0:T(128)S(1)}) fusion(f32[32]{0:T(128)S(1)} %get-tuple-element.188, f32[8192]{0:T(1024)S(1)} %bitcast.132, f32[32]{0:T(128)S(1)} %get-tuple-element.190, f32[8192]{0:T(1024)S(1)} %bitcast.134, ...), kind=kLoop, calls=%fused_computation.25.clone.1 | loop fusion | flops 10485568 | bytes 230912 | tf_op jit(solution)/shard_map/while/body/eval_jaxpr/reduce_sum | solution.py:70
  48.4 0.1 reshape.131
  48.5 3.3 %collective-permute-start.3 = (f32[6,128]{1,0:T(8,128)S(1)}, f32[6,128]{1,0:T(8,128)S(1)}, u32[]{:S(2)}, u32[]{:S(2)}) collective-permute-start(f32[6,128]{1,0:T(8,128)S(1)} %slice_select_fusion), channel_id=1, source_target_pairs={{0,128},{32,160},{64,192},{96,224},{128,0},{160,32},{192,64},{224,... | collective-permute-start | bytes 9224 | tf_op jit(solution)/shard_map/ppermute | solution.py:14
  51.8 0.3 slice_reduce_fusion.1
  52.0 0.4 copy-done.2
  52.5 0.1 copy.108
  52.6 0.5 copy-done.3
  53.1 0.1 copy.110
  53.3 0.6 gather_fusion.2
  53.9 0.1 copy.109
  53.9 0.6 gather_fusion.3
  54.5 0.1 copy.111
  54.7 0.7 %collective-permute-start.4 = (f32[6,64]{1,0:T(8,128)S(1)}, f32[6,64]{1,0:T(8,128)S(1)}, u32[]{:S(2)}, u32[]{:S(2)}) collective-permute-start(f32[6,64]{1,0:T(8,128)S(1)} %slice_select_fusion.2), channel_id=1, source_target_pairs={{0,64},{32,96},{64,0},{96,32},{128,192},{160,224},{192,128},{224,1... | collective-permute-start | bytes 4616 | tf_op jit(solution)/shard_map/ppermute | solution.py:14
  55.5 2.9 %collective-permute-done.4 = f32[6,64]{1,0:T(8,128)S(1)} collective-permute-done((f32[6,64]{1,0:T(8,128)S(1)}, f32[6,64]{1,0:T(8,128)S(1)}, u32[]{:S(2)}, u32[]{:S(2)}) %collective-permute-start.4) | collective-permute-done | bytes 1568 | tf_op jit(solution)/shard_map/ppermute | solution.py:14
  58.4 0.1 slice_select_fusion.1
  58.5 2.7 %collective-permute-start.5 = (f32[6,32]{1,0:T(8,128)S(1)}, f32[6,32]{1,0:T(8,128)S(1)}, u32[]{:S(2)}, u32[]{:S(2)}) collective-permute-start(f32[6,32]{1,0:T(8,128)S(1)} %slice_select_fusion.1), channel_id=1, source_target_pairs={{0,32},{32,0},{64,96},{96,64},{128,160},{160,128},{192,224},{224,1... | collective-permute-start | bytes 2312 | tf_op jit(solution)/shard_map/ppermute | solution.py:14
  61.2 2.0 %fusion.29 = (f32[32]{0:T(128)S(1)}, f32[32]{0:T(128)S(1)}, f32[32]{0:T(128)S(1)}, f32[32]{0:T(128)S(1)}, f32[32]{0:T(128)S(1)}, /*index=5*/f32[32]{0:T(128)S(1)}) fusion(f32[32]{0:T(128)S(1)} %get-tuple-element.96, f32[8192]{0:T(1024)S(1)} %bitcast.139, f32[32]{0:T(128)S(1)} %get-tuple-element.93, f32[8192]{0:T(1024)S(1)} %bitcast.141, ...), kind=kLoop, calls=%fused_computation.74 | loop fusion | flops 10485568 | bytes 230912 | tf_op jit(solution)/shard_map/reduce_sum | solution.py:70
  63.2 0.6 stack.52
  63.9 0.6 copy-done.1
  64.5 0.6 pad_maximum_fusion.2
  (74 shorter events, 1.7 us)
Async XLA Ops:
  0.6 0.8 %copy-start = (f32[256]{0:T(256)S(1)}, f32[256]{0:T(256)}, u32[]{:S(2)}) copy-start(f32[256]{0:T(256)} %param.17) | copy-start | bytes 3076
  2.1 0.7 %copy-start.4 = (f32[256]{0:T(256)S(1)}, f32[256]{0:T(256)}, u32[]{:S(2)}) copy-start(f32[256]{0:T(256)} %param.18) | copy-start | bytes 3076
  3.5 26.1 %all-to-all-start = ((f32[7,32,256]{2,0,1:T(8,128)}), f32[7,32,256]{2,0,1:T(8,128)S(1)}, u32[]{:S(2)}, u32[]{:S(2)}) async-start(f32[7,32,256]{2,0,1:T(8,128)} %broadcast_in_dim.90), calls=%async_computation | async-start | bytes 524288 | tf_op jit(solution)/shard_map/all_to_all | solution.py:47
  13.2 0.7 %copy-start.5 = (s32[32]{0:T(128)S(1)}, s32[32]{0:T(128)}, u32[]{:S(2)}) copy-start(s32[32]{0:T(128)} %param.19) | copy-start | bytes 388
  15.3 5.3 %collective-permute-start = (f32[6,32]{0,1:T(8,128)S(1)}, f32[6,32]{0,1:T(8,128)S(1)}, u32[]{:S(2)}, u32[]{:S(2)}) collective-permute-start(f32[6,32]{0,1:T(8,128)S(1)} %bitcast_select_fusion.1), channel_id=1, source_target_pairs={{0,32},{32,0},{64,96},{96,64},{128,160},{160,128},{192,224},{224,1... | collective-permute-start | bytes 2312 | tf_op jit(solution)/shard_map/ppermute | solution.py:14
  18.8 0.7 %copy-start.6 = (s32[1,64]{1,0:T(1,128)S(1)}, s32[1,64]{1,0:T(1,128)}, u32[]{:S(2)}) copy-start(s32[1,64]{1,0:T(1,128)} %param.20) | copy-start | bytes 772
  20.7 3.6 %collective-permute-start.1 = (f32[6,64]{1,0:T(8,128)S(1)}, f32[6,64]{1,0:T(8,128)S(1)}, u32[]{:S(2)}, u32[]{:S(2)}) collective-permute-start(f32[6,64]{1,0:T(8,128)S(1)} %maximum_select_fusion.3), channel_id=1, source_target_pairs={{0,64},{32,96},{64,0},{96,32},{128,192},{160,224},{192,128},{224,1... | collective-permute-start | bytes 4616 | tf_op jit(solution)/shard_map/ppermute | solution.py:14
  24.5 5.1 %collective-permute-start.2 = (f32[6,128]{1,0:T(8,128)S(1)}, f32[6,128]{1,0:T(8,128)S(1)}, u32[]{:S(2)}, u32[]{:S(2)}) collective-permute-start(f32[6,128]{1,0:T(8,128)S(1)} %maximum_select_fusion.4), channel_id=1, source_target_pairs={{0,128},{32,160},{64,192},{96,224},{128,0},{160,32},{192,64},{224,... | collective-permute-start | bytes 9224 | tf_op jit(solution)/shard_map/ppermute | solution.py:14
  48.5 6.1 %collective-permute-start.3 = (f32[6,128]{1,0:T(8,128)S(1)}, f32[6,128]{1,0:T(8,128)S(1)}, u32[]{:S(2)}, u32[]{:S(2)}) collective-permute-start(f32[6,128]{1,0:T(8,128)S(1)} %slice_select_fusion), channel_id=1, source_target_pairs={{0,128},{32,160},{64,192},{96,224},{128,0},{160,32},{192,64},{224,... | collective-permute-start | bytes 9224 | tf_op jit(solution)/shard_map/ppermute | solution.py:14
  51.8 0.7 %copy-start.2 = (f32[3,256]{1,0:T(4,128)S(1)}, f32[3,256]{1,0:T(4,128)}, u32[]{:S(2)}) copy-start(f32[3,256]{1,0:T(4,128)} %param.15) | copy-start | bytes 9220
  52.5 0.7 %copy-start.3 = (f32[3,256]{1,0:T(4,128)S(1)}, f32[3,256]{1,0:T(4,128)}, u32[]{:S(2)}) copy-start(f32[3,256]{1,0:T(4,128)} %param.16) | copy-start | bytes 9220
  54.7 3.6 %collective-permute-start.4 = (f32[6,64]{1,0:T(8,128)S(1)}, f32[6,64]{1,0:T(8,128)S(1)}, u32[]{:S(2)}, u32[]{:S(2)}) collective-permute-start(f32[6,64]{1,0:T(8,128)S(1)} %slice_select_fusion.2), channel_id=1, source_target_pairs={{0,64},{32,96},{64,0},{96,32},{128,192},{160,224},{192,128},{224,1... | collective-permute-start | bytes 4616 | tf_op jit(solution)/shard_map/ppermute | solution.py:14
  58.5 5.4 %collective-permute-start.5 = (f32[6,32]{1,0:T(8,128)S(1)}, f32[6,32]{1,0:T(8,128)S(1)}, u32[]{:S(2)}, u32[]{:S(2)}) collective-permute-start(f32[6,32]{1,0:T(8,128)S(1)} %slice_select_fusion.1), channel_id=1, source_target_pairs={{0,32},{32,0},{64,96},{96,64},{128,160},{160,128},{192,224},{224,1... | collective-permute-start | bytes 2312 | tf_op jit(solution)/shard_map/ppermute | solution.py:14
  63.9 0.6 copy-start.1

commit v3 on v2

--- a/solution.py
+++ b/solution.py
@@ -2,6 +2,7 @@
 import jax.numpy as jnp
 from jax import lax
 from jax.sharding import PartitionSpec as P
+
 
 BLOCK = 128
 
@@ -27,9 +28,8 @@
     return block
 
 
-def reduce_halving(block, axis):
+def reduce_halving(block, axis, bit):
     me = lax.axis_index(axis)
-    bit = lax.axis_size(axis) // 2
     while bit >= 1:
         width = block.shape[1] // 2
         low, high = block[:, :width], block[:, width:]
@@ -89,10 +89,10 @@
     own_set = jnp.take(sources, active_stars, axis=1)
     act_dev = active_stars.shape[0]
     block_data = jnp.concatenate([sources, masses[None, :]], axis=0)
+    targets = gather_doubling(own_set, "blk")
     group = gather_all_to_all(block_data, "grp")
     group_src = group[:6]
     group_mass = group[6]
-    targets = gather_doubling(own_set, "blk")
     blk_size = lax.axis_size("blk")
     blk_here = lax.axis_index("blk")
     block_total = group_src.shape[1] // BLOCK
@@ -103,18 +103,29 @@
         & (neighbour_list[0][:, None] == jnp.arange(block_total)[None, :]),
         axis=0,
     ).astype(jnp.float32)
-    owner_rows = jnp.arange(blk_size)
-    keep = jnp.where((owner_rows == blk_here)[:, None], 1.0 - near[None, :], 1.0)
-    target_pieces = targets.reshape(6, blk_size, act_dev).transpose(1, 0, 2)
+    half = blk_size // 2
+    upper = (blk_here // half) % 2 == 1
+    other_start = jnp.where(upper, 0, half)
+    mine_start = half - other_start
 
-    def one_piece(items):
-        target_piece, keep_piece = items
-        weight = jnp.repeat(keep_piece, BLOCK)[None, :] * group_mass[None, :]
-        return pair_sums(target_piece, group_src, weight)
+    def half_sums(start):
+        owners = start + jnp.arange(half)
+        keep = jnp.where((owners == blk_here)[:, None], 1.0 - near[None, :], 1.0)
+        pieces = lax.dynamic_slice_in_dim(targets, start * act_dev, half * act_dev, 1)
+        pieces = pieces.reshape(6, half, act_dev).transpose(1, 0, 2)
 
-    sums = lax.map(one_piece, (target_pieces, keep))
-    partial_terms = sums.transpose(1, 0, 2).reshape(6, blk_size * act_dev)
-    regular = reduce_halving(partial_terms, "blk")
+        def one_piece(items):
+            target_piece, keep_piece = items
+            weight = jnp.repeat(keep_piece, BLOCK)[None, :] * group_mass[None, :]
+            return pair_sums(target_piece, group_src, weight)
+
+        sums = lax.map(one_piece, (pieces, keep))
+        return sums.transpose(1, 0, 2).reshape(6, half * act_dev)
+
+    send = half_sums(other_start)
+    got = exchange(send, "blk", half)
+    kept = half_sums(mine_start)
+    regular = reduce_halving(kept + got, "blk", half // 2)
     near_mass = (jnp.repeat(near, BLOCK) * group_mass)[None, :]
     irregular = pair_sums(own_set, group_src, near_mass)
     accel_now = regular[:3] + irregular[:3]
@@ -141,6 +152,7 @@
         P(("blk", "grp")),
     )
     out_specs = (P(None, ("blk", "grp")), P(None, ("blk", "grp")), P(None, ("blk", "grp")))
+
     return jax.shard_map(
         per_device, mesh=mesh, in_specs=in_specs, out_specs=out_specs, check_vma=False
     )

time: 65.8 us -> 61.9 us (0.941)
  waiting for transfers between devices: 7.43 us -> 5.48 us
  starting transfers between devices: 23.9 us -> 22.6 us
    ppermute x6, waiting for transfers between devices: 7.42 us -> 5.32 us  [exchange(): return lax.ppermute(block, axis, [(i, i ^ bit) for i in range(size)])]
    all_to_all x1, starting transfers between devices: 9.66 us -> 8.76 us  [gather_all_to_all(): got = lax.all_to_all(spread, axis, 1, 1, tiled=True)]
  transfers between devices with their start and end apart: 7 -> 7, of which waited for: 4 -> 4; matrix products, arithmetic and copies ran while one was open for 11% -> 25% of each run, Pallas kernels for 0% -> 0%
where the time goes in v3:
time: 61.9 us; the launch traced here: 61.2 us
  starting transfers between devices  22.6 us (37%)
  other arithmetic  21.5 us (35%)
  local copies, waits for them, and re-layouts  9.81 us (16%)
  waiting for transfers between devices  5.48 us (9%)
  between operations  1.51 us (2%)
    reduce_sum x9, other arithmetic, pair_sums(): return jnp.stack([jnp.sum(scaled * term, axis=1) for term in term_list])  17.9 us
    ppermute x6, starting transfers between devices, exchange(): return lax.ppermute(block, axis, [(i, i ^ bit) for i in range(size)])  13.8 us
    all_to_all x1, starting transfers between devices, gather_all_to_all(): got = lax.all_to_all(spread, axis, 1, 1, tiled=True)  8.76 us
    ppermute x6, waiting for transfers between devices, exchange(): return lax.ppermute(block, axis, [(i, i ^ bit) for i in range(size)])  5.32 us
    unnamed x16, local copies, waits for them, and re-layouts  3.22 us
    slice x9, local copies, waits for them, and re-layouts, pair_sums(): rel_x = sources[3][None, :] - targets[3][:, None]  1.27 us
  transfers between devices with their start and end apart: 7, of which 4 were waited for; matrix products, arithmetic and copies ran while one was open for 25% of the time, Pallas kernels for 0%

profile of v3, /device:TPU:32, one launch (start us, length us, event | category | flops | bytes accessed | tf_op | source)
XLA Modules:
  0.0 61.2 jit_solution(18124297285380595814)
XLA Ops:
  0.6 0.7 %broadcast_multiply_fusion = f32[256]{0:T(256)S(1)} fusion(f32[256]{0:T(256)} %param.19), kind=kLoop, calls=%fused_computation.174 | loop fusion | flops 256 | bytes 2048 | tf_op jit(solution)/shard_map/mul | solution.py:87
  1.4 0.7 %multiply_add_fusion.1 = (f32[3,256]{1,0:T(4,128)S(1)}, f32[3,256]{1,0:T(4,128)S(1)}) fusion(f32[3,256]{1,0:T(4,128)} %param.15, f32[3,256]{1,0:T(4,128)} %param.16, f32[3,256]{1,0:T(4,128)} %param.18, f32[3,256]{1,0:T(4,128)} %param.17, f32[256]{0:T(256)S(1)} %copy-done, f32[256]{0:T(256)S(1)} %broadcast_multiply_fusion), kind=kLoop, calls=%fused_computation.156 | loop fusion | flops 9216 | bytes 20480 | tf_op jit(solution)/shard_map/add | solution.py:84
  2.2 0.1 copy.97
  2.3 0.5 copy-done.5
  2.8 0.7 %gather_fusion.1 = f32[32]{0:T(128)S(1)} fusion(f32[256]{0:T(256)S(1)} %copy-done, s32[1024]{0:T(1024)S(1)} %pad_clamp_fusion), kind=kCustom, calls=%fused_computation.3 | custom fusion | bytes 384 | tf_op jit(solution)/shard_map/jit(_take)/gather | solution.py:133
  3.5 0.6 gather_fusion
  4.2 3.1 %collective-permute-start = (f32[6,32]{0,1:T(8,128)S(1)}, f32[6,32]{0,1:T(8,128)S(1)}, u32[]{:S(2)}, u32[]{:S(2)}) collective-permute-start(f32[6,32]{0,1:T(8,128)S(1)} %select_bitcast_fusion), channel_id=1, source_target_pairs={{0,32},{32,0},{64,96},{96,64},{128,160},{160,128},{192,224},{224,1... | collective-permute-start | bytes 2312 | tf_op jit(solution)/shard_map/ppermute | solution.py:15
  7.3 0.7 %broadcast_in_dim.99 = f32[7,32,256]{2,0,1:T(8,128)} broadcast(f32[7,256]{1,0:T(8,128)S(1)} %pad_maximum_fusion), dimensions={0,2} | broadcast | bytes 236544 | tf_op jit(solution)/shard_map/broadcast_in_dim | solution.py:46
  8.0 8.8 %all-to-all-start = ((f32[7,32,256]{2,0,1:T(8,128)}), f32[7,32,256]{2,0,1:T(8,128)S(1)}, u32[]{:S(2)}, u32[]{:S(2)}) async-start(f32[7,32,256]{2,0,1:T(8,128)} %broadcast_in_dim.99), calls=%async_computation | async-start | bytes 524288 | tf_op jit(solution)/shard_map/all_to_all | solution.py:47
  17.5 0.6 %copy-done.6 = s32[1,64]{1,0:T(1,128)S(1)} copy-done((s32[1,64]{1,0:T(1,128)S(1)}, s32[1,64]{1,0:T(1,128)}, u32[]{:S(2)}) %copy-start.6) | copy-done | bytes 280
  18.1 0.1 fusion.66
  18.3 0.1 copy.99
  18.3 0.1 copy.98
  18.4 0.1 maximum_select_fusion.1
  18.5 1.6 %collective-permute-start.1 = (f32[6,64]{1,0:T(8,128)S(1)}, f32[6,64]{1,0:T(8,128)S(1)}, u32[]{:S(2)}, u32[]{:S(2)}) collective-permute-start(f32[6,64]{1,0:T(8,128)S(1)} %maximum_select_fusion.1), channel_id=1, source_target_pairs={{0,64},{32,96},{64,0},{96,32},{128,192},{160,224},{192,128},{224,1... | collective-permute-start | bytes 4616 | tf_op jit(solution)/shard_map/ppermute | solution.py:15
  20.2 2.0 %collective-permute-done.1 = f32[6,64]{1,0:T(8,128)S(1)} collective-permute-done((f32[6,64]{1,0:T(8,128)S(1)}, f32[6,64]{1,0:T(8,128)S(1)}, u32[]{:S(2)}, u32[]{:S(2)}) %collective-permute-start.1) | collective-permute-done | bytes 1568 | tf_op jit(solution)/shard_map/ppermute | solution.py:15
  22.1 0.1 maximum_select_fusion.2
  22.2 3.2 %collective-permute-start.2 = (f32[6,128]{1,0:T(8,128)S(1)}, f32[6,128]{1,0:T(8,128)S(1)}, u32[]{:S(2)}, u32[]{:S(2)}) collective-permute-start(f32[6,128]{1,0:T(8,128)S(1)} %maximum_select_fusion.2), channel_id=1, source_target_pairs={{0,128},{32,160},{64,192},{96,224},{128,0},{160,32},{192,64},{224,... | collective-permute-start | bytes 9224 | tf_op jit(solution)/shard_map/ppermute | solution.py:15
  25.4 0.3 slice_reduce_fusion.1
  25.7 0.7 %copy-done.2 = f32[3,256]{1,0:T(4,128)S(1)} copy-done((f32[3,256]{1,0:T(4,128)S(1)}, f32[3,256]{1,0:T(4,128)}, u32[]{:S(2)}) %copy-start.2) | copy-done | bytes 3096
  26.4 0.1 copy.106
  26.5 0.5 copy-done.3
  27.1 0.1 copy.108
  27.2 0.6 gather_fusion.2
  27.8 0.1 copy.107
  27.9 0.6 gather_fusion.3
  28.4 0.1 copy.109
  28.5 0.1 reshape.163
  28.6 0.1 reshape.161
  28.7 0.2 all-to-all-done
  28.9 0.2 fusion.75
  29.0 9.3 %while.21 = (s32[]{:T(128)}, f32[4,6,32]{2,1,0:T(8,128)S(1)}, f32[4,64]{1,0:T(4,128)S(1)}, f32[1,8192]{1,0:T(1,128)S(1)}, f32[6,8192]{1,0:T(8,128)S(1)}, /*index...) while((s32[]{:T(128)}, f32[4,6,32]{2,1,0:T(8,128)S(1)}, ...), condition=%wide.region_16.17_spmd, body=%wide.region_9.16_spmd.sunk | while | flops 10493767 | bytes 701913 | solution.py:122
  29.1 0.1 fusion.89
  29.2 0.1 bitcast_multiply_fusion.7
  29.3 2.0 %fusion.91 = (f32[32]{0:T(128)S(1)}, f32[32]{0:T(128)S(1)}, f32[32]{0:T(128)S(1)}, f32[32]{0:T(128)S(1)}, f32[32]{0:T(128)S(1)}, /*index=5*/f32[32]{0:T(128)S(1)}) fusion(f32[32]{0:T(128)S(1)} %get-tuple-element.346, f32[8192]{0:T(1024)S(1)} %bitcast.207, f32[32]{0:T(128)S(1)} %get-tuple-element.348, f32[8192]{0:T(1024)S(1)} %bitcast.209, ...), kind=kLoop, calls=%fused_computation.74.clone.1 | loop fusion | flops 10485568 | bytes 230912 | tf_op jit(solution)/shard_map/while/body/eval_jaxpr/reduce_sum | solution.py:70
  31.4 0.1 fusion.89
  31.6 2.0 %fusion.91 = (f32[32]{0:T(128)S(1)}, f32[32]{0:T(128)S(1)}, f32[32]{0:T(128)S(1)}, f32[32]{0:T(128)S(1)}, f32[32]{0:T(128)S(1)}, /*index=5*/f32[32]{0:T(128)S(1)}) fusion(f32[32]{0:T(128)S(1)} %get-tuple-element.346, f32[8192]{0:T(1024)S(1)} %bitcast.207, f32[32]{0:T(128)S(1)} %get-tuple-element.348, f32[8192]{0:T(1024)S(1)} %bitcast.209, ...), kind=kLoop, calls=%fused_computation.74.clone.1 | loop fusion | flops 10485568 | bytes 230912 | tf_op jit(solution)/shard_map/while/body/eval_jaxpr/reduce_sum | solution.py:70
  33.7 0.1 fusion.89
  34.0 2.0 %fusion.91 = (f32[32]{0:T(128)S(1)}, f32[32]{0:T(128)S(1)}, f32[32]{0:T(128)S(1)}, f32[32]{0:T(128)S(1)}, f32[32]{0:T(128)S(1)}, /*index=5*/f32[32]{0:T(128)S(1)}) fusion(f32[32]{0:T(128)S(1)} %get-tuple-element.346, f32[8192]{0:T(1024)S(1)} %bitcast.207, f32[32]{0:T(128)S(1)} %get-tuple-element.348, f32[8192]{0:T(1024)S(1)} %bitcast.209, ...), kind=kLoop, calls=%fused_computation.74.clone.1 | loop fusion | flops 10485568 | bytes 230912 | tf_op jit(solution)/shard_map/while/body/eval_jaxpr/reduce_sum | solution.py:70
  36.0 0.1 fusion.89
  36.2 0.1 bitcast_multiply_fusion.7
  36.3 2.0 %fusion.91 = (f32[32]{0:T(128)S(1)}, f32[32]{0:T(128)S(1)}, f32[32]{0:T(128)S(1)}, f32[32]{0:T(128)S(1)}, f32[32]{0:T(128)S(1)}, /*index=5*/f32[32]{0:T(128)S(1)}) fusion(f32[32]{0:T(128)S(1)} %get-tuple-element.346, f32[8192]{0:T(1024)S(1)} %bitcast.207, f32[32]{0:T(128)S(1)} %get-tuple-element.348, f32[8192]{0:T(1024)S(1)} %bitcast.209, ...), kind=kLoop, calls=%fused_computation.74.clone.1 | loop fusion | flops 10485568 | bytes 230912 | tf_op jit(solution)/shard_map/while/body/eval_jaxpr/reduce_sum | solution.py:70
  38.3 0.1 reshape.164
  38.4 3.2 %collective-permute-start.3 = (f32[6,128]{1,0:T(8,128)S(1)}, f32[6,128]{1,0:T(8,128)S(1)}, u32[]{:S(2)}, u32[]{:S(2)}) collective-permute-start(f32[6,128]{1,0:T(8,128)S(1)} %reshape.164), channel_id=1, source_target_pairs={{0,128},{32,160},{64,192},{96,224},{128,0},{160,32},{192,64},{224,... | collective-permute-start | bytes 9224 | tf_op jit(solution)/shard_map/ppermute | solution.py:15
  41.6 9.2 %while.20 = (s32[]{:T(128)}, f32[4,6,32]{2,1,0:T(8,128)S(1)}, f32[4,64]{1,0:T(4,128)S(1)}, f32[1,8192]{1,0:T(1,128)S(1)}, f32[6,8192]{1,0:T(8,128)S(1)}, /*index...) while((s32[]{:T(128)}, f32[4,6,32]{2,1,0:T(8,128)S(1)}, ...), condition=%wide.region_8.9_spmd, body=%wide.region_1.8_spmd.sunk | while | flops 10493767 | bytes 701913 | solution.py:122
  41.6 0.1 fusion.85
  41.9 2.0 %fusion.87 = (f32[32]{0:T(128)S(1)}, f32[32]{0:T(128)S(1)}, f32[32]{0:T(128)S(1)}, f32[32]{0:T(128)S(1)}, f32[32]{0:T(128)S(1)}, /*index=5*/f32[32]{0:T(128)S(1)}) fusion(f32[32]{0:T(128)S(1)} %get-tuple-element.322, f32[8192]{0:T(1024)S(1)} %bitcast.213, f32[32]{0:T(128)S(1)} %get-tuple-element.324, f32[8192]{0:T(1024)S(1)} %bitcast.215, ...), kind=kLoop, calls=%fused_computation.25.clone.1 | loop fusion | flops 10485568 | bytes 230912 | tf_op jit(solution)/shard_map/while/body/eval_jaxpr/reduce_sum | solution.py:70
  44.0 0.1 fusion.85
  44.2 2.0 %fusion.87 = (f32[32]{0:T(128)S(1)}, f32[32]{0:T(128)S(1)}, f32[32]{0:T(128)S(1)}, f32[32]{0:T(128)S(1)}, f32[32]{0:T(128)S(1)}, /*index=5*/f32[32]{0:T(128)S(1)}) fusion(f32[32]{0:T(128)S(1)} %get-tuple-element.322, f32[8192]{0:T(1024)S(1)} %bitcast.213, f32[32]{0:T(128)S(1)} %get-tuple-element.324, f32[8192]{0:T(1024)S(1)} %bitcast.215, ...), kind=kLoop, calls=%fused_computation.25.clone.1 | loop fusion | flops 10485568 | bytes 230912 | tf_op jit(solution)/shard_map/while/body/eval_jaxpr/reduce_sum | solution.py:70
  46.3 0.1 fusion.85
  46.5 2.0 %fusion.87 = (f32[32]{0:T(128)S(1)}, f32[32]{0:T(128)S(1)}, f32[32]{0:T(128)S(1)}, f32[32]{0:T(128)S(1)}, f32[32]{0:T(128)S(1)}, /*index=5*/f32[32]{0:T(128)S(1)}) fusion(f32[32]{0:T(128)S(1)} %get-tuple-element.322, f32[8192]{0:T(1024)S(1)} %bitcast.213, f32[32]{0:T(128)S(1)} %get-tuple-element.324, f32[8192]{0:T(1024)S(1)} %bitcast.215, ...), kind=kLoop, calls=%fused_computation.25.clone.1 | loop fusion | flops 10485568 | bytes 230912 | tf_op jit(solution)/shard_map/while/body/eval_jaxpr/reduce_sum | solution.py:70
  48.6 0.1 fusion.85
  48.8 2.0 %fusion.87 = (f32[32]{0:T(128)S(1)}, f32[32]{0:T(128)S(1)}, f32[32]{0:T(128)S(1)}, f32[32]{0:T(128)S(1)}, f32[32]{0:T(128)S(1)}, /*index=5*/f32[32]{0:T(128)S(1)}) fusion(f32[32]{0:T(128)S(1)} %get-tuple-element.322, f32[8192]{0:T(1024)S(1)} %bitcast.213, f32[32]{0:T(128)S(1)} %get-tuple-element.324, f32[8192]{0:T(1024)S(1)} %bitcast.215, ...), kind=kLoop, calls=%fused_computation.25.clone.1 | loop fusion | flops 10485568 | bytes 230912 | tf_op jit(solution)/shard_map/while/body/eval_jaxpr/reduce_sum | solution.py:70
  50.9 0.1 reshape.162
  51.0 0.1 slice_select_fusion.1
  51.1 0.7 %collective-permute-start.4 = (f32[6,64]{1,0:T(8,128)S(1)}, f32[6,64]{1,0:T(8,128)S(1)}, u32[]{:S(2)}, u32[]{:S(2)}) collective-permute-start(f32[6,64]{1,0:T(8,128)S(1)} %slice_select_fusion.1), channel_id=1, source_target_pairs={{0,64},{32,96},{64,0},{96,32},{128,192},{160,224},{192,128},{224,1... | collective-permute-start | bytes 4616 | tf_op jit(solution)/shard_map/ppermute | solution.py:15
  51.8 2.9 %collective-permute-done.4 = f32[6,64]{1,0:T(8,128)S(1)} collective-permute-done((f32[6,64]{1,0:T(8,128)S(1)}, f32[6,64]{1,0:T(8,128)S(1)}, u32[]{:S(2)}, u32[]{:S(2)}) %collective-permute-start.4) | collective-permute-done | bytes 1568 | tf_op jit(solution)/shard_map/ppermute | solution.py:15
  54.8 0.1 slice_select_fusion
  54.8 2.0 %collective-permute-start.5 = (f32[6,32]{1,0:T(8,128)S(1)}, f32[6,32]{1,0:T(8,128)S(1)}, u32[]{:S(2)}, u32[]{:S(2)}) collective-permute-start(f32[6,32]{1,0:T(8,128)S(1)} %slice_select_fusion), channel_id=1, source_target_pairs={{0,32},{32,0},{64,96},{96,64},{128,160},{160,128},{192,224},{224,1... | collective-permute-start | bytes 2312 | tf_op jit(solution)/shard_map/ppermute | solution.py:15
  56.9 2.0 %fusion.53 = (f32[32]{0:T(128)S(1)}, f32[32]{0:T(128)S(1)}, f32[32]{0:T(128)S(1)}, f32[32]{0:T(128)S(1)}, f32[32]{0:T(128)S(1)}, /*index=5*/f32[32]{0:T(128)S(1)}) fusion(f32[32]{0:T(128)S(1)} %get-tuple-element.153, f32[8192]{0:T(1024)S(1)} %bitcast.223, f32[32]{0:T(128)S(1)} %get-tuple-element.150, f32[8192]{0:T(1024)S(1)} %bitcast.225, ...), kind=kLoop, calls=%fused_computation.123 | loop fusion | flops 10485568 | bytes 230912 | tf_op jit(solution)/shard_map/reduce_sum | solution.py:70
  58.8 0.6 %stack.73 = f32[6,32]{1,0:T(8,128)} concatenate(f32[1,32]{1,0:T(1,128)S(1)} %bitcast.255, f32[1,32]{1,0:T(1,128)S(1)} %bitcast.249, f32[1,32]{1,0:T(1,128)S(1)} %bitcast.252, f32[1,32]{1,0:T(1,128)S(1)} %bitcast.246, f32[1,32]{1,0:T(1,128)S(1)} %bitcast.243, f32[1,32]{1,0:T(1,128)S(1)} %bitcast.240), dimensions={0} | concatenate | bytes 1536 | tf_op jit(solution)/shard_map/stack | solution.py:70
  59.5 0.5 collective-permute-done.5
  60.1 0.6 copy-done.1
  60.6 0.6 pad_maximum_fusion.2
  (74 shorter events, 1.5 us)
Async XLA Ops:
  0.6 0.8 %copy-start = (f32[256]{0:T(256)S(1)}, f32[256]{0:T(256)}, u32[]{:S(2)}) copy-start(f32[256]{0:T(256)} %param.19) | copy-start | bytes 3076
  2.2 0.7 %copy-start.5 = (s32[32]{0:T(128)S(1)}, s32[32]{0:T(128)}, u32[]{:S(2)}) copy-start(s32[32]{0:T(128)} %param.21) | copy-start | bytes 388
  4.2 3.1 %copy-start.4 = (f32[256]{0:T(256)S(1)}, f32[256]{0:T(256)}, u32[]{:S(2)}) copy-start(f32[256]{0:T(256)} %param.20) | copy-start | bytes 3076
  4.2 14.1 %collective-permute-start = (f32[6,32]{0,1:T(8,128)S(1)}, f32[6,32]{0,1:T(8,128)S(1)}, u32[]{:S(2)}, u32[]{:S(2)}) collective-permute-start(f32[6,32]{0,1:T(8,128)S(1)} %select_bitcast_fusion), channel_id=1, source_target_pairs={{0,32},{32,0},{64,96},{96,64},{128,160},{160,128},{192,224},{224,1... | collective-permute-start | bytes 2312 | tf_op jit(solution)/shard_map/ppermute | solution.py:15
  8.0 20.9 %all-to-all-start = ((f32[7,32,256]{2,0,1:T(8,128)}), f32[7,32,256]{2,0,1:T(8,128)S(1)}, u32[]{:S(2)}, u32[]{:S(2)}) async-start(f32[7,32,256]{2,0,1:T(8,128)} %broadcast_in_dim.99), calls=%async_computation | async-start | bytes 524288 | tf_op jit(solution)/shard_map/all_to_all | solution.py:47
  17.5 0.7 %copy-start.6 = (s32[1,64]{1,0:T(1,128)S(1)}, s32[1,64]{1,0:T(1,128)}, u32[]{:S(2)}) copy-start(s32[1,64]{1,0:T(1,128)} %param.22) | copy-start | bytes 772
  18.5 3.6 %collective-permute-start.1 = (f32[6,64]{1,0:T(8,128)S(1)}, f32[6,64]{1,0:T(8,128)S(1)}, u32[]{:S(2)}, u32[]{:S(2)}) collective-permute-start(f32[6,64]{1,0:T(8,128)S(1)} %maximum_select_fusion.1), channel_id=1, source_target_pairs={{0,64},{32,96},{64,0},{96,32},{128,192},{160,224},{192,128},{224,1... | collective-permute-start | bytes 4616 | tf_op jit(solution)/shard_map/ppermute | solution.py:15
  22.2 6.3 %collective-permute-start.2 = (f32[6,128]{1,0:T(8,128)S(1)}, f32[6,128]{1,0:T(8,128)S(1)}, u32[]{:S(2)}, u32[]{:S(2)}) collective-permute-start(f32[6,128]{1,0:T(8,128)S(1)} %maximum_select_fusion.2), channel_id=1, source_target_pairs={{0,128},{32,160},{64,192},{96,224},{128,0},{160,32},{192,64},{224,... | collective-permute-start | bytes 9224 | tf_op jit(solution)/shard_map/ppermute | solution.py:15
  25.7 0.7 %copy-start.2 = (f32[3,256]{1,0:T(4,128)S(1)}, f32[3,256]{1,0:T(4,128)}, u32[]{:S(2)}) copy-start(f32[3,256]{1,0:T(4,128)} %param.17) | copy-start | bytes 9220
  26.4 0.7 %copy-start.3 = (f32[3,256]{1,0:T(4,128)S(1)}, f32[3,256]{1,0:T(4,128)}, u32[]{:S(2)}) copy-start(f32[3,256]{1,0:T(4,128)} %param.18) | copy-start | bytes 9220
  38.4 12.6 %collective-permute-start.3 = (f32[6,128]{1,0:T(8,128)S(1)}, f32[6,128]{1,0:T(8,128)S(1)}, u32[]{:S(2)}, u32[]{:S(2)}) collective-permute-start(f32[6,128]{1,0:T(8,128)S(1)} %reshape.164), channel_id=1, source_target_pairs={{0,128},{32,160},{64,192},{96,224},{128,0},{160,32},{192,64},{224,... | collective-permute-start | bytes 9224 | tf_op jit(solution)/shard_map/ppermute | solution.py:15
  51.1 3.6 %collective-permute-start.4 = (f32[6,64]{1,0:T(8,128)S(1)}, f32[6,64]{1,0:T(8,128)S(1)}, u32[]{:S(2)}, u32[]{:S(2)}) collective-permute-start(f32[6,64]{1,0:T(8,128)S(1)} %slice_select_fusion.1), channel_id=1, source_target_pairs={{0,64},{32,96},{64,0},{96,32},{128,192},{160,224},{192,128},{224,1... | collective-permute-start | bytes 4616 | tf_op jit(solution)/shard_map/ppermute | solution.py:15
  54.8 5.1 %collective-permute-start.5 = (f32[6,32]{1,0:T(8,128)S(1)}, f32[6,32]{1,0:T(8,128)S(1)}, u32[]{:S(2)}, u32[]{:S(2)}) collective-permute-start(f32[6,32]{1,0:T(8,128)S(1)} %slice_select_fusion), channel_id=1, source_target_pairs={{0,32},{32,0},{64,96},{96,64},{128,160},{160,128},{192,224},{224,1... | collective-permute-start | bytes 2312 | tf_op jit(solution)/shard_map/ppermute | solution.py:15
  60.0 0.6 copy-start.1

commit v4 on v3

--- a/solution.py
+++ b/solution.py
@@ -57,8 +57,9 @@
     rel_z = sources[5][None, :] - targets[5][:, None]
     dist_sq = gap_x * gap_x + gap_y * gap_y + gap_z * gap_z + soften_sq
     inverse = lax.rsqrt(dist_sq)
-    scaled = weight * (inverse * inverse * inverse)
-    radial = 3.0 * (gap_x * rel_x + gap_y * rel_y + gap_z * rel_z) / dist_sq
+    inverse_sq = inverse * inverse
+    scaled = weight * (inverse_sq * inverse)
+    radial = 3.0 * (gap_x * rel_x + gap_y * rel_y + gap_z * rel_z) * inverse_sq
     term_list = [
         gap_x,
         gap_y,

time: 61.9 us -> 64 us (1.034)
  other arithmetic: 21.5 us -> 23.9 us
    reduce_sum x9, other arithmetic: 17.9 us -> 20.3 us  [pair_sums(): return jnp.stack([jnp.sum(scaled * term, axis=1) for term in term_list])]
  transfers between devices with their start and end apart: 7 -> 7, of which waited for: 4 -> 4; matrix products, arithmetic and copies ran while one was open for 25% -> 26% of each run, Pallas kernels for 0% -> 0%
where the time goes in v4:
time: 64 us; the launch traced here: 63.3 us
  other arithmetic  23.9 us (37%)
  starting transfers between devices  22.6 us (35%)
  local copies, waits for them, and re-layouts  9.8 us (15%)
  waiting for transfers between devices  5.2 us (8%)
  between operations  1.51 us (2%)
    reduce_sum x9, other arithmetic, pair_sums(): return jnp.stack([jnp.sum(scaled * term, axis=1) for term in term_list])  20.3 us
    ppermute x6, starting transfers between devices, exchange(): return lax.ppermute(block, axis, [(i, i ^ bit) for i in range(size)])  13.8 us
    all_to_all x1, starting transfers between devices, gather_all_to_all(): got = lax.all_to_all(spread, axis, 1, 1, tiled=True)  8.76 us
    ppermute x6, waiting for transfers between devices, exchange(): return lax.ppermute(block, axis, [(i, i ^ bit) for i in range(size)])  5.05 us
    unnamed x16, local copies, waits for them, and re-layouts  3.22 us
  transfers between devices with their start and end apart: 7, of which 4 were waited for; matrix products, arithmetic and copies ran while one was open for 26% of the time, Pallas kernels for 0%

profile of v4, /device:TPU:32, one launch (start us, length us, event | category | flops | bytes accessed | tf_op | source)
XLA Modules:
  0.0 63.3 jit_solution(15167056065759199445)
XLA Ops:
  0.6 0.7 %broadcast_multiply_fusion = f32[256]{0:T(256)S(1)} fusion(f32[256]{0:T(256)} %param.19), kind=kLoop, calls=%fused_computation.177 | loop fusion | flops 256 | bytes 2048 | tf_op jit(solution)/shard_map/mul | solution.py:88
  1.4 0.7 %multiply_add_fusion.1 = (f32[3,256]{1,0:T(4,128)S(1)}, f32[3,256]{1,0:T(4,128)S(1)}) fusion(f32[3,256]{1,0:T(4,128)} %param.15, f32[3,256]{1,0:T(4,128)} %param.16, f32[3,256]{1,0:T(4,128)} %param.18, f32[3,256]{1,0:T(4,128)} %param.17, f32[256]{0:T(256)S(1)} %copy-done, f32[256]{0:T(256)S(1)} %broadcast_multiply_fusion), kind=kLoop, calls=%fused_computation.159 | loop fusion | flops 9216 | bytes 20480 | tf_op jit(solution)/shard_map/add | solution.py:85
  2.2 0.1 copy.97
  2.3 0.5 copy-done.5
  2.8 0.7 %gather_fusion.1 = f32[32]{0:T(128)S(1)} fusion(f32[256]{0:T(256)S(1)} %copy-done, s32[1024]{0:T(1024)S(1)} %pad_clamp_fusion), kind=kCustom, calls=%fused_computation.3 | custom fusion | bytes 384 | tf_op jit(solution)/shard_map/jit(_take)/gather | solution.py:134
  3.5 0.6 gather_fusion
  4.2 3.1 %collective-permute-start = (f32[6,32]{0,1:T(8,128)S(1)}, f32[6,32]{0,1:T(8,128)S(1)}, u32[]{:S(2)}, u32[]{:S(2)}) collective-permute-start(f32[6,32]{0,1:T(8,128)S(1)} %select_bitcast_fusion), channel_id=1, source_target_pairs={{0,32},{32,0},{64,96},{96,64},{128,160},{160,128},{192,224},{224,1... | collective-permute-start | bytes 2312 | tf_op jit(solution)/shard_map/ppermute | solution.py:15
  7.3 0.7 %broadcast_in_dim.99 = f32[7,32,256]{2,0,1:T(8,128)} broadcast(f32[7,256]{1,0:T(8,128)S(1)} %pad_maximum_fusion), dimensions={0,2} | broadcast | bytes 236544 | tf_op jit(solution)/shard_map/broadcast_in_dim | solution.py:46
  8.0 8.8 %all-to-all-start = ((f32[7,32,256]{2,0,1:T(8,128)}), f32[7,32,256]{2,0,1:T(8,128)S(1)}, u32[]{:S(2)}, u32[]{:S(2)}) async-start(f32[7,32,256]{2,0,1:T(8,128)} %broadcast_in_dim.99), calls=%async_computation | async-start | bytes 524288 | tf_op jit(solution)/shard_map/all_to_all | solution.py:47
  17.5 0.6 %copy-done.6 = s32[1,64]{1,0:T(1,128)S(1)} copy-done((s32[1,64]{1,0:T(1,128)S(1)}, s32[1,64]{1,0:T(1,128)}, u32[]{:S(2)}) %copy-start.6) | copy-done | bytes 280
  18.1 0.1 fusion.66
  18.3 0.1 copy.99
  18.3 0.1 copy.98
  18.4 0.1 maximum_select_fusion.1
  18.5 1.6 %collective-permute-start.1 = (f32[6,64]{1,0:T(8,128)S(1)}, f32[6,64]{1,0:T(8,128)S(1)}, u32[]{:S(2)}, u32[]{:S(2)}) collective-permute-start(f32[6,64]{1,0:T(8,128)S(1)} %maximum_select_fusion.1), channel_id=1, source_target_pairs={{0,64},{32,96},{64,0},{96,32},{128,192},{160,224},{192,128},{224,1... | collective-permute-start | bytes 4616 | tf_op jit(solution)/shard_map/ppermute | solution.py:15
  20.2 2.0 %collective-permute-done.1 = f32[6,64]{1,0:T(8,128)S(1)} collective-permute-done((f32[6,64]{1,0:T(8,128)S(1)}, f32[6,64]{1,0:T(8,128)S(1)}, u32[]{:S(2)}, u32[]{:S(2)}) %collective-permute-start.1) | collective-permute-done | bytes 1568 | tf_op jit(solution)/shard_map/ppermute | solution.py:15
  22.1 0.1 maximum_select_fusion.2
  22.2 3.2 %collective-permute-start.2 = (f32[6,128]{1,0:T(8,128)S(1)}, f32[6,128]{1,0:T(8,128)S(1)}, u32[]{:S(2)}, u32[]{:S(2)}) collective-permute-start(f32[6,128]{1,0:T(8,128)S(1)} %maximum_select_fusion.2), channel_id=1, source_target_pairs={{0,128},{32,160},{64,192},{96,224},{128,0},{160,32},{192,64},{224,... | collective-permute-start | bytes 9224 | tf_op jit(solution)/shard_map/ppermute | solution.py:15
  25.4 0.3 slice_reduce_fusion.1
  25.7 0.7 %copy-done.2 = f32[3,256]{1,0:T(4,128)S(1)} copy-done((f32[3,256]{1,0:T(4,128)S(1)}, f32[3,256]{1,0:T(4,128)}, u32[]{:S(2)}) %copy-start.2) | copy-done | bytes 3096
  26.4 0.1 copy.106
  26.5 0.5 copy-done.3
  27.1 0.1 copy.108
  27.2 0.6 gather_fusion.2
  27.8 0.1 copy.107
  27.9 0.6 gather_fusion.3
  28.4 0.1 copy.109
  28.5 0.1 reshape.163
  28.6 0.1 reshape.161
  28.7 0.2 all-to-all-done
  28.9 0.2 fusion.75
  29.0 10.3 %while.21 = (s32[]{:T(128)}, f32[4,6,32]{2,1,0:T(8,128)S(1)}, f32[4,64]{1,0:T(4,128)S(1)}, f32[1,8192]{1,0:T(1,128)S(1)}, f32[6,8192]{1,0:T(8,128)S(1)}, /*index...) while((s32[]{:T(128)}, f32[4,6,32]{2,1,0:T(8,128)S(1)}, ...), condition=%wide.region_16.17_spmd, body=%wide.region_9.16_spmd.sunk | while | flops 10493767 | bytes 701913 | solution.py:123
  29.1 0.1 fusion.89
  29.2 0.1 bitcast_multiply_fusion.7
  29.3 2.3 %fusion.91 = (f32[32]{0:T(128)S(1)}, f32[32]{0:T(128)S(1)}, f32[32]{0:T(128)S(1)}, f32[32]{0:T(128)S(1)}, f32[32]{0:T(128)S(1)}, /*index=5*/f32[32]{0:T(128)S(1)}) fusion(f32[32]{0:T(128)S(1)} %get-tuple-element.346, f32[8192]{0:T(1024)S(1)} %bitcast.207, f32[32]{0:T(128)S(1)} %get-tuple-element.348, f32[8192]{0:T(1024)S(1)} %bitcast.209, ...), kind=kLoop, calls=%fused_computation.77.clone.1 | loop fusion | flops 10485568 | bytes 230912 | tf_op jit(solution)/shard_map/while/body/eval_jaxpr/reduce_sum | solution.py:71
  31.7 0.1 fusion.89
  31.9 2.3 %fusion.91 = (f32[32]{0:T(128)S(1)}, f32[32]{0:T(128)S(1)}, f32[32]{0:T(128)S(1)}, f32[32]{0:T(128)S(1)}, f32[32]{0:T(128)S(1)}, /*index=5*/f32[32]{0:T(128)S(1)}) fusion(f32[32]{0:T(128)S(1)} %get-tuple-element.346, f32[8192]{0:T(1024)S(1)} %bitcast.207, f32[32]{0:T(128)S(1)} %get-tuple-element.348, f32[8192]{0:T(1024)S(1)} %bitcast.209, ...), kind=kLoop, calls=%fused_computation.77.clone.1 | loop fusion | flops 10485568 | bytes 230912 | tf_op jit(solution)/shard_map/while/body/eval_jaxpr/reduce_sum | solution.py:71
  34.2 0.1 fusion.89
  34.5 2.3 %fusion.91 = (f32[32]{0:T(128)S(1)}, f32[32]{0:T(128)S(1)}, f32[32]{0:T(128)S(1)}, f32[32]{0:T(128)S(1)}, f32[32]{0:T(128)S(1)}, /*index=5*/f32[32]{0:T(128)S(1)}) fusion(f32[32]{0:T(128)S(1)} %get-tuple-element.346, f32[8192]{0:T(1024)S(1)} %bitcast.207, f32[32]{0:T(128)S(1)} %get-tuple-element.348, f32[8192]{0:T(1024)S(1)} %bitcast.209, ...), kind=kLoop, calls=%fused_computation.77.clone.1 | loop fusion | flops 10485568 | bytes 230912 | tf_op jit(solution)/shard_map/while/body/eval_jaxpr/reduce_sum | solution.py:71
  36.8 0.1 fusion.89
  37.0 0.1 bitcast_multiply_fusion.7
  37.1 2.3 %fusion.91 = (f32[32]{0:T(128)S(1)}, f32[32]{0:T(128)S(1)}, f32[32]{0:T(128)S(1)}, f32[32]{0:T(128)S(1)}, f32[32]{0:T(128)S(1)}, /*index=5*/f32[32]{0:T(128)S(1)}) fusion(f32[32]{0:T(128)S(1)} %get-tuple-element.346, f32[8192]{0:T(1024)S(1)} %bitcast.207, f32[32]{0:T(128)S(1)} %get-tuple-element.348, f32[8192]{0:T(1024)S(1)} %bitcast.209, ...), kind=kLoop, calls=%fused_computation.77.clone.1 | loop fusion | flops 10485568 | bytes 230912 | tf_op jit(solution)/shard_map/while/body/eval_jaxpr/reduce_sum | solution.py:71
  39.4 0.1 reshape.164
  39.5 3.2 %collective-permute-start.3 = (f32[6,128]{1,0:T(8,128)S(1)}, f32[6,128]{1,0:T(8,128)S(1)}, u32[]{:S(2)}, u32[]{:S(2)}) collective-permute-start(f32[6,128]{1,0:T(8,128)S(1)} %reshape.164), channel_id=1, source_target_pairs={{0,128},{32,160},{64,192},{96,224},{128,0},{160,32},{192,64},{224,... | collective-permute-start | bytes 9224 | tf_op jit(solution)/shard_map/ppermute | solution.py:15
  42.7 10.3 %while.20 = (s32[]{:T(128)}, f32[4,6,32]{2,1,0:T(8,128)S(1)}, f32[4,64]{1,0:T(4,128)S(1)}, f32[1,8192]{1,0:T(1,128)S(1)}, f32[6,8192]{1,0:T(8,128)S(1)}, /*index...) while((s32[]{:T(128)}, f32[4,6,32]{2,1,0:T(8,128)S(1)}, ...), condition=%wide.region_8.9_spmd, body=%wide.region_1.8_spmd.sunk | while | flops 10493767 | bytes 701913 | solution.py:123
  42.7 0.1 fusion.85
  42.9 2.3 %fusion.87 = (f32[32]{0:T(128)S(1)}, f32[32]{0:T(128)S(1)}, f32[32]{0:T(128)S(1)}, f32[32]{0:T(128)S(1)}, f32[32]{0:T(128)S(1)}, /*index=5*/f32[32]{0:T(128)S(1)}) fusion(f32[32]{0:T(128)S(1)} %get-tuple-element.322, f32[8192]{0:T(1024)S(1)} %bitcast.213, f32[32]{0:T(128)S(1)} %get-tuple-element.324, f32[8192]{0:T(1024)S(1)} %bitcast.215, ...), kind=kLoop, calls=%fused_computation.27.clone.1 | loop fusion | flops 10485568 | bytes 230912 | tf_op jit(solution)/shard_map/while/body/eval_jaxpr/reduce_sum | solution.py:71
  45.3 0.1 fusion.85
  45.5 2.3 %fusion.87 = (f32[32]{0:T(128)S(1)}, f32[32]{0:T(128)S(1)}, f32[32]{0:T(128)S(1)}, f32[32]{0:T(128)S(1)}, f32[32]{0:T(128)S(1)}, /*index=5*/f32[32]{0:T(128)S(1)}) fusion(f32[32]{0:T(128)S(1)} %get-tuple-element.322, f32[8192]{0:T(1024)S(1)} %bitcast.213, f32[32]{0:T(128)S(1)} %get-tuple-element.324, f32[8192]{0:T(1024)S(1)} %bitcast.215, ...), kind=kLoop, calls=%fused_computation.27.clone.1 | loop fusion | flops 10485568 | bytes 230912 | tf_op jit(solution)/shard_map/while/body/eval_jaxpr/reduce_sum | solution.py:71
  47.8 0.1 fusion.85
  48.1 2.3 %fusion.87 = (f32[32]{0:T(128)S(1)}, f32[32]{0:T(128)S(1)}, f32[32]{0:T(128)S(1)}, f32[32]{0:T(128)S(1)}, f32[32]{0:T(128)S(1)}, /*index=5*/f32[32]{0:T(128)S(1)}) fusion(f32[32]{0:T(128)S(1)} %get-tuple-element.322, f32[8192]{0:T(1024)S(1)} %bitcast.213, f32[32]{0:T(128)S(1)} %get-tuple-element.324, f32[8192]{0:T(1024)S(1)} %bitcast.215, ...), kind=kLoop, calls=%fused_computation.27.clone.1 | loop fusion | flops 10485568 | bytes 230912 | tf_op jit(solution)/shard_map/while/body/eval_jaxpr/reduce_sum | solution.py:71
  50.4 0.1 fusion.85
  50.7 2.3 %fusion.87 = (f32[32]{0:T(128)S(1)}, f32[32]{0:T(128)S(1)}, f32[32]{0:T(128)S(1)}, f32[32]{0:T(128)S(1)}, f32[32]{0:T(128)S(1)}, /*index=5*/f32[32]{0:T(128)S(1)}) fusion(f32[32]{0:T(128)S(1)} %get-tuple-element.322, f32[8192]{0:T(1024)S(1)} %bitcast.213, f32[32]{0:T(128)S(1)} %get-tuple-element.324, f32[8192]{0:T(1024)S(1)} %bitcast.215, ...), kind=kLoop, calls=%fused_computation.27.clone.1 | loop fusion | flops 10485568 | bytes 230912 | tf_op jit(solution)/shard_map/while/body/eval_jaxpr/reduce_sum | solution.py:71
  53.0 0.1 reshape.162
  53.1 0.1 slice_select_fusion.1
  53.1 0.7 %collective-permute-start.4 = (f32[6,64]{1,0:T(8,128)S(1)}, f32[6,64]{1,0:T(8,128)S(1)}, u32[]{:S(2)}, u32[]{:S(2)}) collective-permute-start(f32[6,64]{1,0:T(8,128)S(1)} %slice_select_fusion.1), channel_id=1, source_target_pairs={{0,64},{32,96},{64,0},{96,32},{128,192},{160,224},{192,128},{224,1... | collective-permute-start | bytes 4616 | tf_op jit(solution)/shard_map/ppermute | solution.py:15
  53.9 2.9 %collective-permute-done.4 = f32[6,64]{1,0:T(8,128)S(1)} collective-permute-done((f32[6,64]{1,0:T(8,128)S(1)}, f32[6,64]{1,0:T(8,128)S(1)}, u32[]{:S(2)}, u32[]{:S(2)}) %collective-permute-start.4) | collective-permute-done | bytes 1568 | tf_op jit(solution)/shard_map/ppermute | solution.py:15
  56.8 0.1 slice_select_fusion
  56.9 2.0 %collective-permute-start.5 = (f32[6,32]{1,0:T(8,128)S(1)}, f32[6,32]{1,0:T(8,128)S(1)}, u32[]{:S(2)}, u32[]{:S(2)}) collective-permute-start(f32[6,32]{1,0:T(8,128)S(1)} %slice_select_fusion), channel_id=1, source_target_pairs={{0,32},{32,0},{64,96},{96,64},{128,160},{160,128},{192,224},{224,1... | collective-permute-start | bytes 2312 | tf_op jit(solution)/shard_map/ppermute | solution.py:15
  58.9 2.3 %fusion.54 = (f32[32]{0:T(128)S(1)}, f32[32]{0:T(128)S(1)}, f32[32]{0:T(128)S(1)}, f32[32]{0:T(128)S(1)}, f32[32]{0:T(128)S(1)}, /*index=5*/f32[32]{0:T(128)S(1)}) fusion(f32[32]{0:T(128)S(1)} %get-tuple-element.153, f32[8192]{0:T(1024)S(1)} %bitcast.223, f32[32]{0:T(128)S(1)} %get-tuple-element.150, f32[8192]{0:T(1024)S(1)} %bitcast.225, ...), kind=kLoop, calls=%fused_computation.127 | loop fusion | flops 10485568 | bytes 230912 | tf_op jit(solution)/shard_map/reduce_sum | solution.py:71
  61.2 0.6 stack.73
  61.8 0.2 collective-permute-done.5
  62.1 0.6 copy-done.1
  62.7 0.6 pad_maximum_fusion.2
  (74 shorter events, 1.5 us)
Async XLA Ops:
  0.6 0.8 %copy-start = (f32[256]{0:T(256)S(1)}, f32[256]{0:T(256)}, u32[]{:S(2)}) copy-start(f32[256]{0:T(256)} %param.19) | copy-start | bytes 3076
  2.2 0.7 %copy-start.5 = (s32[32]{0:T(128)S(1)}, s32[32]{0:T(128)}, u32[]{:S(2)}) copy-start(s32[32]{0:T(128)} %param.21) | copy-start | bytes 388
  4.2 3.1 %copy-start.4 = (f32[256]{0:T(256)S(1)}, f32[256]{0:T(256)}, u32[]{:S(2)}) copy-start(f32[256]{0:T(256)} %param.20) | copy-start | bytes 3076
  4.2 14.1 %collective-permute-start = (f32[6,32]{0,1:T(8,128)S(1)}, f32[6,32]{0,1:T(8,128)S(1)}, u32[]{:S(2)}, u32[]{:S(2)}) collective-permute-start(f32[6,32]{0,1:T(8,128)S(1)} %select_bitcast_fusion), channel_id=1, source_target_pairs={{0,32},{32,0},{64,96},{96,64},{128,160},{160,128},{192,224},{224,1... | collective-permute-start | bytes 2312 | tf_op jit(solution)/shard_map/ppermute | solution.py:15
  8.0 20.9 %all-to-all-start = ((f32[7,32,256]{2,0,1:T(8,128)}), f32[7,32,256]{2,0,1:T(8,128)S(1)}, u32[]{:S(2)}, u32[]{:S(2)}) async-start(f32[7,32,256]{2,0,1:T(8,128)} %broadcast_in_dim.99), calls=%async_computation | async-start | bytes 524288 | tf_op jit(solution)/shard_map/all_to_all | solution.py:47
  17.5 0.7 %copy-start.6 = (s32[1,64]{1,0:T(1,128)S(1)}, s32[1,64]{1,0:T(1,128)}, u32[]{:S(2)}) copy-start(s32[1,64]{1,0:T(1,128)} %param.22) | copy-start | bytes 772
  18.5 3.6 %collective-permute-start.1 = (f32[6,64]{1,0:T(8,128)S(1)}, f32[6,64]{1,0:T(8,128)S(1)}, u32[]{:S(2)}, u32[]{:S(2)}) collective-permute-start(f32[6,64]{1,0:T(8,128)S(1)} %maximum_select_fusion.1), channel_id=1, source_target_pairs={{0,64},{32,96},{64,0},{96,32},{128,192},{160,224},{192,128},{224,1... | collective-permute-start | bytes 4616 | tf_op jit(solution)/shard_map/ppermute | solution.py:15
  22.2 6.3 %collective-permute-start.2 = (f32[6,128]{1,0:T(8,128)S(1)}, f32[6,128]{1,0:T(8,128)S(1)}, u32[]{:S(2)}, u32[]{:S(2)}) collective-permute-start(f32[6,128]{1,0:T(8,128)S(1)} %maximum_select_fusion.2), channel_id=1, source_target_pairs={{0,128},{32,160},{64,192},{96,224},{128,0},{160,32},{192,64},{224,... | collective-permute-start | bytes 9224 | tf_op jit(solution)/shard_map/ppermute | solution.py:15
  25.7 0.7 %copy-start.2 = (f32[3,256]{1,0:T(4,128)S(1)}, f32[3,256]{1,0:T(4,128)}, u32[]{:S(2)}) copy-start(f32[3,256]{1,0:T(4,128)} %param.17) | copy-start | bytes 9220
  26.4 0.7 %copy-start.3 = (f32[3,256]{1,0:T(4,128)S(1)}, f32[3,256]{1,0:T(4,128)}, u32[]{:S(2)}) copy-start(f32[3,256]{1,0:T(4,128)} %param.18) | copy-start | bytes 9220
  39.5 13.6 %collective-permute-start.3 = (f32[6,128]{1,0:T(8,128)S(1)}, f32[6,128]{1,0:T(8,128)S(1)}, u32[]{:S(2)}, u32[]{:S(2)}) collective-permute-start(f32[6,128]{1,0:T(8,128)S(1)} %reshape.164), channel_id=1, source_target_pairs={{0,128},{32,160},{64,192},{96,224},{128,0},{160,32},{192,64},{224,... | collective-permute-start | bytes 9224 | tf_op jit(solution)/shard_map/ppermute | solution.py:15
  53.1 3.6 %collective-permute-start.4 = (f32[6,64]{1,0:T(8,128)S(1)}, f32[6,64]{1,0:T(8,128)S(1)}, u32[]{:S(2)}, u32[]{:S(2)}) collective-permute-start(f32[6,64]{1,0:T(8,128)S(1)} %slice_select_fusion.1), channel_id=1, source_target_pairs={{0,64},{32,96},{64,0},{96,32},{128,192},{160,224},{192,128},{224,1... | collective-permute-start | bytes 4616 | tf_op jit(solution)/shard_map/ppermute | solution.py:15
  56.9 5.1 %collective-permute-start.5 = (f32[6,32]{1,0:T(8,128)S(1)}, f32[6,32]{1,0:T(8,128)S(1)}, u32[]{:S(2)}, u32[]{:S(2)}) collective-permute-start(f32[6,32]{1,0:T(8,128)S(1)} %slice_select_fusion), channel_id=1, source_target_pairs={{0,32},{32,0},{64,96},{96,64},{128,160},{160,128},{192,224},{224,1... | collective-permute-start | bytes 2312 | tf_op jit(solution)/shard_map/ppermute | solution.py:15
  62.1 0.6 copy-start.1

commit v5 on v2

v5 whole, which is shorter than its diff:
```python
import jax
import jax.numpy as jnp
from jax import lax
from jax.sharding import PartitionSpec as P


BLOCK = 128


soften_sq = 0.0001


def exchange(block, axis, bit):
    size = lax.axis_size(axis)
    return lax.ppermute(block, axis, [(i, i ^ bit) for i in range(size)])


def gather_doubling(block, axis):
    me = lax.axis_index(axis)
    bit = 1
    while bit < lax.axis_size(axis):
        got = exchange(block, axis, bit)
        upper = (me // bit) % 2 == 1
        block = jnp.where(
            upper, jnp.concatenate([got, block], 1), jnp.concatenate([block, got], 1)
        )
        bit *= 2
    return block


def gather_doubling_split(block, axis):
    me = lax.axis_index(axis)
    last = lax.axis_size(axis) // 2
    bit = 1
    while bit < last:
        got = exchange(block, axis, bit)
        upper = (me // bit) % 2 == 1
        block = jnp.where(
            upper, jnp.concatenate([got, block], 1), jnp.concatenate([block, got], 1)
        )
        bit *= 2
    got = exchange(block, axis, last)
    return block, got


def pair_terms(targets, sources):
    gap_x = sources[0][None, :] - targets[0][:, None]
    gap_y = sources[1][None, :] - targets[1][:, None]
    gap_z = sources[2][None, :] - targets[2][:, None]
    rel_x = sources[3][None, :] - targets[3][:, None]
    rel_y = sources[4][None, :] - targets[4][:, None]
    rel_z = sources[5][None, :] - targets[5][:, None]
    dist_sq = gap_x * gap_x + gap_y * gap_y + gap_z * gap_z + soften_sq
    inverse = lax.rsqrt(dist_sq)
    inv_cube = inverse * inverse * inverse
    radial = 3.0 * (gap_x * rel_x + gap_y * rel_y + gap_z * rel_z) / dist_sq
    term_list = [
        gap_x,
        gap_y,
        gap_z,
        rel_x - radial * gap_x,
        rel_y - radial * gap_y,
        rel_z - radial * gap_z,
    ]
    return inv_cube, term_list


def pair_sums(targets, sources, weight):
    inv_cube, term_list = pair_terms(targets, sources)
    scaled = weight * inv_cube
    return jnp.stack([jnp.sum(scaled * term, axis=1) for term in term_list])


def pair_sums_split(targets, sources, far_weight, near_weight):
    inv_cube, term_list = pair_terms(targets, sources)
    far_scaled = far_weight * inv_cube
    near_scaled = near_weight * inv_cube
    far = jnp.stack([jnp.sum(far_scaled * term, axis=1) for term in term_list])
    near = jnp.stack([jnp.sum(near_scaled * term, axis=1) for term in term_list])
    return far, near


def per_device(
    position,
    velocity,
    accel_old,
    jerk_old,
    elapsed,
    masses,
    active_stars,
    neighbour_list,
    neighbour_count,
):
    moved_pos = position + elapsed * (
        velocity + elapsed * (0.5 * accel_old + elapsed * jerk_old / 6.0)
    )
    turned = velocity + elapsed * (accel_old + 0.5 * elapsed * jerk_old)
    sources = jnp.concatenate([moved_pos, turned], axis=0)
    own_set = jnp.take(sources, active_stars, axis=1)
    act_dev = active_stars.shape[0]
    block_data = jnp.concatenate([sources, masses[None, :]], axis=0)
    targets = gather_doubling(own_set, "blk")
    near_half, far_half = gather_doubling_split(block_data, "grp")
    blk_size = lax.axis_size("blk")
    blk_here = lax.axis_index("blk")
    block_total = lax.axis_size("grp") * block_data.shape[1] // BLOCK
    slot_total = neighbour_list.shape[1]
    own_live = jnp.arange(slot_total) < neighbour_count[0]
    near = jnp.any(
        own_live[:, None]
        & (neighbour_list[0][:, None] == jnp.arange(block_total)[None, :]),
        axis=0,
    ).astype(jnp.float32)
    grp_here = lax.axis_index("grp")
    half_devices = lax.axis_size("grp") // 2
    blocks_half = near_half.shape[1] // BLOCK
    blocks_device = block_data.shape[1] // BLOCK
    near_start = (grp_here - grp_here % half_devices) * blocks_device
    far_device = grp_here ^ half_devices
    far_start = (far_device - far_device % half_devices) * blocks_device
    near_a = lax.dynamic_slice_in_dim(near, near_start, blocks_half)
    near_b = lax.dynamic_slice_in_dim(near, far_start, blocks_half)
    src_a, mass_a = near_half[:6], near_half[6]
    src_b, mass_b = far_half[:6], far_half[6]

    owners = jnp.arange(blk_size)
    keep = jnp.where((owners == blk_here)[:, None], 1.0 - near_a[None, :], 1.0)
    pieces = targets.reshape(6, blk_size, act_dev).transpose(1, 0, 2)

    def first_piece(items):
        target_piece, keep_piece = items
        piece_weight = jnp.repeat(keep_piece, BLOCK)[None, :] * mass_a[None, :]
        return pair_sums(target_piece, src_a, piece_weight)

    first = lax.map(first_piece, (pieces, keep))
    first = first.transpose(1, 0, 2).reshape(6, blk_size * act_dev)
    irregular_a = pair_sums(
        own_set, src_a, (jnp.repeat(near_a, BLOCK) * mass_a)[None, :]
    )

    weight = mass_b[None, :]

    def owner_sums(start, count):
        pieces = lax.dynamic_slice_in_dim(targets, start * act_dev, count * act_dev, 1)
        done = lax.dynamic_slice_in_dim(first, start * act_dev, count * act_dev, 1)
        if count == 1:
            return pair_sums(pieces, src_b, weight) + done
        pieces = pieces.reshape(6, count, act_dev).transpose(1, 0, 2)
        sums = lax.map(lambda piece: pair_sums(piece, src_b, weight), pieces)
        return sums.transpose(1, 0, 2).reshape(6, count * act_dev) + done

    def owner_cols(block, owner, span):
        return lax.dynamic_slice_in_dim(block, (owner % span) * act_dev, act_dev, 1)

    bit4, bit2 = blk_size // 2, blk_size // 4
    base4 = blk_here - blk_here % bit4
    start4 = blk_here - blk_here % (2 * bit4) + ((blk_here // bit4 + 1) % 2) * bit4
    sent4 = owner_sums(start4, bit4)
    got4 = exchange(sent4, "blk", bit4)
    start2 = base4 + ((blk_here // bit2 + 1) % 2) * bit2
    sent2 = owner_sums(start2, bit2) + lax.dynamic_slice_in_dim(
        got4, (start2 - base4) * act_dev, bit2 * act_dev, 1
    )
    got2 = exchange(sent2, "blk", bit2)
    partner = blk_here ^ 1
    sent1 = (
        owner_sums(partner, 1)
        + owner_cols(got4, partner, bit4)
        + owner_cols(got2, partner, bit2)
    )
    got1 = exchange(sent1, "blk", 1)
    near_rep = jnp.repeat(near_b, BLOCK)[None, :]
    own_far, irregular_b = pair_sums_split(
        own_set, src_b, weight * (1.0 - near_rep), weight * near_rep
    )
    regular = (
        own_far
        + owner_cols(first, blk_here, blk_size)
        + owner_cols(got4, blk_here, bit4)
        + owner_cols(got2, blk_here, bit2)
        + got1
    )
    irregular = irregular_a + irregular_b
    accel_now = regular[:3] + irregular[:3]
    jerk_now = regular[3:] + irregular[3:]
    step_time = jnp.take(elapsed, active_stars)
    start_accel = jnp.take(accel_old, active_stars, axis=1)
    start_jerk = jnp.take(jerk_old, active_stars, axis=1)
    change = start_accel - accel_now
    snap_term = -6.0 * change - step_time * (4.0 * start_jerk + 2.0 * jerk_now)
    crackle_term = 12.0 * change + 6.0 * step_time * (start_jerk + jerk_now)
    return (regular, irregular, jnp.concatenate([snap_term, crackle_term], axis=0))


def solution(mesh):
    in_specs = (
        P(None, ("blk", "grp")),
        P(None, ("blk", "grp")),
        P(None, ("blk", "grp")),
        P(None, ("blk", "grp")),
        P(("blk", "grp")),
        P(("blk", "grp")),
        P(("blk", "grp")),
        P(("blk", "grp"), None),
        P(("blk", "grp")),
    )
    out_specs = (P(None, ("blk", "grp")), P(None, ("blk", "grp")), P(None, ("blk", "grp")))

    return jax.shard_map(
        per_device, mesh=mesh, in_specs=in_specs, out_specs=out_specs, check_vma=False
    )
```

time: 65.8 us -> 89.4 us (1.36); the launches traced: 65.1 us -> 87.7 us
  local copies, waits for them, and re-layouts: 10.3 us -> 20.5 us
  waiting for transfers between devices: 7.43 us -> 15.9 us
  other arithmetic: 21.6 us -> 24.1 us
  starting transfers between devices: 23.9 us -> 25.1 us
    ppermute x6 -> x11, starting transfers between devices: 14.3 us -> 25.1 us  [exchange(): return lax.ppermute(block, axis, [(i, i ^ bit) for i in range(size)])]
    slice x10 -> x15, local copies, waits for them, and re-layouts: 1.53 us -> 11.8 us  [the longest x14 11.5 us: pair_terms(): rel_x = sources[3][None, :] - targets[3][:, None]]
    all_to_all x1 -> x0, starting transfers between devices: 9.66 us -> none  [gather_all_to_all(): got = lax.all_to_all(spread, axis, 1, 1, tiled=True)]
    ppermute x6 -> x11, waiting for transfers between devices: 7.42 us -> 15.9 us  [exchange(): return lax.ppermute(block, axis, [(i, i ^ bit) for i in range(size)])]
    slice x0 -> x1, other arithmetic: none -> 1.52 us  [pair_terms(): rel_x = sources[3][None, :] - targets[3][:, None]]
    reduce_sum x0 -> x1, other arithmetic: none -> 1.46 us  [pair_sums_split(): jnp.sum(near_scaled * term, axis=1)]
    reduce_sum x9 -> x16, other arithmetic: 17.9 us -> 16.7 us  [pair_sums(): return jnp.stack([jnp.sum(scaled * term, axis=1) for term in term_list])]
    unnamed x16 -> x18, local copies, waits for them, and re-layouts: 3.64 us -> 3.87 us
  transfers between devices with their start and end apart: 7 -> 11, of which waited for: 4 -> 8; matrix products, arithmetic and copies ran while one was open for 11% -> 35% of each run, Pallas kernels for 0% -> 0%
where the time goes in v5:
time: 89.4 us; the launch traced here: 87.7 us
  starting transfers between devices  25.1 us (28%)
  other arithmetic  24.1 us (27%)
  local copies, waits for them, and re-layouts  20.5 us (23%)
  waiting for transfers between devices  15.9 us (18%)
  between operations  1.57 us (2%)
    ppermute x11, starting transfers between devices, exchange(): return lax.ppermute(block, axis, [(i, i ^ bit) for i in range(size)])  25.1 us
    reduce_sum x16, other arithmetic, pair_sums(): return jnp.stack([jnp.sum(scaled * term, axis=1) for term in term_list])  16.7 us
    ppermute x11, waiting for transfers between devices, exchange(): return lax.ppermute(block, axis, [(i, i ^ bit) for i in range(size)])  15.9 us
    slice x14, local copies, waits for them, and re-layouts, pair_terms(): rel_x = sources[3][None, :] - targets[3][:, None]  11.5 us
    unnamed x18, local copies, waits for them, and re-layouts  3.87 us
  transfers between devices with their start and end apart: 11, of which 8 were waited for; matrix products, arithmetic and copies ran while one was open for 35% of the time, Pallas kernels for 0%

profile of v5, /device:TPU:32, one launch (start us, length us, event | category | flops | bytes accessed | tf_op | source)
XLA Modules:
  0.0 87.7 jit_solution(10015567719264506248)
XLA Ops:
  0.6 0.7 broadcast_multiply_fusion
  1.4 0.7 multiply_add_fusion.1
  2.1 0.7 copy-done.5
  3.0 0.5 copy-done.6
  3.5 0.7 gather_fusion.1
  4.2 0.1 copy.172
  4.4 0.6 gather_fusion
  5.0 3.0 %collective-permute-start.5 = (f32[6,32]{0,1:T(8,128)S(1)}, f32[6,32]{0,1:T(8,128)S(1)}, u32[]{:S(2)}, u32[]{:S(2)}) collective-permute-start(f32[6,32]{0,1:T(8,128)S(1)} %bitcast_select_fusion.1), channel_id=1, source_target_pairs={{0,32},{32,0},{64,96},{96,64},{128,160},{160,128},{192,224},{224,1... | collective-permute-start | bytes 2312 | tf_op jit(solution)/shard_map/ppermute | solution.py:15
  8.1 0.3 slice_reduce_fusion.1
  8.5 0.6 copy-done.1
  9.1 0.1 copy.187
  9.2 0.5 copy-done.2
  10.7 0.6 copy-done.7
  11.7 0.6 gather_fusion.2
  12.3 0.6 gather_fusion.3
  13.2 1.6 %collective-permute-start.6 = (f32[6,64]{1,0:T(8,128)S(1)}, f32[6,64]{1,0:T(8,128)S(1)}, u32[]{:S(2)}, u32[]{:S(2)}) collective-permute-start(f32[6,64]{1,0:T(8,128)S(1)} %maximum_select_fusion.8), channel_id=1, source_target_pairs={{0,64},{32,96},{64,0},{96,32},{128,192},{160,224},{192,128},{224,1... | collective-permute-start | bytes 4616 | tf_op jit(solution)/shard_map/ppermute | solution.py:15
  14.8 2.0 %collective-permute-done.6 = f32[6,64]{1,0:T(8,128)S(1)} collective-permute-done((f32[6,64]{1,0:T(8,128)S(1)}, f32[6,64]{1,0:T(8,128)S(1)}, u32[]{:S(2)}, u32[]{:S(2)}) %collective-permute-start.6) | collective-permute-done | bytes 1568 | tf_op jit(solution)/shard_map/ppermute | solution.py:15
  16.9 3.2 %collective-permute-start.7 = (f32[6,128]{1,0:T(8,128)S(1)}, f32[6,128]{1,0:T(8,128)S(1)}, u32[]{:S(2)}, u32[]{:S(2)}) collective-permute-start(f32[6,128]{1,0:T(8,128)S(1)} %maximum_select_fusion.9), channel_id=1, source_target_pairs={{0,128},{32,160},{64,192},{96,224},{128,0},{160,32},{192,64},{224,... | collective-permute-start | bytes 9224 | tf_op jit(solution)/shard_map/ppermute | solution.py:15
  20.2 1.8 %collective-permute-done.7 = f32[6,128]{1,0:T(8,128)S(1)} collective-permute-done((f32[6,128]{1,0:T(8,128)S(1)}, f32[6,128]{1,0:T(8,128)S(1)}, u32[]{:S(2)}, u32[]{:S(2)}) %collective-permute-start.7) | collective-permute-done | bytes 3104 | tf_op jit(solution)/shard_map/ppermute | solution.py:15
  22.2 0.2 collective-permute-start.1
  22.4 3.6 %collective-permute-done.1 = f32[7,512]{1,0:T(8,128)S(1)} collective-permute-done((f32[7,512]{1,0:T(8,128)S(1)}, f32[7,512]{1,0:T(8,128)S(1)}, u32[]{:S(2)}, u32[]{:S(2)}) %collective-permute-start.1) | collective-permute-done | bytes 14368 | tf_op jit(solution)/shard_map/ppermute | solution.py:15
  26.0 3.6 %collective-permute-start.2 = (f32[7,1024]{1,0:T(8,128)S(1)}, f32[7,1024]{1,0:T(8,128)S(1)}, u32[]{:S(2)}, u32[]{:S(2)}) collective-permute-start(f32[7,1024]{1,0:T(8,128)S(1)} %maximum_select_fusion.2), channel_id=1, source_target_pairs={{0,4},{1,5},{2,6},{3,7},{4,0},{5,1},{6,2},{7,3},{8,12},{9,13},{10,... | collective-permute-start | bytes 86024 | tf_op jit(solution)/shard_map/ppermute | solution.py:15
  29.9 1.6 %collective-permute-done.2 = f32[7,1024]{1,0:T(8,128)S(1)} collective-permute-done((f32[7,1024]{1,0:T(8,128)S(1)}, f32[7,1024]{1,0:T(8,128)S(1)}, u32[]{:S(2)}, u32[]{:S(2)}) %collective-permute-start.2) | collective-permute-done | bytes 28704 | tf_op jit(solution)/shard_map/ppermute | solution.py:15
  31.5 5.7 %collective-permute-start.3 = (f32[7,2048]{1,0:T(8,128)S(1)}, f32[7,2048]{1,0:T(8,128)S(1)}, u32[]{:S(2)}, u32[]{:S(2)}) collective-permute-start(f32[7,2048]{1,0:T(8,128)S(1)} %maximum_select_fusion.1), channel_id=1, source_target_pairs={{0,8},{1,9},{2,10},{3,11},{4,12},{5,13},{6,14},{7,15},{8,0},{9,1},... | collective-permute-start | bytes 172040 | tf_op jit(solution)/shard_map/ppermute | solution.py:15
  37.2 2.5 %collective-permute-done.3 = f32[7,2048]{1,0:T(8,128)S(1)} collective-permute-done((f32[7,2048]{1,0:T(8,128)S(1)}, f32[7,2048]{1,0:T(8,128)S(1)}, u32[]{:S(2)}, u32[]{:S(2)}) %collective-permute-start.3) | collective-permute-done | bytes 57376 | tf_op jit(solution)/shard_map/ppermute | solution.py:15
  39.8 0.7 maximum_select_fusion
  40.4 0.6 collective-permute-start.4
  41.1 1.5 %fusion.130 = (f32[1,4096]{1,0:T(1,128)S(1)}, f32[1,4096]{1,0:T(1,128)S(1)}, f32[1,4096]{1,0:T(1,128)S(1)}, f32[1,4096]{1,0:T(1,128)S(1)}, f32[1,4096]{1,0:T(1,1...) fusion(f32[7,4096]{1,0:T(8,128)} %maximum_select_fusion, f32[1,4096]{1,0:T(1,128)S(1)} %bitcast.330), kind=kLoop, calls=%fused_computation.316 | loop fusion | flops 4096 | bytes 262144 | tf_op jit(solution)/shard_map/slice | solution.py:50
  42.6 20.8 %while.30 = (s32[]{:T(128)}, f32[8,6,32]{2,1,0:T(8,128)S(1)}, f32[8,32]{1,0:T(8,128)S(1)}, f32[1,4096]{1,0:T(1,128)S(1)}, f32[6,4096]{1,0:T(8,128)}, /*index=5*/...) while((s32[]{:T(128)}, f32[8,6,32]{2,1,0:T(8,128)S(1)}, ...), condition=%wide.region_14.15_spmd, body=%wide.region_7.14_spmd.sunk | while | flops 5246791 | bytes 357473 | solution.py:135
  42.8 1.4 %fusion.142 = (f32[1,4096]{1,0:T(1,128)S(1)}, f32[1,4096]{1,0:T(1,128)S(1)}, f32[1,4096]{1,0:T(1,128)S(1)}, f32[1,4096]{1,0:T(1,128)S(1)}, f32[1,4096]{1,0:T(1,128)S(1)}, /*index=5*/f32[1,4096]{1,0:T(1,128)S(1)}) fusion(f32[6,4096]{1,0:T(8,128)} %get-tuple-element.610), kind=kLoop, calls=%fused_computation.313.clone.1 | loop fusion | bytes 196608 | tf_op jit(solution)/shard_map/while/body/eval_jaxpr/slice | solution.py:50
  44.1 1.0 %fusion.144 = (f32[32]{0:T(128)S(1)}, f32[32]{0:T(128)S(1)}, f32[32]{0:T(128)S(1)}, f32[32]{0:T(128)S(1)}, f32[32]{0:T(128)S(1)}, /*index=5*/f32[32]{0:T(128)S(1)}) fusion(f32[32]{0:T(128)S(1)} %get-tuple-element.480, f32[4096]{0:T(1024)S(1)} %bitcast.310, f32[32]{0:T(128)S(1)} %get-tuple-element.482, f32[4096]{0:T(1024)S(1)} %bitcast.312, ...), kind=kLoop, calls=%fused_computation.25.clone.1 | loop fusion | flops 5242688 | bytes 116224 | tf_op jit(solution)/shard_map/while/body/eval_jaxpr/reduce_sum | solution.py:71
  45.4 1.4 %fusion.142 = (f32[1,4096]{1,0:T(1,128)S(1)}, f32[1,4096]{1,0:T(1,128)S(1)}, f32[1,4096]{1,0:T(1,128)S(1)}, f32[1,4096]{1,0:T(1,128)S(1)}, f32[1,4096]{1,0:T(1,128)S(1)}, /*index=5*/f32[1,4096]{1,0:T(1,128)S(1)}) fusion(f32[6,4096]{1,0:T(8,128)} %get-tuple-element.610), kind=kLoop, calls=%fused_computation.313.clone.1 | loop fusion | bytes 196608 | tf_op jit(solution)/shard_map/while/body/eval_jaxpr/slice | solution.py:50
  46.7 1.0 %fusion.144 = (f32[32]{0:T(128)S(1)}, f32[32]{0:T(128)S(1)}, f32[32]{0:T(128)S(1)}, f32[32]{0:T(128)S(1)}, f32[32]{0:T(128)S(1)}, /*index=5*/f32[32]{0:T(128)S(1)}) fusion(f32[32]{0:T(128)S(1)} %get-tuple-element.480, f32[4096]{0:T(1024)S(1)} %bitcast.310, f32[32]{0:T(128)S(1)} %get-tuple-element.482, f32[4096]{0:T(1024)S(1)} %bitcast.312, ...), kind=kLoop, calls=%fused_computation.25.clone.1 | loop fusion | flops 5242688 | bytes 116224 | tf_op jit(solution)/shard_map/while/body/eval_jaxpr/reduce_sum | solution.py:71
  48.0 1.4 %fusion.142 = (f32[1,4096]{1,0:T(1,128)S(1)}, f32[1,4096]{1,0:T(1,128)S(1)}, f32[1,4096]{1,0:T(1,128)S(1)}, f32[1,4096]{1,0:T(1,128)S(1)}, f32[1,4096]{1,0:T(1,128)S(1)}, /*index=5*/f32[1,4096]{1,0:T(1,128)S(1)}) fusion(f32[6,4096]{1,0:T(8,128)} %get-tuple-element.610), kind=kLoop, calls=%fused_computation.313.clone.1 | loop fusion | bytes 196608 | tf_op jit(solution)/shard_map/while/body/eval_jaxpr/slice | solution.py:50
  49.4 1.0 %fusion.144 = (f32[32]{0:T(128)S(1)}, f32[32]{0:T(128)S(1)}, f32[32]{0:T(128)S(1)}, f32[32]{0:T(128)S(1)}, f32[32]{0:T(128)S(1)}, /*index=5*/f32[32]{0:T(128)S(1)}) fusion(f32[32]{0:T(128)S(1)} %get-tuple-element.480, f32[4096]{0:T(1024)S(1)} %bitcast.310, f32[32]{0:T(128)S(1)} %get-tuple-element.482, f32[4096]{0:T(1024)S(1)} %bitcast.312, ...), kind=kLoop, calls=%fused_computation.25.clone.1 | loop fusion | flops 5242688 | bytes 116224 | tf_op jit(solution)/shard_map/while/body/eval_jaxpr/reduce_sum | solution.py:71
  50.6 1.4 %fusion.142 = (f32[1,4096]{1,0:T(1,128)S(1)}, f32[1,4096]{1,0:T(1,128)S(1)}, f32[1,4096]{1,0:T(1,128)S(1)}, f32[1,4096]{1,0:T(1,128)S(1)}, f32[1,4096]{1,0:T(1,128)S(1)}, /*index=5*/f32[1,4096]{1,0:T(1,128)S(1)}) fusion(f32[6,4096]{1,0:T(8,128)} %get-tuple-element.610), kind=kLoop, calls=%fused_computation.313.clone.1 | loop fusion | bytes 196608 | tf_op jit(solution)/shard_map/while/body/eval_jaxpr/slice | solution.py:50
  52.0 1.0 %fusion.144 = (f32[32]{0:T(128)S(1)}, f32[32]{0:T(128)S(1)}, f32[32]{0:T(128)S(1)}, f32[32]{0:T(128)S(1)}, f32[32]{0:T(128)S(1)}, /*index=5*/f32[32]{0:T(128)S(1)}) fusion(f32[32]{0:T(128)S(1)} %get-tuple-element.480, f32[4096]{0:T(1024)S(1)} %bitcast.310, f32[32]{0:T(128)S(1)} %get-tuple-element.482, f32[4096]{0:T(1024)S(1)} %bitcast.312, ...), kind=kLoop, calls=%fused_computation.25.clone.1 | loop fusion | flops 5242688 | bytes 116224 | tf_op jit(solution)/shard_map/while/body/eval_jaxpr/reduce_sum | solution.py:71
  53.2 1.4 %fusion.142 = (f32[1,4096]{1,0:T(1,128)S(1)}, f32[1,4096]{1,0:T(1,128)S(1)}, f32[1,4096]{1,0:T(1,128)S(1)}, f32[1,4096]{1,0:T(1,128)S(1)}, f32[1,4096]{1,0:T(1,128)S(1)}, /*index=5*/f32[1,4096]{1,0:T(1,128)S(1)}) fusion(f32[6,4096]{1,0:T(8,128)} %get-tuple-element.610), kind=kLoop, calls=%fused_computation.313.clone.1 | loop fusion | bytes 196608 | tf_op jit(solution)/shard_map/while/body/eval_jaxpr/slice | solution.py:50
  54.6 1.0 %fusion.144 = (f32[32]{0:T(128)S(1)}, f32[32]{0:T(128)S(1)}, f32[32]{0:T(128)S(1)}, f32[32]{0:T(128)S(1)}, f32[32]{0:T(128)S(1)}, /*index=5*/f32[32]{0:T(128)S(1)}) fusion(f32[32]{0:T(128)S(1)} %get-tuple-element.480, f32[4096]{0:T(1024)S(1)} %bitcast.310, f32[32]{0:T(128)S(1)} %get-tuple-element.482, f32[4096]{0:T(1024)S(1)} %bitcast.312, ...), kind=kLoop, calls=%fused_computation.25.clone.1 | loop fusion | flops 5242688 | bytes 116224 | tf_op jit(solution)/shard_map/while/body/eval_jaxpr/reduce_sum | solution.py:71
  55.8 1.4 %fusion.142 = (f32[1,4096]{1,0:T(1,128)S(1)}, f32[1,4096]{1,0:T(1,128)S(1)}, f32[1,4096]{1,0:T(1,128)S(1)}, f32[1,4096]{1,0:T(1,128)S(1)}, f32[1,4096]{1,0:T(1,128)S(1)}, /*index=5*/f32[1,4096]{1,0:T(1,128)S(1)}) fusion(f32[6,4096]{1,0:T(8,128)} %get-tuple-element.610), kind=kLoop, calls=%fused_computation.313.clone.1 | loop fusion | bytes 196608 | tf_op jit(solution)/shard_map/while/body/eval_jaxpr/slice | solution.py:50
  57.2 1.0 %fusion.144 = (f32[32]{0:T(128)S(1)}, f32[32]{0:T(128)S(1)}, f32[32]{0:T(128)S(1)}, f32[32]{0:T(128)S(1)}, f32[32]{0:T(128)S(1)}, /*index=5*/f32[32]{0:T(128)S(1)}) fusion(f32[32]{0:T(128)S(1)} %get-tuple-element.480, f32[4096]{0:T(1024)S(1)} %bitcast.310, f32[32]{0:T(128)S(1)} %get-tuple-element.482, f32[4096]{0:T(1024)S(1)} %bitcast.312, ...), kind=kLoop, calls=%fused_computation.25.clone.1 | loop fusion | flops 5242688 | bytes 116224 | tf_op jit(solution)/shard_map/while/body/eval_jaxpr/reduce_sum | solution.py:71
  58.4 1.4 %fusion.142 = (f32[1,4096]{1,0:T(1,128)S(1)}, f32[1,4096]{1,0:T(1,128)S(1)}, f32[1,4096]{1,0:T(1,128)S(1)}, f32[1,4096]{1,0:T(1,128)S(1)}, f32[1,4096]{1,0:T(1,128)S(1)}, /*index=5*/f32[1,4096]{1,0:T(1,128)S(1)}) fusion(f32[6,4096]{1,0:T(8,128)} %get-tuple-element.610), kind=kLoop, calls=%fused_computation.313.clone.1 | loop fusion | bytes 196608 | tf_op jit(solution)/shard_map/while/body/eval_jaxpr/slice | solution.py:50
  59.8 1.0 %fusion.144 = (f32[32]{0:T(128)S(1)}, f32[32]{0:T(128)S(1)}, f32[32]{0:T(128)S(1)}, f32[32]{0:T(128)S(1)}, f32[32]{0:T(128)S(1)}, /*index=5*/f32[32]{0:T(128)S(1)}) fusion(f32[32]{0:T(128)S(1)} %get-tuple-element.480, f32[4096]{0:T(1024)S(1)} %bitcast.310, f32[32]{0:T(128)S(1)} %get-tuple-element.482, f32[4096]{0:T(1024)S(1)} %bitcast.312, ...), kind=kLoop, calls=%fused_computation.25.clone.1 | loop fusion | flops 5242688 | bytes 116224 | tf_op jit(solution)/shard_map/while/body/eval_jaxpr/reduce_sum | solution.py:71
  61.0 1.4 %fusion.142 = (f32[1,4096]{1,0:T(1,128)S(1)}, f32[1,4096]{1,0:T(1,128)S(1)}, f32[1,4096]{1,0:T(1,128)S(1)}, f32[1,4096]{1,0:T(1,128)S(1)}, f32[1,4096]{1,0:T(1,128)S(1)}, /*index=5*/f32[1,4096]{1,0:T(1,128)S(1)}) fusion(f32[6,4096]{1,0:T(8,128)} %get-tuple-element.610), kind=kLoop, calls=%fused_computation.313.clone.1 | loop fusion | bytes 196608 | tf_op jit(solution)/shard_map/while/body/eval_jaxpr/slice | solution.py:50
  62.4 1.0 %fusion.144 = (f32[32]{0:T(128)S(1)}, f32[32]{0:T(128)S(1)}, f32[32]{0:T(128)S(1)}, f32[32]{0:T(128)S(1)}, f32[32]{0:T(128)S(1)}, /*index=5*/f32[32]{0:T(128)S(1)}) fusion(f32[32]{0:T(128)S(1)} %get-tuple-element.480, f32[4096]{0:T(1024)S(1)} %bitcast.310, f32[32]{0:T(128)S(1)} %get-tuple-element.482, f32[4096]{0:T(1024)S(1)} %bitcast.312, ...), kind=kLoop, calls=%fused_computation.25.clone.1 | loop fusion | flops 5242688 | bytes 116224 | tf_op jit(solution)/shard_map/while/body/eval_jaxpr/reduce_sum | solution.py:71
  63.5 1.1 %fusion.81 = (f32[32]{0:T(128)S(1)}, f32[32]{0:T(128)S(1)}, f32[32]{0:T(128)S(1)}, f32[32]{0:T(128)S(1)}, f32[32]{0:T(128)S(1)}, /*index=5*/f32[32]{0:T(128)S(1)}) fusion(f32[4096]{0:T(1024)S(1)} %bitcast.352, f32[4096]{0:T(1024)S(1)} %bitcast.354, f32[32]{0:T(128)S(1)} %get-tuple-element.231, f32[32]{0:T(128)S(1)} %get-tuple-element.233, ...), kind=kLoop, calls=%fused_computation.207 | loop fusion | flops 5242688 | bytes 116224 | tf_op jit(solution)/shard_map/reduce_sum | solution.py:71
  64.8 2.4 %while.32 = (s32[]{:T(128)}, f32[2,6,32]{2,1,0:T(8,128)S(1)}, f32[1,4096]{1,0:T(1,128)S(1)}, f32[6,4096]{1,0:T(8,128)S(1)}, f32[2,6,32]{2,0,1:T(2,128)S(1)}, /*i...) while((s32[]{:T(128)}, f32[2,6,32]{2,1,0:T(8,128)S(1)}, f32[1,4096]{1,0:T(1,128)S(1)}, ...), condition=%wide.region_30.31_spmd, body=%wide.region_23.30_spmd.sunk | while | flops 5242695 | bytes 324309 | solution.py:149
  64.9 1.0 %fusion.150 = (f32[32]{0:T(128)S(1)}, f32[32]{0:T(128)S(1)}, f32[32]{0:T(128)S(1)}, f32[32]{0:T(128)S(1)}, f32[32]{0:T(128)S(1)}, /*index=5*/f32[32]{0:T(128)S(1)}) fusion(f32[32]{0:T(128)S(1)} %get-tuple-element.526, f32[4096]{0:T(1024)S(1)} %bitcast.316, f32[32]{0:T(128)S(1)} %get-tuple-element.528, f32[4096]{0:T(1024)S(1)} %bitcast.318, ...), kind=kLoop, calls=%fused_computation.120.clone.1 | loop fusion | flops 5242688 | bytes 116224 | tf_op jit(solution)/shard_map/while/body/eval_jaxpr/reduce_sum | solution.py:71
  66.2 1.0 %fusion.150 = (f32[32]{0:T(128)S(1)}, f32[32]{0:T(128)S(1)}, f32[32]{0:T(128)S(1)}, f32[32]{0:T(128)S(1)}, f32[32]{0:T(128)S(1)}, /*index=5*/f32[32]{0:T(128)S(1)}) fusion(f32[32]{0:T(128)S(1)} %get-tuple-element.526, f32[4096]{0:T(1024)S(1)} %bitcast.316, f32[32]{0:T(128)S(1)} %get-tuple-element.528, f32[4096]{0:T(1024)S(1)} %bitcast.318, ...), kind=kLoop, calls=%fused_computation.120.clone.1 | loop fusion | flops 5242688 | bytes 116224 | tf_op jit(solution)/shard_map/while/body/eval_jaxpr/reduce_sum | solution.py:71
  67.2 4.8 %while.31 = (s32[]{:T(128)}, f32[4,6,32]{2,1,0:T(8,128)S(1)}, f32[1,4096]{1,0:T(1,128)S(1)}, f32[6,4096]{1,0:T(8,128)S(1)}, f32[4,6,32]{2,0,1:T(4,128)S(1)}, /*i...) while((s32[]{:T(128)}, f32[4,6,32]{2,1,0:T(8,128)S(1)}, f32[1,4096]{1,0:T(1,128)S(1)}, ...), condition=%wide.region_22.23_spmd, body=%wide.region_15.22_spmd.sunk | while | flops 5242695 | bytes 324309 | solution.py:149
  67.4 1.0 %fusion.147 = (f32[32]{0:T(128)S(1)}, f32[32]{0:T(128)S(1)}, f32[32]{0:T(128)S(1)}, f32[32]{0:T(128)S(1)}, f32[32]{0:T(128)S(1)}, /*index=5*/f32[32]{0:T(128)S(1)}) fusion(f32[32]{0:T(128)S(1)} %get-tuple-element.503, f32[4096]{0:T(1024)S(1)} %bitcast.322, f32[32]{0:T(128)S(1)} %get-tuple-element.505, f32[4096]{0:T(1024)S(1)} %bitcast.324, ...), kind=kLoop, calls=%fused_computation.74.clone.1 | loop fusion | flops 5242688 | bytes 116224 | tf_op jit(solution)/shard_map/while/body/eval_jaxpr/reduce_sum | solution.py:71
  68.6 1.0 %fusion.147 = (f32[32]{0:T(128)S(1)}, f32[32]{0:T(128)S(1)}, f32[32]{0:T(128)S(1)}, f32[32]{0:T(128)S(1)}, f32[32]{0:T(128)S(1)}, /*index=5*/f32[32]{0:T(128)S(1)}) fusion(f32[32]{0:T(128)S(1)} %get-tuple-element.503, f32[4096]{0:T(1024)S(1)} %bitcast.322, f32[32]{0:T(128)S(1)} %get-tuple-element.505, f32[4096]{0:T(1024)S(1)} %bitcast.324, ...), kind=kLoop, calls=%fused_computation.74.clone.1 | loop fusion | flops 5242688 | bytes 116224 | tf_op jit(solution)/shard_map/while/body/eval_jaxpr/reduce_sum | solution.py:71
  69.8 1.0 %fusion.147 = (f32[32]{0:T(128)S(1)}, f32[32]{0:T(128)S(1)}, f32[32]{0:T(128)S(1)}, f32[32]{0:T(128)S(1)}, f32[32]{0:T(128)S(1)}, /*index=5*/f32[32]{0:T(128)S(1)}) fusion(f32[32]{0:T(128)S(1)} %get-tuple-element.503, f32[4096]{0:T(1024)S(1)} %bitcast.322, f32[32]{0:T(128)S(1)} %get-tuple-element.505, f32[4096]{0:T(1024)S(1)} %bitcast.324, ...), kind=kLoop, calls=%fused_computation.74.clone.1 | loop fusion | flops 5242688 | bytes 116224 | tf_op jit(solution)/shard_map/while/body/eval_jaxpr/reduce_sum | solution.py:71
  71.0 1.0 %fusion.147 = (f32[32]{0:T(128)S(1)}, f32[32]{0:T(128)S(1)}, f32[32]{0:T(128)S(1)}, f32[32]{0:T(128)S(1)}, f32[32]{0:T(128)S(1)}, /*index=5*/f32[32]{0:T(128)S(1)}) fusion(f32[32]{0:T(128)S(1)} %get-tuple-element.503, f32[4096]{0:T(1024)S(1)} %bitcast.322, f32[32]{0:T(128)S(1)} %get-tuple-element.505, f32[4096]{0:T(1024)S(1)} %bitcast.324, ...), kind=kLoop, calls=%fused_computation.74.clone.1 | loop fusion | flops 5242688 | bytes 116224 | tf_op jit(solution)/shard_map/while/body/eval_jaxpr/reduce_sum | solution.py:71
  72.2 3.4 %collective-permute-start.8 = (f32[6,128]{1,0:T(8,128)S(1)}, f32[6,128]{1,0:T(8,128)S(1)}, u32[]{:S(2)}, u32[]{:S(2)}) collective-permute-start(f32[6,128]{1,0:T(8,128)S(1)} %dynamic-slice_add_fusion.2), channel_id=1, source_target_pairs={{0,128},{32,160},{64,192},{96,224},{128,0},{160,32},{192,64},{224,... | collective-permute-start | bytes 9224 | tf_op jit(solution)/shard_map/ppermute | solution.py:15
  75.6 1.5 %multiply_reduce_fusion = (f32[32]{0:T(128)S(1)}, f32[32]{0:T(128)S(1)}, f32[32]{0:T(128)S(1)}, f32[32]{0:T(128)S(1)}, f32[32]{0:T(128)S(1)}, /*index=5*/f32[32]...) fusion(f32[32]{0:T(128)S(1)} %get-tuple-element.231, ...), kind=kLoop, calls=%fused_computation.243 | loop fusion | flops 6946432 | bytes 133376 | tf_op jit(solution)/shard_map/reduce_sum | solution.py:79
  77.2 0.4 collective-permute-done.8
  77.6 1.6 %collective-permute-start.9 = (f32[6,64]{1,0:T(8,128)S(1)}, f32[6,64]{1,0:T(8,128)S(1)}, u32[]{:S(2)}, u32[]{:S(2)}) collective-permute-start(f32[6,64]{1,0:T(8,128)S(1)} %dynamic-slice_add_fusion.1), channel_id=1, source_target_pairs={{0,64},{32,96},{64,0},{96,32},{128,192},{160,224},{192,128},{224,1... | collective-permute-start | bytes 4616 | tf_op jit(solution)/shard_map/ppermute | solution.py:15
  79.2 1.0 %fusion.75 = (f32[32]{0:T(128)S(1)}, f32[32]{0:T(128)S(1)}, f32[32]{0:T(128)S(1)}, f32[32]{0:T(128)S(1)}, f32[32]{0:T(128)S(1)}, /*index=5*/f32[32]{0:T(128)S(1)}) fusion(f32[32]{0:T(128)S(1)} %get-tuple-element.331, f32[32]{0:T(128)S(1)} %get-tuple-element.333, f32[4096]{0:T(1024)S(1)} %bitcast.334, f32[4096]{0:T(1024)S(1)} %bitcast.340, ...), kind=kLoop, calls=%fused_computation.201 | loop fusion | flops 5242688 | bytes 116224 | tf_op jit(solution)/shard_map/reduce_sum | solution.py:71
  80.3 1.0 %collective-permute-done.9 = f32[6,64]{1,0:T(8,128)S(1)} collective-permute-done((f32[6,64]{1,0:T(8,128)S(1)}, f32[6,64]{1,0:T(8,128)S(1)}, u32[]{:S(2)}, u32[]{:S(2)}) %collective-permute-start.9) | collective-permute-done | bytes 1568 | tf_op jit(solution)/shard_map/ppermute | solution.py:15
  81.3 2.0 %collective-permute-start.10 = (f32[6,32]{1,0:T(8,128)S(1)}, f32[6,32]{1,0:T(8,128)S(1)}, u32[]{:S(2)}, u32[]{:S(2)}) collective-permute-start(f32[6,32]{1,0:T(8,128)S(1)} %dynamic-slice_add_fusion), channel_id=1, source_target_pairs={{0,32},{32,0},{64,96},{96,64},{128,160},{160,128},{192,224},{224,1... | collective-permute-start | bytes 2312 | tf_op jit(solution)/shard_map/ppermute | solution.py:15
  83.4 3.0 %collective-permute-done.10 = f32[6,32]{1,0:T(8,128)S(1)} collective-permute-done((f32[6,32]{1,0:T(8,128)S(1)}, f32[6,32]{1,0:T(8,128)S(1)}, u32[]{:S(2)}, u32[]{:S(2)}) %collective-permute-start.10) | collective-permute-done | bytes 800 | tf_op jit(solution)/shard_map/ppermute | solution.py:15
  86.6 0.6 copy-done.4
  87.1 0.6 pad_maximum_fusion.2
  (137 shorter events, 4.7 us)
Async XLA Ops:
  0.6 0.8 copy-start
  2.1 0.7 copy-start.5
  2.8 0.7 copy-start.6
  2.8 19.3 %collective-permute-start = (f32[7,256]{1,0:T(8,128)S(1)}, f32[7,256]{1,0:T(8,128)S(1)}, u32[]{:S(2)}, u32[]{:S(2)}) collective-permute-start(f32[7,256]{1,0:T(8,128)S(1)} %pad_maximum_fusion), channel_id=1, source_target_pairs={{0,1},{1,0},{2,3},{3,2},{4,5},{5,4},{6,7},{7,6},{8,9},{9,8},{10,11... | collective-permute-start | bytes 21512 | tf_op jit(solution)/shard_map/ppermute | solution.py:15
  5.0 8.0 %collective-permute-start.5 = (f32[6,32]{0,1:T(8,128)S(1)}, f32[6,32]{0,1:T(8,128)S(1)}, u32[]{:S(2)}, u32[]{:S(2)}) collective-permute-start(f32[6,32]{0,1:T(8,128)S(1)} %bitcast_select_fusion.1), channel_id=1, source_target_pairs={{0,32},{32,0},{64,96},{96,64},{128,160},{160,128},{192,224},{224,1... | collective-permute-start | bytes 2312 | tf_op jit(solution)/shard_map/ppermute | solution.py:15
  8.4 0.7 copy-start.1
  9.1 0.7 copy-start.2
  10.6 0.7 copy-start.7
  13.2 3.6 %collective-permute-start.6 = (f32[6,64]{1,0:T(8,128)S(1)}, f32[6,64]{1,0:T(8,128)S(1)}, u32[]{:S(2)}, u32[]{:S(2)}) collective-permute-start(f32[6,64]{1,0:T(8,128)S(1)} %maximum_select_fusion.8), channel_id=1, source_target_pairs={{0,64},{32,96},{64,0},{96,32},{128,192},{160,224},{192,128},{224,1... | collective-permute-start | bytes 4616 | tf_op jit(solution)/shard_map/ppermute | solution.py:15
  16.9 5.1 %collective-permute-start.7 = (f32[6,128]{1,0:T(8,128)S(1)}, f32[6,128]{1,0:T(8,128)S(1)}, u32[]{:S(2)}, u32[]{:S(2)}) collective-permute-start(f32[6,128]{1,0:T(8,128)S(1)} %maximum_select_fusion.9), channel_id=1, source_target_pairs={{0,128},{32,160},{64,192},{96,224},{128,0},{160,32},{192,64},{224,... | collective-permute-start | bytes 9224 | tf_op jit(solution)/shard_map/ppermute | solution.py:15
  22.2 3.8 %collective-permute-start.1 = (f32[7,512]{1,0:T(8,128)S(1)}, f32[7,512]{1,0:T(8,128)S(1)}, u32[]{:S(2)}, u32[]{:S(2)}) collective-permute-start(f32[7,512]{1,0:T(8,128)S(1)} %maximum_select_fusion.4), channel_id=1, source_target_pairs={{0,2},{1,3},{2,0},{3,1},{4,6},{5,7},{6,4},{7,5},{8,10},{9,11},{10,... | collective-permute-start | bytes 43016 | tf_op jit(solution)/shard_map/ppermute | solution.py:15
  26.0 5.5 %collective-permute-start.2 = (f32[7,1024]{1,0:T(8,128)S(1)}, f32[7,1024]{1,0:T(8,128)S(1)}, u32[]{:S(2)}, u32[]{:S(2)}) collective-permute-start(f32[7,1024]{1,0:T(8,128)S(1)} %maximum_select_fusion.2), channel_id=1, source_target_pairs={{0,4},{1,5},{2,6},{3,7},{4,0},{5,1},{6,2},{7,3},{8,12},{9,13},{10,... | collective-permute-start | bytes 86024 | tf_op jit(solution)/shard_map/ppermute | solution.py:15
  31.5 8.3 %collective-permute-start.3 = (f32[7,2048]{1,0:T(8,128)S(1)}, f32[7,2048]{1,0:T(8,128)S(1)}, u32[]{:S(2)}, u32[]{:S(2)}) collective-permute-start(f32[7,2048]{1,0:T(8,128)S(1)} %maximum_select_fusion.1), channel_id=1, source_target_pairs={{0,8},{1,9},{2,10},{3,11},{4,12},{5,13},{6,14},{7,15},{8,0},{9,1},... | collective-permute-start | bytes 172040 | tf_op jit(solution)/shard_map/ppermute | solution.py:15
  40.4 24.2 %collective-permute-start.4 = (f32[7,4096]{1,0:T(8,128)}, f32[7,4096]{1,0:T(8,128)S(1)}, u32[]{:S(2)}, u32[]{:S(2)}) collective-permute-start(f32[7,4096]{1,0:T(8,128)} %maximum_select_fusion), channel_id=1, source_target_pairs={{0,16},{1,17},{2,18},{3,19},{4,20},{5,21},{6,22},{7,23},{8,24},{9,... | collective-permute-start | bytes 344072 | tf_op jit(solution)/shard_map/ppermute | solution.py:15
  72.2 5.3 %collective-permute-start.8 = (f32[6,128]{1,0:T(8,128)S(1)}, f32[6,128]{1,0:T(8,128)S(1)}, u32[]{:S(2)}, u32[]{:S(2)}) collective-permute-start(f32[6,128]{1,0:T(8,128)S(1)} %dynamic-slice_add_fusion.2), channel_id=1, source_target_pairs={{0,128},{32,160},{64,192},{96,224},{128,0},{160,32},{192,64},{224,... | collective-permute-start | bytes 9224 | tf_op jit(solution)/shard_map/ppermute | solution.py:15
  77.6 3.6 %collective-permute-start.9 = (f32[6,64]{1,0:T(8,128)S(1)}, f32[6,64]{1,0:T(8,128)S(1)}, u32[]{:S(2)}, u32[]{:S(2)}) collective-permute-start(f32[6,64]{1,0:T(8,128)S(1)} %dynamic-slice_add_fusion.1), channel_id=1, source_target_pairs={{0,64},{32,96},{64,0},{96,32},{128,192},{160,224},{192,128},{224,1... | collective-permute-start | bytes 4616 | tf_op jit(solution)/shard_map/ppermute | solution.py:15
  81.3 5.1 %collective-permute-start.10 = (f32[6,32]{1,0:T(8,128)S(1)}, f32[6,32]{1,0:T(8,128)S(1)}, u32[]{:S(2)}, u32[]{:S(2)}) collective-permute-start(f32[6,32]{1,0:T(8,128)S(1)} %dynamic-slice_add_fusion), channel_id=1, source_target_pairs={{0,32},{32,0},{64,96},{96,64},{128,160},{160,128},{192,224},{224,1... | collective-permute-start | bytes 2312 | tf_op jit(solution)/shard_map/ppermute | solution.py:15
  83.4 3.2 %copy-start.3 = (f32[6,32]{1,0:T(8,128)}, f32[6,32]{1,0:T(8,128)S(1)}, u32[]{:S(2)}) copy-start(f32[6,32]{1,0:T(8,128)S(1)} %add.346) | copy-start | bytes 2308
  86.6 0.6 copy-start.4

commit v6 on v2

v6 whole, which is shorter than its diff:
```python
import jax
import jax.numpy as jnp
from jax import lax
from jax.experimental import pallas as pl
from jax.experimental.pallas import tpu as pltpu
from jax.sharding import PartitionSpec as P
import functools


BLOCK = 128


soften_sq = 0.0001


def exchange(block, axis, bit):
    size = lax.axis_size(axis)
    return lax.ppermute(block, axis, [(i, i ^ bit) for i in range(size)])


def gather_doubling(block, axis):
    me = lax.axis_index(axis)
    bit = 1
    while bit < lax.axis_size(axis):
        got = exchange(block, axis, bit)
        upper = (me // bit) % 2 == 1
        block = jnp.where(
            upper, jnp.concatenate([got, block], 1), jnp.concatenate([block, got], 1)
        )
        bit *= 2
    return block


def gather_all_to_all(block, axis):
    size = lax.axis_size(axis)
    spread = jnp.broadcast_to(block[:, None, :], (block.shape[0], size, block.shape[1]))
    got = lax.all_to_all(spread, axis, 1, 1, tiled=True)
    return got.reshape(block.shape[0], size * block.shape[1])


LANES = 128
SUB = 8


def pair_kernel(tgt_ref, src_ref, out_ref, *, weights):
    rows = tgt_ref.shape[1]
    chunks = src_ref.shape[1] // LANES
    outs = 6 * weights

    def block_body(b, carry):
        r0 = pl.multiple_of(b * SUB, SUB)
        t = [tgt_ref[k, pl.ds(r0, SUB), :] for k in range(6)]

        def chunk_body(c, accs):
            c0 = pl.multiple_of(c * LANES, LANES)
            s = [
                jnp.broadcast_to(src_ref[pl.ds(k, 1), pl.ds(c0, LANES)], (SUB, LANES))
                for k in range(6 + weights)
            ]
            gap_x = s[0] - t[0]
            gap_y = s[1] - t[1]
            gap_z = s[2] - t[2]
            rel_x = s[3] - t[3]
            rel_y = s[4] - t[4]
            rel_z = s[5] - t[5]
            dist_sq = gap_x * gap_x + gap_y * gap_y + gap_z * gap_z + soften_sq
            inverse = lax.rsqrt(dist_sq)
            inv_cube = inverse * inverse * inverse
            radial = 3.0 * (gap_x * rel_x + gap_y * rel_y + gap_z * rel_z) / dist_sq
            terms = (
                gap_x,
                gap_y,
                gap_z,
                rel_x - radial * gap_x,
                rel_y - radial * gap_y,
                rel_z - radial * gap_z,
            )
            new = []
            for w in range(weights):
                scaled = s[6 + w] * inv_cube
                for i, term in enumerate(terms):
                    new.append(accs[6 * w + i] + scaled * term)
            return tuple(new)

        zeros = tuple(jnp.zeros((SUB, LANES), jnp.float32) for _ in range(outs))
        accs = lax.fori_loop(0, chunks, chunk_body, zeros, unroll=8)
        for i in range(outs):
            out_ref[pl.ds(r0, SUB), pl.ds(i, 1)] = jnp.sum(accs[i], axis=1, keepdims=True)
        return carry

    lax.fori_loop(0, rows // SUB, block_body, 0)


def kernel_sums(targets, src):
    rows = targets.shape[1]
    weights = src.shape[0] - 6
    sources = src[:6]
    tgt = jnp.broadcast_to(targets[:, :, None], (6, rows, LANES))
    pairs = rows * sources.shape[1]
    out = pl.pallas_call(
        functools.partial(pair_kernel, weights=weights),
        out_shape=jax.ShapeDtypeStruct((rows, LANES), jnp.float32),
        in_specs=[pl.BlockSpec(memory_space=pltpu.VMEM)] * 2,
        out_specs=pl.BlockSpec(memory_space=pltpu.VMEM),
        cost_estimate=pl.CostEstimate(
            flops=pairs * (30 + 12 * weights),
            transcendentals=pairs,
            bytes_accessed=4 * (tgt.size + src.size + rows * LANES),
        ),
    )(tgt, src)
    sums = out[:, : 6 * weights].T
    return [sums[6 * w : 6 * w + 6] for w in range(weights)]


def per_device(
    position,
    velocity,
    accel_old,
    jerk_old,
    elapsed,
    masses,
    active_stars,
    neighbour_list,
    neighbour_count,
):
    moved_pos = position + elapsed * (
        velocity + elapsed * (0.5 * accel_old + elapsed * jerk_old / 6.0)
    )
    turned = velocity + elapsed * (accel_old + 0.5 * elapsed * jerk_old)
    sources = jnp.concatenate([moved_pos, turned], axis=0)
    own_set = jnp.take(sources, active_stars, axis=1)
    act_dev = active_stars.shape[0]
    block_data = jnp.concatenate([sources, masses[None, :]], axis=0)
    targets = gather_doubling(own_set, "blk")
    group = gather_all_to_all(block_data, "grp")
    group_src = group[:6]
    group_mass = group[6]
    blk_size = lax.axis_size("blk")
    blk_here = lax.axis_index("blk")
    block_total = group_src.shape[1] // BLOCK
    slot_total = neighbour_list.shape[1]
    own_live = jnp.arange(slot_total) < neighbour_count[0]
    near = jnp.any(
        own_live[:, None]
        & (neighbour_list[0][:, None] == jnp.arange(block_total)[None, :]),
        axis=0,
    ).astype(jnp.float32)
    weight = group_mass[None, :]

    def owner_sums(start, count):
        pieces = lax.dynamic_slice_in_dim(targets, start * act_dev, count * act_dev, 1)
        return kernel_sums(pieces, group)[0]

    def owner_cols(block, owner, span):
        return lax.dynamic_slice_in_dim(block, (owner % span) * act_dev, act_dev, 1)

    bit4, bit2 = blk_size // 2, blk_size // 4
    base4 = blk_here - blk_here % bit4
    start4 = blk_here - blk_here % (2 * bit4) + ((blk_here // bit4 + 1) % 2) * bit4
    sent4 = owner_sums(start4, bit4)
    got4 = exchange(sent4, "blk", bit4)
    start2 = base4 + ((blk_here // bit2 + 1) % 2) * bit2
    sent2 = owner_sums(start2, bit2) + lax.dynamic_slice_in_dim(
        got4, (start2 - base4) * act_dev, bit2 * act_dev, 1
    )
    got2 = exchange(sent2, "blk", bit2)
    partner = blk_here ^ 1
    sent1 = (
        owner_sums(partner, 1)
        + owner_cols(got4, partner, bit4)
        + owner_cols(got2, partner, bit2)
    )
    got1 = exchange(sent1, "blk", 1)
    near_rep = jnp.repeat(near, BLOCK)[None, :]
    split_src = jnp.concatenate(
        [group_src, weight * (1.0 - near_rep), weight * near_rep], axis=0
    )
    own_far, irregular = kernel_sums(own_set, split_src)
    regular = (
        own_far
        + owner_cols(got4, blk_here, bit4)
        + owner_cols(got2, blk_here, bit2)
        + got1
    )
    accel_now = regular[:3] + irregular[:3]
    jerk_now = regular[3:] + irregular[3:]
    step_time = jnp.take(elapsed, active_stars)
    start_accel = jnp.take(accel_old, active_stars, axis=1)
    start_jerk = jnp.take(jerk_old, active_stars, axis=1)
    change = start_accel - accel_now
    snap_term = -6.0 * change - step_time * (4.0 * start_jerk + 2.0 * jerk_now)
    crackle_term = 12.0 * change + 6.0 * step_time * (start_jerk + jerk_now)
    return (regular, irregular, jnp.concatenate([snap_term, crackle_term], axis=0))


def solution(mesh):
    in_specs = (
        P(None, ("blk", "grp")),
        P(None, ("blk", "grp")),
        P(None, ("blk", "grp")),
        P(None, ("blk", "grp")),
        P(("blk", "grp")),
        P(("blk", "grp")),
        P(("blk", "grp")),
        P(("blk", "grp"), None),
        P(("blk", "grp")),
    )
    out_specs = (P(None, ("blk", "grp")), P(None, ("blk", "grp")), P(None, ("blk", "grp")))

    return jax.shard_map(
        per_device, mesh=mesh, in_specs=in_specs, out_specs=out_specs, check_vma=False
    )
```

time: 65.8 us -> 71.9 us (1.093)
  Pallas kernels: 0 us -> 22.7 us
  other arithmetic: 21.6 us -> 4.27 us
  local copies, waits for them, and re-layouts: 10.3 us -> 13.6 us
  waiting for transfers between devices: 7.43 us -> 5.56 us
  starting transfers between devices: 23.9 us -> 23.1 us
    pallas_call x0 -> x4, Pallas kernels: none -> 22.7 us  [kernel_sums(): pl.pallas_call(functools.partial(pair_kernel, weights=weights), out_shape...]
    reduce_sum x9 -> x0, other arithmetic: 17.9 us -> none  [pair_sums(): return jnp.stack([jnp.sum(scaled * term, axis=1) for term in term_list])]
    broadcast_in_dim x0 -> x5, local copies, waits for them, and re-layouts: none -> 3.23 us  [the longest x4 3.16 us: kernel_sums(): tgt = jnp.broadcast_to(targets[:, :, None], (6, rows, LANES))]
    ppermute x6, waiting for transfers between devices: 7.42 us -> 5.56 us  [exchange(): return lax.ppermute(block, axis, [(i, i ^ bit) for i in range(size)])]
    unnamed x16 -> x24, local copies, waits for them, and re-layouts: 3.64 us -> 4.68 us
    transpose x1 -> x2, local copies, waits for them, and re-layouts: 0.01 us -> 0.89 us  [kernel_sums(): sums = out[:, :6 * weights].T]
    ppermute x6, starting transfers between devices: 14.3 us -> 13.4 us  [exchange(): return lax.ppermute(block, axis, [(i, i ^ bit) for i in range(size)])]
    another operation x9 -> x0, local copies, waits for them, and re-layouts: 0.82 us -> none  [pair_sums(): return jnp.stack([jnp.sum(scaled * term, axis=1) for term in term_list])]
  transfers between devices with their start and end apart: 7 -> 7, of which waited for: 4 -> 3; matrix products, arithmetic and copies ran while one was open for 11% -> 11% of each run, Pallas kernels for 0% -> 19%
where the time goes in v6:
time: 71.9 us; the launch traced here: 70.8 us
  starting transfers between devices  23.1 us (32%)
  Pallas kernels  22.7 us (32%)
  local copies, waits for them, and re-layouts  13.6 us (19%)
  waiting for transfers between devices  5.56 us (8%)
  other arithmetic  4.27 us (6%)
  between operations  1.55 us (2%)
    pallas_call x4, Pallas kernels, kernel_sums(): pl.pallas_call(functools.partial(pair_kernel, weights=weights), out_shape...  22.7 us
    ppermute x6, starting transfers between devices, exchange(): return lax.ppermute(block, axis, [(i, i ^ bit) for i in range(size)])  13.4 us
    all_to_all x1, starting transfers between devices, gather_all_to_all(): got = lax.all_to_all(spread, axis, 1, 1, tiled=True)  9.66 us
    ppermute x6, waiting for transfers between devices, exchange(): return lax.ppermute(block, axis, [(i, i ^ bit) for i in range(size)])  5.56 us
    unnamed x24, local copies, waits for them, and re-layouts  4.68 us
    broadcast_in_dim x4, local copies, waits for them, and re-layouts, kernel_sums(): tgt = jnp.broadcast_to(targets[:, :, None], (6, rows, LANES))  3.16 us
  transfers between devices with their start and end apart: 7, of which 3 were waited for; matrix products, arithmetic and copies ran while one was open for 11% of the time, Pallas kernels for 19%

profile of v6, /device:TPU:32, one launch (start us, length us, event | category | flops | bytes accessed | tf_op | source)
XLA Modules:
  0.0 70.8 jit_solution(5511907043510379264)
XLA Ops:
  0.6 0.7 %broadcast_multiply_fusion = f32[256]{0:T(256)S(1)} fusion(f32[256]{0:T(256)} %param.15), kind=kLoop, calls=%fused_computation.45 | loop fusion | flops 256 | bytes 2048 | tf_op jit(solution)/shard_map/mul | solution.py:129
  1.4 0.0 copy-done
  1.4 0.7 %multiply_add_fusion.1 = (f32[3,256]{1,0:T(4,128)S(1)}, f32[3,256]{1,0:T(4,128)S(1)}) fusion(f32[3,256]{1,0:T(4,128)} %param.11, f32[3,256]{1,0:T(4,128)} %param.12, f32[3,256]{1,0:T(4,128)} %param.14, f32[3,256]{1,0:T(4,128)} %param.13, f32[256]{0:T(256)S(1)} %copy-done, f32[256]{0:T(256)S(1)} %broadcast_multiply_fusion), kind=kLoop, calls=%fused_computation.38 | loop fusion | flops 9216 | bytes 20480 | tf_op jit(solution)/shard_map/add | solution.py:126
  2.1 0.0 copy-start.7
  2.1 0.7 copy-done.7
  2.8 0.7 %broadcast_in_dim.46 = f32[7,32,256]{2,0,1:T(8,128)} broadcast(f32[7,256]{1,0:T(8,128)S(1)} %pad_maximum_fusion.2), dimensions={0,2} | broadcast | bytes 236544 | tf_op jit(solution)/shard_map/broadcast_in_dim | solution.py:36
  3.6 9.7 %all-to-all-start = ((f32[7,32,256]{2,0,1:T(8,128)}), f32[7,32,256]{2,0,1:T(8,128)S(1)}, u32[]{:S(2)}, u32[]{:S(2)}) async-start(f32[7,32,256]{2,0,1:T(8,128)} %broadcast_in_dim.46), calls=%async_computation | async-start | bytes 524288 | tf_op jit(solution)/shard_map/all_to_all | solution.py:37
  13.2 0.0 copy-start.8
  13.2 0.1 copy.79
  13.4 0.5 copy-done.8
  13.9 0.7 gather_fusion.1
  14.6 0.6 gather_fusion
  15.2 0.1 select_bitcast_fusion
  15.3 2.8 %collective-permute-start = (f32[6,32]{0,1:T(8,128)S(1)}, f32[6,32]{0,1:T(8,128)S(1)}, u32[]{:S(2)}, u32[]{:S(2)}) collective-permute-start(f32[6,32]{0,1:T(8,128)S(1)} %select_bitcast_fusion), channel_id=1, source_target_pairs={{0,32},{32,0},{64,96},{96,64},{128,160},{160,128},{192,224},{224,1... | collective-permute-start | bytes 2312 | tf_op jit(solution)/shard_map/ppermute | solution.py:18
  18.0 0.1 copy.80
  18.8 0.0 copy-start.9
  18.8 0.6 copy-done.9
  19.4 0.1 fusion.2
  19.6 1.0 %collective-permute-done = f32[6,32]{0,1:T(8,128)S(1)} collective-permute-done((f32[6,32]{0,1:T(8,128)S(1)}, f32[6,32]{0,1:T(8,128)S(1)}, u32[]{:S(2)}, u32[]{:S(2)}) %collective-permute-start) | collective-permute-done | bytes 800 | tf_op jit(solution)/shard_map/ppermute | solution.py:18
  20.6 0.1 copy.81
  20.7 0.1 maximum_select_fusion.1
  20.7 1.6 %collective-permute-start.1 = (f32[6,64]{1,0:T(8,128)S(1)}, f32[6,64]{1,0:T(8,128)S(1)}, u32[]{:S(2)}, u32[]{:S(2)}) collective-permute-start(f32[6,64]{1,0:T(8,128)S(1)} %maximum_select_fusion.1), channel_id=1, source_target_pairs={{0,64},{32,96},{64,0},{96,32},{128,192},{160,224},{192,128},{224,1... | collective-permute-start | bytes 4616 | tf_op jit(solution)/shard_map/ppermute | solution.py:18
  22.4 2.0 %collective-permute-done.1 = f32[6,64]{1,0:T(8,128)S(1)} collective-permute-done((f32[6,64]{1,0:T(8,128)S(1)}, f32[6,64]{1,0:T(8,128)S(1)}, u32[]{:S(2)}, u32[]{:S(2)}) %collective-permute-start.1) | collective-permute-done | bytes 1568 | tf_op jit(solution)/shard_map/ppermute | solution.py:18
  24.4 0.1 maximum_select_fusion.2
  24.5 3.2 %collective-permute-start.2 = (f32[6,128]{1,0:T(8,128)S(1)}, f32[6,128]{1,0:T(8,128)S(1)}, u32[]{:S(2)}, u32[]{:S(2)}) collective-permute-start(f32[6,128]{1,0:T(8,128)S(1)} %maximum_select_fusion.2), channel_id=1, source_target_pairs={{0,128},{32,160},{64,192},{96,224},{128,0},{160,32},{192,64},{224,... | collective-permute-start | bytes 9224 | tf_op jit(solution)/shard_map/ppermute | solution.py:18
  27.7 0.7 copy-done.4
  28.4 0.1 copy.86
  28.5 0.5 copy-done.5
  29.1 0.1 copy.85
  29.2 0.6 gather_fusion.3
  29.8 0.6 gather_fusion.2
  30.4 0.0 collective-permute-done.2
  30.4 0.1 constant_dynamic-slice_fusion
  30.5 0.1 constant_dynamic-slice_fusion.1
  30.6 0.1 constant_dynamic-slice_fusion.2
  30.7 0.0 all-to-all-done
  30.7 0.9 %broadcast_in_dim.79.tgt_ref = f32[6,128,128]{2,1,0:T(8,128)} broadcast(f32[6,128]{1,0:T(8,128)S(1)} %constant_dynamic-slice_fusion.2), dimensions={0,1} | broadcast | bytes 396288 | tf_op jit(solution)/shard_map/broadcast_in_dim | solution.py:98
  31.6 0.0 copy-done.1
  31.6 9.5 %shard_map.113 = f32[128,128]{1,0:T(8,128)} custom-call(f32[6,128,128]{2,1,0:T(8,128)} %broadcast_in_dim.79.tgt_ref, f32[7,8192]{1,0:T(8,128)} %bitcast.44), custom_call_target="tpu_custom_call" | custom-call | flops 44040192 | bytes 688128 | tf_op jit(solution)/shard_map/pallas_call | solution.py:100
  41.1 0.9 %slice_bitcast_fusion = f32[6,128]{0,1:T(8,128)S(1)} fusion(f32[128,128]{1,0:T(8,128)} %shard_map.113), kind=kLoop, calls=%fused_computation.5 | loop fusion | bytes 6144 | tf_op jit(solution)/shard_map/transpose | solution.py:111
  42.0 2.4 %collective-permute-start.3 = (f32[6,128]{0,1:T(8,128)S(1)}, f32[6,128]{0,1:T(8,128)S(1)}, u32[]{:S(2)}, u32[]{:S(2)}) collective-permute-start(f32[6,128]{0,1:T(8,128)S(1)} %slice_bitcast_fusion), channel_id=1, source_target_pairs={{0,128},{32,160},{64,192},{96,224},{128,0},{160,32},{192,64},{224,... | collective-permute-start | bytes 9224 | tf_op jit(solution)/shard_map/ppermute | solution.py:18
  44.4 1.0 %slice.67 = f32[1,32,256]{2,0,1:T(1,128)S(1)} slice(f32[7,32,256]{2,0,1:T(8,128)} %copy-done.1), slice={[6:7], [0:32], [0:256]} | slice | bytes 65536 | tf_op jit(solution)/shard_map/slice | solution.py:137
  45.4 0.1 broadcast_in_dim.78
  45.4 0.1 subtract_multiply_fusion
  45.5 0.8 %pad_maximum_fusion.src_ref = f32[8,8192]{1,0:T(8,128)} fusion(f32[1,8192]{1,0:T(1,128)S(1)} %get-tuple-element.25, f32[1,8192]{1,0:T(1,128)S(1)} %get-tuple-element.24, f32[6,8192]{1,0:T(8,128)S(1)} %bitcast.47), kind=kLoop, calls=%fused_computation.4 | loop fusion | flops 131072 | bytes 524288 | tf_op jit(solution)/shard_map/concatenate | solution.py:175
  46.3 0.8 %broadcast_in_dim.80.tgt_ref = f32[6,64,128]{2,1,0:T(8,128)} broadcast(f32[6,64]{1,0:T(8,128)S(1)} %constant_dynamic-slice_fusion.1), dimensions={0,1} | broadcast | bytes 198144 | tf_op jit(solution)/shard_map/broadcast_in_dim | solution.py:98
  47.1 5.6 %shard_map.114 = f32[64,128]{1,0:T(8,128)} custom-call(f32[6,64,128]{2,1,0:T(8,128)} %broadcast_in_dim.80.tgt_ref, f32[7,8192]{1,0:T(8,128)} %bitcast.45), custom_call_target="tpu_custom_call" | custom-call | flops 22020096 | bytes 458752 | tf_op jit(solution)/shard_map/pallas_call | solution.py:100
  52.7 0.0 collective-permute-done.3
  52.7 0.8 %fusion = f32[6,64]{0,1:T(8,128)S(1)} fusion(f32[64,128]{1,0:T(8,128)} %shard_map.114, f32[6,128]{0,1:T(8,128)S(1)} %collective-permute-done.3, s32[]{:T(128)S(6)} %select_n.149), kind=kLoop, calls=%fused_computation.7 | loop fusion | flops 384 | bytes 4612 | tf_op jit(solution)/shard_map/add | solution.py:163
  53.4 0.7 collective-permute-start.4
  54.1 0.7 %broadcast_in_dim.81.tgt_ref = f32[6,32,128]{2,1,0:T(8,128)} broadcast(f32[6,32]{1,0:T(8,128)S(1)} %constant_dynamic-slice_fusion), dimensions={0,1} | broadcast | bytes 99072 | tf_op jit(solution)/shard_map/broadcast_in_dim | solution.py:98
  54.8 3.6 %shard_map.115 = f32[32,128]{1,0:T(8,128)} custom-call(f32[6,32,128]{2,1,0:T(8,128)} %broadcast_in_dim.81.tgt_ref, f32[7,8192]{1,0:T(8,128)} %bitcast.46), custom_call_target="tpu_custom_call" | custom-call | flops 11010048 | bytes 344064 | tf_op jit(solution)/shard_map/pallas_call | solution.py:100
  58.4 0.7 %broadcast_in_dim.41.tgt_ref = f32[6,32,128]{2,1,0:T(8,128)} broadcast(f32[6,32]{1,0:T(8,128)S(1)} %copy.80), dimensions={0,1} | broadcast | bytes 99072 | tf_op jit(solution)/shard_map/broadcast_in_dim | solution.py:98
  59.1 4.0 %shard_map.112 = f32[32,128]{1,0:T(8,128)} custom-call(f32[6,32,128]{2,1,0:T(8,128)} %broadcast_in_dim.41.tgt_ref, f32[8,8192]{1,0:T(8,128)} %pad_maximum_fusion.src_ref), custom_call_target="tpu_custom_call" | custom-call | flops 14155776 | bytes 376832 | tf_op jit(solution)/shard_map/pallas_call | solution.py:100
  63.2 0.0 collective-permute-done.4
  63.2 2.8 %collective-permute-start.5 = (f32[6,32]{0,1:T(8,128)S(1)}, f32[6,32]{0,1:T(8,128)S(1)}, u32[]{:S(2)}, u32[]{:S(2)}) collective-permute-start(f32[6,32]{0,1:T(8,128)S(1)} %fusion.5), channel_id=1, source_target_pairs={{0,32},{32,0},{64,96},{96,64},{128,160},{160,128},{192,224},{224,1... | collective-permute-start | bytes 2312 | tf_op jit(solution)/shard_map/ppermute | solution.py:18
  66.0 2.5 %collective-permute-done.5 = f32[6,32]{0,1:T(8,128)S(1)} collective-permute-done((f32[6,32]{0,1:T(8,128)S(1)}, f32[6,32]{0,1:T(8,128)S(1)}, u32[]{:S(2)}, u32[]{:S(2)}) %collective-permute-start.5) | collective-permute-done | bytes 800 | tf_op jit(solution)/shard_map/ppermute | solution.py:18
  68.5 0.1 fusion.13
  68.6 0.7 copy.89
  69.3 0.7 copy.90
  69.9 0.1 fusion.10
  70.0 0.1 copy.88
  70.1 0.1 copy.87
  70.2 0.6 pad_maximum_fusion.3
  (20 shorter events, 0.1 us)
Async XLA Ops:
  0.6 0.8 %copy-start = (f32[256]{0:T(256)S(1)}, f32[256]{0:T(256)}, u32[]{:S(2)}) copy-start(f32[256]{0:T(256)} %param.15) | copy-start | bytes 3076
  2.1 0.7 copy-start.7
  3.6 27.1 %all-to-all-start = ((f32[7,32,256]{2,0,1:T(8,128)}), f32[7,32,256]{2,0,1:T(8,128)S(1)}, u32[]{:S(2)}, u32[]{:S(2)}) async-start(f32[7,32,256]{2,0,1:T(8,128)} %broadcast_in_dim.46), calls=%async_computation | async-start | bytes 524288 | tf_op jit(solution)/shard_map/all_to_all | solution.py:37
  13.2 0.7 copy-start.8
  15.3 5.3 %collective-permute-start = (f32[6,32]{0,1:T(8,128)S(1)}, f32[6,32]{0,1:T(8,128)S(1)}, u32[]{:S(2)}, u32[]{:S(2)}) collective-permute-start(f32[6,32]{0,1:T(8,128)S(1)} %select_bitcast_fusion), channel_id=1, source_target_pairs={{0,32},{32,0},{64,96},{96,64},{128,160},{160,128},{192,224},{224,1... | collective-permute-start | bytes 2312 | tf_op jit(solution)/shard_map/ppermute | solution.py:18
  18.8 0.7 copy-start.9
  20.7 3.6 %collective-permute-start.1 = (f32[6,64]{1,0:T(8,128)S(1)}, f32[6,64]{1,0:T(8,128)S(1)}, u32[]{:S(2)}, u32[]{:S(2)}) collective-permute-start(f32[6,64]{1,0:T(8,128)S(1)} %maximum_select_fusion.1), channel_id=1, source_target_pairs={{0,64},{32,96},{64,0},{96,32},{128,192},{160,224},{192,128},{224,1... | collective-permute-start | bytes 4616 | tf_op jit(solution)/shard_map/ppermute | solution.py:18
  24.5 5.9 %collective-permute-start.2 = (f32[6,128]{1,0:T(8,128)S(1)}, f32[6,128]{1,0:T(8,128)S(1)}, u32[]{:S(2)}, u32[]{:S(2)}) collective-permute-start(f32[6,128]{1,0:T(8,128)S(1)} %maximum_select_fusion.2), channel_id=1, source_target_pairs={{0,128},{32,160},{64,192},{96,224},{128,0},{160,32},{192,64},{224,... | collective-permute-start | bytes 9224 | tf_op jit(solution)/shard_map/ppermute | solution.py:18
  27.7 0.7 copy-start.4
  28.4 0.7 copy-start.5
  30.7 0.9 %copy-start.1 = (f32[7,32,256]{2,0,1:T(8,128)}, f32[7,32,256]{2,0,1:T(8,128)S(1)}, u32[]{:S(2)}) copy-start(f32[7,32,256]{2,0,1:T(8,128)S(1)} %all-to-all-done) | copy-start | bytes 688132
  41.1 4.4 %copy-start.2 = (f32[7,32,256]{2,0,1:T(8,128)S(1)}, f32[7,32,256]{2,0,1:T(8,128)}, u32[]{:S(2)}) copy-start(f32[7,32,256]{2,0,1:T(8,128)} %copy-done.1) | copy-start | bytes 688132
  42.0 10.7 %collective-permute-start.3 = (f32[6,128]{0,1:T(8,128)S(1)}, f32[6,128]{0,1:T(8,128)S(1)}, u32[]{:S(2)}, u32[]{:S(2)}) collective-permute-start(f32[6,128]{0,1:T(8,128)S(1)} %slice_bitcast_fusion), channel_id=1, source_target_pairs={{0,128},{32,160},{64,192},{96,224},{128,0},{160,32},{192,64},{224,... | collective-permute-start | bytes 9224 | tf_op jit(solution)/shard_map/ppermute | solution.py:18
  53.4 9.7 %collective-permute-start.4 = (f32[6,64]{0,1:T(8,128)S(1)}, f32[6,64]{0,1:T(8,128)S(1)}, u32[]{:S(2)}, u32[]{:S(2)}) collective-permute-start(f32[6,64]{0,1:T(8,128)S(1)} %fusion), channel_id=1, source_target_pairs={{0,64},{32,96},{64,0},{96,32},{128,192},{160,224},{192,128},{224,1... | collective-permute-start | bytes 4616 | tf_op jit(solution)/shard_map/ppermute | solution.py:18
  59.1 4.0 %copy-start.6 = (f32[32,128]{1,0:T(8,128)S(1)}, f32[32,128]{1,0:T(8,128)}, u32[]{:S(2)}) copy-start(f32[32,128]{1,0:T(8,128)} %shard_map.115) | copy-start | bytes 49156
  63.2 2.9 %copy-start.3 = (f32[32,128]{1,0:T(8,128)S(1)}, f32[32,128]{1,0:T(8,128)}, u32[]{:S(2)}) copy-start(f32[32,128]{1,0:T(8,128)} %shard_map.112) | copy-start | bytes 49156
  63.2 5.3 %collective-permute-start.5 = (f32[6,32]{0,1:T(8,128)S(1)}, f32[6,32]{0,1:T(8,128)S(1)}, u32[]{:S(2)}, u32[]{:S(2)}) collective-permute-start(f32[6,32]{0,1:T(8,128)S(1)} %fusion.5), channel_id=1, source_target_pairs={{0,32},{32,0},{64,96},{96,64},{128,160},{160,128},{192,224},{224,1... | collective-permute-start | bytes 2312 | tf_op jit(solution)/shard_map/ppermute | solution.py:18

commit v7 on v5

--- a/solution.py
+++ b/solution.py
@@ -28,19 +28,11 @@
     return block
 
 
-def gather_doubling_split(block, axis):
-    me = lax.axis_index(axis)
-    last = lax.axis_size(axis) // 2
-    bit = 1
-    while bit < last:
-        got = exchange(block, axis, bit)
-        upper = (me // bit) % 2 == 1
-        block = jnp.where(
-            upper, jnp.concatenate([got, block], 1), jnp.concatenate([block, got], 1)
-        )
-        bit *= 2
-    got = exchange(block, axis, last)
-    return block, got
+def gather_all_to_all(block, axis):
+    size = lax.axis_size(axis)
+    spread = jnp.broadcast_to(block[:, None, :], (block.shape[0], size, block.shape[1]))
+    got = lax.all_to_all(spread, axis, 1, 1, tiled=True)
+    return got.reshape(block.shape[0], size * block.shape[1])
 
 
 def pair_terms(targets, sources):
@@ -91,19 +83,24 @@
     neighbour_list,
     neighbour_count,
 ):
-    moved_pos = position + elapsed * (
-        velocity + elapsed * (0.5 * accel_old + elapsed * jerk_old / 6.0)
-    )
-    turned = velocity + elapsed * (accel_old + 0.5 * elapsed * jerk_old)
-    sources = jnp.concatenate([moved_pos, turned], axis=0)
-    own_set = jnp.take(sources, active_stars, axis=1)
+    def predict(pos, vel, acc, jerk, time):
+        moved_pos = pos + time * (vel + time * (0.5 * acc + time * jerk / 6.0))
+        turned = vel + time * (acc + 0.5 * time * jerk)
+        return jnp.concatenate([moved_pos, turned], axis=0)
+
+    raw = jnp.concatenate([position, velocity, accel_old, jerk_old, elapsed[None, :]], axis=0)
+    raw_act = raw.at[:, active_stars].get(mode="promise_in_bounds")
+    own_set = predict(raw_act[0:3], raw_act[3:6], raw_act[6:9], raw_act[9:12], raw_act[12])
+    sources = predict(position, velocity, accel_old, jerk_old, elapsed)
     act_dev = active_stars.shape[0]
     block_data = jnp.concatenate([sources, masses[None, :]], axis=0)
     targets = gather_doubling(own_set, "blk")
-    near_half, far_half = gather_doubling_split(block_data, "grp")
+    group = gather_all_to_all(block_data, "grp")
+    group_src = group[:6]
+    group_mass = group[6]
     blk_size = lax.axis_size("blk")
     blk_here = lax.axis_index("blk")
-    block_total = lax.axis_size("grp") * block_data.shape[1] // BLOCK
+    block_total = group_src.shape[1] // BLOCK
     slot_total = neighbour_list.shape[1]
     own_live = jnp.arange(slot_total) < neighbour_count[0]
     near = jnp.any(
@@ -111,43 +108,15 @@
         & (neighbour_list[0][:, None] == jnp.arange(block_total)[None, :]),
         axis=0,
     ).astype(jnp.float32)
-    grp_here = lax.axis_index("grp")
-    half_devices = lax.axis_size("grp") // 2
-    blocks_half = near_half.shape[1] // BLOCK
-    blocks_device = block_data.shape[1] // BLOCK
-    near_start = (grp_here - grp_here % half_devices) * blocks_device
-    far_device = grp_here ^ half_devices
-    far_start = (far_device - far_device % half_devices) * blocks_device
-    near_a = lax.dynamic_slice_in_dim(near, near_start, blocks_half)
-    near_b = lax.dynamic_slice_in_dim(near, far_start, blocks_half)
-    src_a, mass_a = near_half[:6], near_half[6]
-    src_b, mass_b = far_half[:6], far_half[6]
-
-    owners = jnp.arange(blk_size)
-    keep = jnp.where((owners == blk_here)[:, None], 1.0 - near_a[None, :], 1.0)
-    pieces = targets.reshape(6, blk_size, act_dev).transpose(1, 0, 2)
-
-    def first_piece(items):
-        target_piece, keep_piece = items
-        piece_weight = jnp.repeat(keep_piece, BLOCK)[None, :] * mass_a[None, :]
-        return pair_sums(target_piece, src_a, piece_weight)
-
-    first = lax.map(first_piece, (pieces, keep))
-    first = first.transpose(1, 0, 2).reshape(6, blk_size * act_dev)
-    irregular_a = pair_sums(
-        own_set, src_a, (jnp.repeat(near_a, BLOCK) * mass_a)[None, :]
-    )
-
-    weight = mass_b[None, :]
+    weight = group_mass[None, :]
 
     def owner_sums(start, count):
         pieces = lax.dynamic_slice_in_dim(targets, start * act_dev, count * act_dev, 1)
-        done = lax.dynamic_slice_in_dim(first, start * act_dev, count * act_dev, 1)
         if count == 1:
-            return pair_sums(pieces, src_b, weight) + done
+            return pair_sums(pieces, group_src, weight)
         pieces = pieces.reshape(6, count, act_dev).transpose(1, 0, 2)
-        sums = lax.map(lambda piece: pair_sums(piece, src_b, weight), pieces)
-        return sums.transpose(1, 0, 2).reshape(6, count * act_dev) + done
+        sums = lax.map(lambda piece: pair_sums(piece, group_src, weight), pieces)
+        return sums.transpose(1, 0, 2).reshape(6, count * act_dev)
 
     def owner_cols(block, owner, span):
         return lax.dynamic_slice_in_dim(block, (owner % span) * act_dev, act_dev, 1)
@@ -169,23 +138,21 @@
         + owner_cols(got2, partner, bit2)
     )
     got1 = exchange(sent1, "blk", 1)
-    near_rep = jnp.repeat(near_b, BLOCK)[None, :]
-    own_far, irregular_b = pair_sums_split(
-        own_set, src_b, weight * (1.0 - near_rep), weight * near_rep
+    near_rep = jnp.repeat(near, BLOCK)[None, :]
+    own_far, irregular = pair_sums_split(
+        own_set, group_src, weight * (1.0 - near_rep), weight * near_rep
     )
     regular = (
         own_far
-        + owner_cols(first, blk_here, blk_size)
         + owner_cols(got4, blk_here, bit4)
         + owner_cols(got2, blk_here, bit2)
         + got1
     )
-    irregular = irregular_a + irregular_b
     accel_now = regular[:3] + irregular[:3]
     jerk_now = regular[3:] + irregular[3:]
-    step_time = jnp.take(elapsed, active_stars)
-    start_accel = jnp.take(accel_old, active_stars, axis=1)
-    start_jerk = jnp.take(jerk_old, active_stars, axis=1)
+    step_time = raw_act[12]
+    start_accel = raw_act[6:9]
+    start_jerk = raw_act[9:12]
     change = start_accel - accel_now
     snap_term = -6.0 * change - step_time * (4.0 * start_jerk + 2.0 * jerk_now)
     crackle_term = 12.0 * change + 6.0 * step_time * (start_jerk + jerk_now)

time: 89.4 us -> 60.2 us (0.67); the launches traced: 87.7 us -> 59.4 us
  local copies, waits for them, and re-layouts: 20.5 us -> 6.57 us
  waiting for transfers between devices: 15.9 us -> 7.56 us
  other arithmetic: 24.1 us -> 19.3 us
    ppermute x11 -> x6, starting transfers between devices: 25.1 us -> 14.5 us  [exchange(): return lax.ppermute(block, axis, [(i, i ^ bit) for i in range(size)])]
    slice x14 -> x7, local copies, waits for them, and re-layouts: 11.5 us -> 0.99 us  [pair_terms(): rel_x = sources[3][None, :] - targets[3][:, None]]
    all_to_all x0 -> x1, starting transfers between devices: none -> 9.8 us  [gather_all_to_all(): got = lax.all_to_all(spread, axis, 1, 1, tiled=True)]
    ppermute x11 -> x6, waiting for transfers between devices: 15.9 us -> 7.56 us  [exchange(): return lax.ppermute(block, axis, [(i, i ^ bit) for i in range(size)])]
    reduce_sum x16 -> x7, other arithmetic: 16.7 us -> 13.9 us  [pair_sums(): return jnp.stack([jnp.sum(scaled * term, axis=1) for term in term_list])]
    gather x6 -> x2, local copies, waits for them, and re-layouts: 2.6 us -> 0.65 us  [per_device(): raw_act = raw.at[:, active_stars].get(mode='promise_in_bounds')]
    slice x1 -> x0, other arithmetic: 1.52 us -> none  [pair_terms(): rel_x = sources[3][None, :] - targets[3][:, None]]
    unnamed x18, local copies, waits for them, and re-layouts: 3.87 us -> 2.45 us
  transfers between devices with their start and end apart: 11 -> 7, of which waited for: 8 -> 5; matrix products, arithmetic and copies ran while one was open for 35% -> 19% of each run, Pallas kernels for 0% -> 0%
where the time goes in v7:
time: 60.2 us; the launch traced here: 59.4 us
  starting transfers between devices  24.3 us (40%)
  other arithmetic  19.3 us (32%)
  waiting for transfers between devices  7.56 us (13%)
  local copies, waits for them, and re-layouts  6.57 us (11%)
  between operations  1.48 us (2%)
    ppermute x6, starting transfers between devices, exchange(): return lax.ppermute(block, axis, [(i, i ^ bit) for i in range(size)])  14.5 us
    reduce_sum x7, other arithmetic, pair_sums(): return jnp.stack([jnp.sum(scaled * term, axis=1) for term in term_list])  13.9 us
    all_to_all x1, starting transfers between devices, gather_all_to_all(): got = lax.all_to_all(spread, axis, 1, 1, tiled=True)  9.8 us
    ppermute x6, waiting for transfers between devices, exchange(): return lax.ppermute(block, axis, [(i, i ^ bit) for i in range(size)])  7.56 us
    reduce_sum x1, other arithmetic, pair_sums_split(): jnp.sum(near_scaled * term, axis=1)  2.66 us
    unnamed x18, local copies, waits for them, and re-layouts  2.45 us
  transfers between devices with their start and end apart: 7, of which 5 were waited for; matrix products, arithmetic and copies ran while one was open for 19% of the time, Pallas kernels for 0%

profile of v7, /device:TPU:32, one launch (start us, length us, event | category | flops | bytes accessed | tf_op | source)
XLA Modules:
  0.0 59.4 jit_solution(3610009202220574252)
XLA Ops:
  0.6 0.0 copy-start.5
  0.6 0.7 %broadcast_multiply_fusion = f32[256]{0:T(256)S(1)} fusion(f32[256]{0:T(256)} %param.17), kind=kLoop, calls=%fused_computation.210 | loop fusion | flops 256 | bytes 2048 | tf_op jit(solution)/shard_map/mul | solution.py:88
  1.4 0.0 copy-done.5
  1.4 0.7 %multiply_add_fusion.1 = (f32[3,256]{1,0:T(4,128)S(1)}, f32[3,256]{1,0:T(4,128)S(1)}) fusion(f32[3,256]{1,0:T(4,128)} %param.13, f32[3,256]{1,0:T(4,128)} %param.14, f32[3,256]{1,0:T(4,128)} %param.16, f32[3,256]{1,0:T(4,128)} %param.15, f32[256]{0:T(256)S(1)} %copy-done.5, f32[256]{0:T(256)S(1)} %broadcast_multiply_fusion), kind=kLoop, calls=%fused_computation.183 | loop fusion | flops 9216 | bytes 20480 | tf_op jit(solution)/shard_map/add | solution.py:87
  2.1 0.0 copy-start.6
  2.1 0.7 %copy-done.6 = f32[256]{0:T(256)S(1)} copy-done((f32[256]{0:T(256)S(1)}, f32[256]{0:T(256)}, u32[]{:S(2)}) %copy-start.6) | copy-done | bytes 1048
  2.8 0.7 %broadcast_in_dim.42 = f32[7,32,256]{2,0,1:T(8,128)} broadcast(f32[7,256]{1,0:T(8,128)S(1)} %pad_maximum_fusion), dimensions={0,2} | broadcast | bytes 236544 | tf_op jit(solution)/shard_map/broadcast_in_dim | solution.py:33
  3.6 9.8 %all-to-all-start = ((f32[7,32,256]{2,0,1:T(8,128)}), f32[7,32,256]{2,0,1:T(8,128)S(1)}, u32[]{:S(2)}, u32[]{:S(2)}) async-start(f32[7,32,256]{2,0,1:T(8,128)} %broadcast_in_dim.42), calls=%async_computation | async-start | bytes 524288 | tf_op jit(solution)/shard_map/all_to_all | solution.py:34
  13.4 0.0 copy-done.1
  13.4 0.0 copy-done.2
  13.4 0.1 concatenate.33
  13.5 0.1 copy.97
  13.7 0.5 copy-done.7
  14.2 0.6 gather_fusion
  14.8 0.1 copy.98
  14.9 2.8 %collective-permute-start = (f32[6,32]{1,0:T(8,128)S(1)}, f32[6,32]{1,0:T(8,128)S(1)}, u32[]{:S(2)}, u32[]{:S(2)}) collective-permute-start(f32[6,32]{1,0:T(8,128)S(1)} %pad_maximum_fusion.1), channel_id=1, source_target_pairs={{0,32},{32,0},{64,96},{96,64},{128,160},{160,128},{192,224},{224,1... | collective-permute-start | bytes 2312 | tf_op jit(solution)/shard_map/ppermute | solution.py:15
  18.4 0.0 copy-start.8
  18.4 0.6 %copy-done.8 = s32[1,64]{1,0:T(1,128)S(1)} copy-done((s32[1,64]{1,0:T(1,128)S(1)}, s32[1,64]{1,0:T(1,128)}, u32[]{:S(2)}) %copy-start.8) | copy-done | bytes 280
  19.0 0.1 fusion.80
  19.2 0.9 %collective-permute-done = f32[6,32]{1,0:T(8,128)S(1)} collective-permute-done((f32[6,32]{1,0:T(8,128)S(1)}, f32[6,32]{1,0:T(8,128)S(1)}, u32[]{:S(2)}, u32[]{:S(2)}) %collective-permute-start) | collective-permute-done | bytes 800 | tf_op jit(solution)/shard_map/ppermute | solution.py:15
  20.1 0.1 maximum_select_fusion.1
  20.2 1.6 %collective-permute-start.1 = (f32[6,64]{1,0:T(8,128)S(1)}, f32[6,64]{1,0:T(8,128)S(1)}, u32[]{:S(2)}, u32[]{:S(2)}) collective-permute-start(f32[6,64]{1,0:T(8,128)S(1)} %maximum_select_fusion.1), channel_id=1, source_target_pairs={{0,64},{32,96},{64,0},{96,32},{128,192},{160,224},{192,128},{224,1... | collective-permute-start | bytes 4616 | tf_op jit(solution)/shard_map/ppermute | solution.py:15
  21.8 2.0 %collective-permute-done.1 = f32[6,64]{1,0:T(8,128)S(1)} collective-permute-done((f32[6,64]{1,0:T(8,128)S(1)}, f32[6,64]{1,0:T(8,128)S(1)}, u32[]{:S(2)}, u32[]{:S(2)}) %collective-permute-start.1) | collective-permute-done | bytes 1568 | tf_op jit(solution)/shard_map/ppermute | solution.py:15
  23.8 0.1 maximum_select_fusion.2
  23.9 3.2 %collective-permute-start.2 = (f32[6,128]{1,0:T(8,128)S(1)}, f32[6,128]{1,0:T(8,128)S(1)}, u32[]{:S(2)}, u32[]{:S(2)}) collective-permute-start(f32[6,128]{1,0:T(8,128)S(1)} %maximum_select_fusion.2), channel_id=1, source_target_pairs={{0,128},{32,160},{64,192},{96,224},{128,0},{160,32},{192,64},{224,... | collective-permute-start | bytes 9224 | tf_op jit(solution)/shard_map/ppermute | solution.py:15
  27.1 1.9 %collective-permute-done.2 = f32[6,128]{1,0:T(8,128)S(1)} collective-permute-done((f32[6,128]{1,0:T(8,128)S(1)}, f32[6,128]{1,0:T(8,128)S(1)}, u32[]{:S(2)}, u32[]{:S(2)}) %collective-permute-start.2) | collective-permute-done | bytes 3104 | tf_op jit(solution)/shard_map/ppermute | solution.py:15
  29.0 0.1 constant_dynamic-slice_fusion.14
  29.1 0.1 reshape.116
  29.2 0.1 constant_dynamic-slice_fusion.13
  29.3 0.1 reshape.118
  29.3 0.1 constant_dynamic-slice_fusion.12
  29.4 0.0 all-to-all-done
  29.4 0.2 fusion.84
  29.6 8.9 %while.20 = (s32[]{:T(128)}, f32[4,6,32]{2,1,0:T(8,128)S(1)}, f32[1,8192]{1,0:T(1,128)S(1)}, f32[6,8192]{1,0:T(8,128)S(1)}, f32[4,6,32]{2,0,1:T(4,128)S(1)}, /*i...) while((s32[]{:T(128)}, f32[4,6,32]{2,1,0:T(8,128)S(1)}, f32[1,8192]{1,0:T(1,128)S(1)}, ...), condition=%wide.region_14.15_spmd, body=%wide.region_7.0_spmd.sunk | while | flops 10485575 | bytes 635597 | solution.py:118
  29.6 0.1 fusion.92
  29.8 2.0 %fusion.93 = (f32[32]{0:T(128)S(1)}, f32[32]{0:T(128)S(1)}, f32[32]{0:T(128)S(1)}, f32[32]{0:T(128)S(1)}, f32[32]{0:T(128)S(1)}, /*index=5*/f32[32]{0:T(128)S(1)}) fusion(f32[32]{0:T(128)S(1)} %get-tuple-element.312, f32[8192]{0:T(1024)S(1)} %bitcast.213, f32[32]{0:T(128)S(1)} %get-tuple-element.314, f32[8192]{0:T(1024)S(1)} %bitcast.215, ...), kind=kLoop, calls=%fused_computation.22.clone.1 | loop fusion | flops 10485568 | bytes 230912 | tf_op jit(solution)/shard_map/while/body/eval_jaxpr/reduce_sum | solution.py:63
  31.9 0.1 fusion.92
  32.0 2.0 %fusion.93 = (f32[32]{0:T(128)S(1)}, f32[32]{0:T(128)S(1)}, f32[32]{0:T(128)S(1)}, f32[32]{0:T(128)S(1)}, f32[32]{0:T(128)S(1)}, /*index=5*/f32[32]{0:T(128)S(1)}) fusion(f32[32]{0:T(128)S(1)} %get-tuple-element.312, f32[8192]{0:T(1024)S(1)} %bitcast.213, f32[32]{0:T(128)S(1)} %get-tuple-element.314, f32[8192]{0:T(1024)S(1)} %bitcast.215, ...), kind=kLoop, calls=%fused_computation.22.clone.1 | loop fusion | flops 10485568 | bytes 230912 | tf_op jit(solution)/shard_map/while/body/eval_jaxpr/reduce_sum | solution.py:63
  34.1 0.1 fusion.92
  34.2 2.0 %fusion.93 = (f32[32]{0:T(128)S(1)}, f32[32]{0:T(128)S(1)}, f32[32]{0:T(128)S(1)}, f32[32]{0:T(128)S(1)}, f32[32]{0:T(128)S(1)}, /*index=5*/f32[32]{0:T(128)S(1)}) fusion(f32[32]{0:T(128)S(1)} %get-tuple-element.312, f32[8192]{0:T(1024)S(1)} %bitcast.213, f32[32]{0:T(128)S(1)} %get-tuple-element.314, f32[8192]{0:T(1024)S(1)} %bitcast.215, ...), kind=kLoop, calls=%fused_computation.22.clone.1 | loop fusion | flops 10485568 | bytes 230912 | tf_op jit(solution)/shard_map/while/body/eval_jaxpr/reduce_sum | solution.py:63
  36.3 0.1 fusion.92
  36.4 2.0 %fusion.93 = (f32[32]{0:T(128)S(1)}, f32[32]{0:T(128)S(1)}, f32[32]{0:T(128)S(1)}, f32[32]{0:T(128)S(1)}, f32[32]{0:T(128)S(1)}, /*index=5*/f32[32]{0:T(128)S(1)}) fusion(f32[32]{0:T(128)S(1)} %get-tuple-element.312, f32[8192]{0:T(1024)S(1)} %bitcast.213, f32[32]{0:T(128)S(1)} %get-tuple-element.314, f32[8192]{0:T(1024)S(1)} %bitcast.215, ...), kind=kLoop, calls=%fused_computation.22.clone.1 | loop fusion | flops 10485568 | bytes 230912 | tf_op jit(solution)/shard_map/while/body/eval_jaxpr/reduce_sum | solution.py:63
  38.5 0.1 reshape.117
  38.6 3.2 %collective-permute-start.3 = (f32[6,128]{1,0:T(8,128)S(1)}, f32[6,128]{1,0:T(8,128)S(1)}, u32[]{:S(2)}, u32[]{:S(2)}) collective-permute-start(f32[6,128]{1,0:T(8,128)S(1)} %reshape.117), channel_id=1, source_target_pairs={{0,128},{32,160},{64,192},{96,224},{128,0},{160,32},{192,64},{224,... | collective-permute-start | bytes 9224 | tf_op jit(solution)/shard_map/ppermute | solution.py:15
  41.8 4.4 %while.21 = (s32[]{:T(128)}, f32[2,6,32]{2,1,0:T(8,128)S(1)}, f32[1,8192]{1,0:T(1,128)S(1)}, f32[6,8192]{1,0:T(8,128)S(1)}, f32[2,6,32]{2,0,1:T(2,128)S(1)}, /*i...) while((s32[]{:T(128)}, f32[2,6,32]{2,1,0:T(8,128)S(1)}, f32[1,8192]{1,0:T(1,128)S(1)}, ...), condition=%wide.region_22.23_spmd, body=%wide.region_15.22_spmd.sunk | while | flops 10485575 | bytes 635597 | solution.py:118
  41.8 0.1 fusion.95
  42.0 2.0 %fusion.96 = (f32[32]{0:T(128)S(1)}, f32[32]{0:T(128)S(1)}, f32[32]{0:T(128)S(1)}, f32[32]{0:T(128)S(1)}, f32[32]{0:T(128)S(1)}, /*index=5*/f32[32]{0:T(128)S(1)}) fusion(f32[32]{0:T(128)S(1)} %get-tuple-element.335, f32[8192]{0:T(1024)S(1)} %bitcast.219, f32[32]{0:T(128)S(1)} %get-tuple-element.337, f32[8192]{0:T(1024)S(1)} %bitcast.221, ...), kind=kLoop, calls=%fused_computation.68.clone.1 | loop fusion | flops 10485568 | bytes 230912 | tf_op jit(solution)/shard_map/while/body/eval_jaxpr/reduce_sum | solution.py:63
  44.0 0.1 fusion.95
  44.2 2.0 %fusion.96 = (f32[32]{0:T(128)S(1)}, f32[32]{0:T(128)S(1)}, f32[32]{0:T(128)S(1)}, f32[32]{0:T(128)S(1)}, f32[32]{0:T(128)S(1)}, /*index=5*/f32[32]{0:T(128)S(1)}) fusion(f32[32]{0:T(128)S(1)} %get-tuple-element.335, f32[8192]{0:T(1024)S(1)} %bitcast.219, f32[32]{0:T(128)S(1)} %get-tuple-element.337, f32[8192]{0:T(1024)S(1)} %bitcast.221, ...), kind=kLoop, calls=%fused_computation.68.clone.1 | loop fusion | flops 10485568 | bytes 230912 | tf_op jit(solution)/shard_map/while/body/eval_jaxpr/reduce_sum | solution.py:63
  46.2 0.1 fusion.78
  46.3 2.7 %multiply_reduce_fusion = (f32[32]{0:T(128)S(1)}, f32[32]{0:T(128)S(1)}, f32[32]{0:T(128)S(1)}, f32[32]{0:T(128)S(1)}, f32[32]{0:T(128)S(1)}, /*index=5*/f32[32]...) fusion(f32[32]{0:T(128)S(1)} %get-tuple-element.211, ...), kind=kLoop, calls=%fused_computation.158 | loop fusion | flops 13893248 | bytes 264448 | tf_op jit(solution)/shard_map/reduce_sum | solution.py:71
  49.0 0.1 reshape.119
  49.1 0.0 collective-permute-done.3
  49.1 0.1 dynamic-slice_add_fusion.1
  49.1 0.9 %collective-permute-start.4 = (f32[6,64]{1,0:T(8,128)S(1)}, f32[6,64]{1,0:T(8,128)S(1)}, u32[]{:S(2)}, u32[]{:S(2)}) collective-permute-start(f32[6,64]{1,0:T(8,128)S(1)} %dynamic-slice_add_fusion.1), channel_id=1, source_target_pairs={{0,64},{32,96},{64,0},{96,32},{128,192},{160,224},{192,128},{224,1... | collective-permute-start | bytes 4616 | tf_op jit(solution)/shard_map/ppermute | solution.py:15
  50.0 2.0 %fusion.51 = (f32[32]{0:T(128)S(1)}, f32[32]{0:T(128)S(1)}, f32[32]{0:T(128)S(1)}, f32[32]{0:T(128)S(1)}, f32[32]{0:T(128)S(1)}, /*index=5*/f32[32]{0:T(128)S(1)}) fusion(f32[32]{0:T(128)S(1)} %get-tuple-element.205, f32[32]{0:T(128)S(1)} %get-tuple-element.207, f32[8192]{0:T(1024)S(1)} %bitcast.238, f32[8192]{0:T(1024)S(1)} %bitcast.242, ...), kind=kLoop, calls=%fused_computation.133 | loop fusion | flops 10485568 | bytes 230912 | tf_op jit(solution)/shard_map/reduce_sum | solution.py:63
  52.0 0.9 %collective-permute-done.4 = f32[6,64]{1,0:T(8,128)S(1)} collective-permute-done((f32[6,64]{1,0:T(8,128)S(1)}, f32[6,64]{1,0:T(8,128)S(1)}, u32[]{:S(2)}, u32[]{:S(2)}) %collective-permute-start.4) | collective-permute-done | bytes 1568 | tf_op jit(solution)/shard_map/ppermute | solution.py:15
  52.9 0.1 dynamic-slice_add_fusion
  53.0 2.7 %collective-permute-start.5 = (f32[6,32]{1,0:T(8,128)S(1)}, f32[6,32]{1,0:T(8,128)S(1)}, u32[]{:S(2)}, u32[]{:S(2)}) collective-permute-start(f32[6,32]{1,0:T(8,128)S(1)} %dynamic-slice_add_fusion), channel_id=1, source_target_pairs={{0,32},{32,0},{64,96},{96,64},{128,160},{160,128},{192,224},{224,1... | collective-permute-start | bytes 2312 | tf_op jit(solution)/shard_map/ppermute | solution.py:15
  55.8 0.6 %stack.129 = f32[6,32]{1,0:T(8,128)} concatenate(f32[1,32]{1,0:T(1,128)S(1)} %bitcast.277, f32[1,32]{1,0:T(1,128)S(1)} %bitcast.271, f32[1,32]{1,0:T(1,128)S(1)} %bitcast.274, f32[1,32]{1,0:T(1,128)S(1)} %bitcast.265, f32[1,32]{1,0:T(1,128)S(1)} %bitcast.268, f32[1,32]{1,0:T(1,128)S(1)} %bitcast.262), dimensions={0} | concatenate | bytes 1536 | tf_op jit(solution)/shard_map/stack | solution.py:71
  56.4 1.8 %collective-permute-done.5 = f32[6,32]{1,0:T(8,128)S(1)} collective-permute-done((f32[6,32]{1,0:T(8,128)S(1)}, f32[6,32]{1,0:T(8,128)S(1)}, u32[]{:S(2)}, u32[]{:S(2)}) %collective-permute-start.5) | collective-permute-done | bytes 800 | tf_op jit(solution)/shard_map/ppermute | solution.py:15
  58.2 0.1 add_add_fusion
  58.3 0.6 copy-done
  58.8 0.6 %pad_maximum_fusion.2 = f32[6,32]{1,0:T(8,128)} fusion(f32[3,32]{1,0:T(4,128)S(1)} %multiply_add_fusion.2, f32[3,32]{1,0:T(4,128)S(1)} %multiply_subtract_fusion), kind=kLoop, calls=%fused_computation.178 | loop fusion | flops 192 | bytes 1536 | tf_op jit(solution)/shard_map/concatenate | solution.py:159
  (45 shorter events, 0.5 us)
Async XLA Ops:
  0.6 0.8 %copy-start.5 = (f32[256]{0:T(256)S(1)}, f32[256]{0:T(256)}, u32[]{:S(2)}) copy-start(f32[256]{0:T(256)} %param.17) | copy-start | bytes 3076
  2.1 0.7 %copy-start.6 = (f32[256]{0:T(256)S(1)}, f32[256]{0:T(256)}, u32[]{:S(2)}) copy-start(f32[256]{0:T(256)} %param.18) | copy-start | bytes 3076
  3.5 9.8 %copy-start.1 = (f32[3,256]{1,0:T(4,128)S(1)}, f32[3,256]{1,0:T(4,128)}, u32[]{:S(2)}) copy-start(f32[3,256]{1,0:T(4,128)} %param.13) | copy-start | bytes 9220
  3.5 9.8 %copy-start.2 = (f32[3,256]{1,0:T(4,128)S(1)}, f32[3,256]{1,0:T(4,128)}, u32[]{:S(2)}) copy-start(f32[3,256]{1,0:T(4,128)} %param.14) | copy-start | bytes 9220
  3.5 9.8 %copy-start.3 = (f32[3,256]{1,0:T(4,128)S(1)}, f32[3,256]{1,0:T(4,128)}, u32[]{:S(2)}) copy-start(f32[3,256]{1,0:T(4,128)} %param.16) | copy-start | bytes 9220
  3.5 9.8 %copy-start.4 = (f32[3,256]{1,0:T(4,128)S(1)}, f32[3,256]{1,0:T(4,128)}, u32[]{:S(2)}) copy-start(f32[3,256]{1,0:T(4,128)} %param.15) | copy-start | bytes 9220
  3.6 25.9 %all-to-all-start = ((f32[7,32,256]{2,0,1:T(8,128)}), f32[7,32,256]{2,0,1:T(8,128)S(1)}, u32[]{:S(2)}, u32[]{:S(2)}) async-start(f32[7,32,256]{2,0,1:T(8,128)} %broadcast_in_dim.42), calls=%async_computation | async-start | bytes 524288 | tf_op jit(solution)/shard_map/all_to_all | solution.py:34
  13.5 0.7 %copy-start.7 = (s32[32]{0:T(128)S(1)}, s32[32]{0:T(128)}, u32[]{:S(2)}) copy-start(s32[32]{0:T(128)} %param.19) | copy-start | bytes 388
  14.9 5.2 %collective-permute-start = (f32[6,32]{1,0:T(8,128)S(1)}, f32[6,32]{1,0:T(8,128)S(1)}, u32[]{:S(2)}, u32[]{:S(2)}) collective-permute-start(f32[6,32]{1,0:T(8,128)S(1)} %pad_maximum_fusion.1), channel_id=1, source_target_pairs={{0,32},{32,0},{64,96},{96,64},{128,160},{160,128},{192,224},{224,1... | collective-permute-start | bytes 2312 | tf_op jit(solution)/shard_map/ppermute | solution.py:15
  18.4 0.7 %copy-start.8 = (s32[1,64]{1,0:T(1,128)S(1)}, s32[1,64]{1,0:T(1,128)}, u32[]{:S(2)}) copy-start(s32[1,64]{1,0:T(1,128)} %param.20) | copy-start | bytes 772
  20.2 3.6 %collective-permute-start.1 = (f32[6,64]{1,0:T(8,128)S(1)}, f32[6,64]{1,0:T(8,128)S(1)}, u32[]{:S(2)}, u32[]{:S(2)}) collective-permute-start(f32[6,64]{1,0:T(8,128)S(1)} %maximum_select_fusion.1), channel_id=1, source_target_pairs={{0,64},{32,96},{64,0},{96,32},{128,192},{160,224},{192,128},{224,1... | collective-permute-start | bytes 4616 | tf_op jit(solution)/shard_map/ppermute | solution.py:15
  23.9 5.1 %collective-permute-start.2 = (f32[6,128]{1,0:T(8,128)S(1)}, f32[6,128]{1,0:T(8,128)S(1)}, u32[]{:S(2)}, u32[]{:S(2)}) collective-permute-start(f32[6,128]{1,0:T(8,128)S(1)} %maximum_select_fusion.2), channel_id=1, source_target_pairs={{0,128},{32,160},{64,192},{96,224},{128,0},{160,32},{192,64},{224,... | collective-permute-start | bytes 9224 | tf_op jit(solution)/shard_map/ppermute | solution.py:15
  38.6 10.5 %collective-permute-start.3 = (f32[6,128]{1,0:T(8,128)S(1)}, f32[6,128]{1,0:T(8,128)S(1)}, u32[]{:S(2)}, u32[]{:S(2)}) collective-permute-start(f32[6,128]{1,0:T(8,128)S(1)} %reshape.117), channel_id=1, source_target_pairs={{0,128},{32,160},{64,192},{96,224},{128,0},{160,32},{192,64},{224,... | collective-permute-start | bytes 9224 | tf_op jit(solution)/shard_map/ppermute | solution.py:15
  49.1 3.8 %collective-permute-start.4 = (f32[6,64]{1,0:T(8,128)S(1)}, f32[6,64]{1,0:T(8,128)S(1)}, u32[]{:S(2)}, u32[]{:S(2)}) collective-permute-start(f32[6,64]{1,0:T(8,128)S(1)} %dynamic-slice_add_fusion.1), channel_id=1, source_target_pairs={{0,64},{32,96},{64,0},{96,32},{128,192},{160,224},{192,128},{224,1... | collective-permute-start | bytes 4616 | tf_op jit(solution)/shard_map/ppermute | solution.py:15
  53.0 5.1 %collective-permute-start.5 = (f32[6,32]{1,0:T(8,128)S(1)}, f32[6,32]{1,0:T(8,128)S(1)}, u32[]{:S(2)}, u32[]{:S(2)}) collective-permute-start(f32[6,32]{1,0:T(8,128)S(1)} %dynamic-slice_add_fusion), channel_id=1, source_target_pairs={{0,32},{32,0},{64,96},{96,64},{128,160},{160,128},{192,224},{224,1... | collective-permute-start | bytes 2312 | tf_op jit(solution)/shard_map/ppermute | solution.py:15
  58.2 0.6 copy-start

commit v8 on v7

--- a/solution.py
+++ b/solution.py
@@ -83,15 +83,12 @@
     neighbour_list,
     neighbour_count,
 ):
-    def predict(pos, vel, acc, jerk, time):
-        moved_pos = pos + time * (vel + time * (0.5 * acc + time * jerk / 6.0))
-        turned = vel + time * (acc + 0.5 * time * jerk)
-        return jnp.concatenate([moved_pos, turned], axis=0)
-
-    raw = jnp.concatenate([position, velocity, accel_old, jerk_old, elapsed[None, :]], axis=0)
-    raw_act = raw.at[:, active_stars].get(mode="promise_in_bounds")
-    own_set = predict(raw_act[0:3], raw_act[3:6], raw_act[6:9], raw_act[9:12], raw_act[12])
-    sources = predict(position, velocity, accel_old, jerk_old, elapsed)
+    moved_pos = position + elapsed * (
+        velocity + elapsed * (0.5 * accel_old + elapsed * jerk_old / 6.0)
+    )
+    turned = velocity + elapsed * (accel_old + 0.5 * elapsed * jerk_old)
+    sources = jnp.concatenate([moved_pos, turned], axis=0)
+    own_set = jnp.take(sources, active_stars, axis=1)
     act_dev = active_stars.shape[0]
     block_data = jnp.concatenate([sources, masses[None, :]], axis=0)
     targets = gather_doubling(own_set, "blk")
@@ -112,11 +109,7 @@
 
     def owner_sums(start, count):
         pieces = lax.dynamic_slice_in_dim(targets, start * act_dev, count * act_dev, 1)
-        if count == 1:
-            return pair_sums(pieces, group_src, weight)
-        pieces = pieces.reshape(6, count, act_dev).transpose(1, 0, 2)
-        sums = lax.map(lambda piece: pair_sums(piece, group_src, weight), pieces)
-        return sums.transpose(1, 0, 2).reshape(6, count * act_dev)
+        return pair_sums(pieces, group_src, weight)
 
     def owner_cols(block, owner, span):
         return lax.dynamic_slice_in_dim(block, (owner % span) * act_dev, act_dev, 1)
@@ -150,9 +143,9 @@
     )
     accel_now = regular[:3] + irregular[:3]
     jerk_now = regular[3:] + irregular[3:]
-    step_time = raw_act[12]
-    start_accel = raw_act[6:9]
-    start_jerk = raw_act[9:12]
+    step_time = jnp.take(elapsed, active_stars)
+    start_accel = jnp.take(accel_old, active_stars, axis=1)
+    start_jerk = jnp.take(jerk_old, active_stars, axis=1)
     change = start_accel - accel_now
     snap_term = -6.0 * change - step_time * (4.0 * start_jerk + 2.0 * jerk_now)
     crackle_term = 12.0 * change + 6.0 * step_time * (start_jerk + jerk_now)

time: 60.2 us -> 55.7 us (0.925)
  other arithmetic: 19.3 us -> 18 us
  starting transfers between devices: 24.3 us -> 23 us
  local copies, waits for them, and re-layouts: 6.57 us -> 5.28 us
    unnamed x18 -> x20, local copies, waits for them, and re-layouts: 2.45 us -> 0.32 us
    gather x2 -> x6, local copies, waits for them, and re-layouts: 0.65 us -> 2.59 us  [the longest x1 0.71 us: per_device(): step_time = jnp.take(elapsed, active_stars)]
    ppermute x6, waiting for transfers between devices: 7.56 us -> 5.73 us  [exchange(): return lax.ppermute(block, axis, [(i, i ^ bit) for i in range(size)])]
    all_to_all x1, waiting for transfers between devices: 0.01 us -> 1.66 us  [gather_all_to_all(): got = lax.all_to_all(spread, axis, 1, 1, tiled=True)]
    reduce_sum x7 -> x3, other arithmetic: 13.9 us -> 12.6 us  [pair_sums(): return jnp.stack([jnp.sum(scaled * term, axis=1) for term in term_list])]
    all_to_all x1, starting transfers between devices: 9.8 us -> 8.89 us  [gather_all_to_all(): got = lax.all_to_all(spread, axis, 1, 1, tiled=True)]
    slice x7 -> x1, local copies, waits for them, and re-layouts: 0.99 us -> 0.16 us  [pair_terms(): rel_x = sources[3][None, :] - targets[3][:, None]]
    add x2 -> x1, other arithmetic: 0.76 us -> 0.01 us  [per_device(): position + elapsed * (velocity + elapsed * (0.5 * accel_old + elapsed * j...]
  transfers between devices with their start and end apart: 7 -> 7, of which waited for: 5 -> 5; matrix products, arithmetic and copies ran while one was open for 19% -> 22% of each run, Pallas kernels for 0% -> 0%
where the time goes in v8:
time: 55.7 us; the launch traced here: 55.2 us
  starting transfers between devices  23 us (41%)
  other arithmetic  18 us (32%)
  waiting for transfers between devices  7.39 us (13%)
  local copies, waits for them, and re-layouts  5.28 us (9%)
  between operations  1.59 us (3%)
    ppermute x6, starting transfers between devices, exchange(): return lax.ppermute(block, axis, [(i, i ^ bit) for i in range(size)])  14.1 us
    reduce_sum x3, other arithmetic, pair_sums(): return jnp.stack([jnp.sum(scaled * term, axis=1) for term in term_list])  12.6 us
    all_to_all x1, starting transfers between devices, gather_all_to_all(): got = lax.all_to_all(spread, axis, 1, 1, tiled=True)  8.89 us
    ppermute x6, waiting for transfers between devices, exchange(): return lax.ppermute(block, axis, [(i, i ^ bit) for i in range(size)])  5.73 us
    reduce_sum x1, other arithmetic, pair_sums_split(): jnp.sum(near_scaled * term, axis=1)  2.66 us
    all_to_all x1, waiting for transfers between devices, gather_all_to_all(): got = lax.all_to_all(spread, axis, 1, 1, tiled=True)  1.66 us
  transfers between devices with their start and end apart: 7, of which 5 were waited for; matrix products, arithmetic and copies ran while one was open for 22% of the time, Pallas kernels for 0%

profile of v8, /device:TPU:32, one launch (start us, length us, event | category | flops | bytes accessed | tf_op | source)
XLA Modules:
  0.0 55.2 jit_solution(8476741648719127992)
XLA Ops:
  0.6 0.0 copy-start
  0.6 0.7 %compare_select_fusion = s32[32]{0:T(128)S(1)} fusion(s32[32]{0:T(128)} %param.17), kind=kLoop, calls=%fused_computation.168 | loop fusion | flops 96 | bytes 256 | tf_op jit(solution)/shard_map/jit(_take)/jit(_where)/select_n | solution.py:91
  1.3 0.7 %broadcast_multiply_fusion = f32[256]{0:T(256)S(1)} fusion(f32[256]{0:T(256)} %param.15), kind=kLoop, calls=%fused_computation.202 | loop fusion | flops 256 | bytes 2048 | tf_op jit(solution)/shard_map/mul | solution.py:89
  2.0 0.0 copy-done
  2.0 0.0 copy-start.7
  2.0 0.0 copy-start.2
  2.0 0.0 copy-start.3
  2.0 0.0 copy-start.4
  2.0 0.0 copy-start.5
  2.1 0.7 %gather_fusion.1 = f32[32]{0:T(128)S(1)} fusion(f32[256]{0:T(256)S(1)} %copy-done, s32[1024]{0:T(1024)S(1)} %pad_clamp_fusion), kind=kCustom, calls=%fused_computation.3 | custom fusion | bytes 384 | tf_op jit(solution)/shard_map/jit(_take)/gather | solution.py:146
  2.8 0.0 copy-done.7
  2.8 0.0 copy-start.6
  2.8 0.0 copy-done.2
  2.8 0.0 copy-done.3
  2.8 0.0 copy-done.4
  2.8 0.0 copy-done.5
  2.9 0.1 copy.137
  3.0 0.6 %gather_fusion = f32[32,6]{1,0:T(8,128)S(1)} fusion(f32[6,256]{0,1:T(8,128)S(1)} %copy.137, s32[1024]{0:T(1024)S(1)} %pad_clamp_fusion), kind=kCustom, calls=%fused_computation.2 | custom fusion | bytes 1664 | tf_op jit(solution)/shard_map/jit(_take)/gather | solution.py:91
  3.6 0.1 select_bitcast_fusion
  3.7 3.0 %collective-permute-start = (f32[6,32]{0,1:T(8,128)S(1)}, f32[6,32]{0,1:T(8,128)S(1)}, u32[]{:S(2)}, u32[]{:S(2)}) collective-permute-start(f32[6,32]{0,1:T(8,128)S(1)} %select_bitcast_fusion), channel_id=1, source_target_pairs={{0,32},{32,0},{64,96},{96,64},{128,160},{160,128},{192,224},{224,1... | collective-permute-start | bytes 2312 | tf_op jit(solution)/shard_map/ppermute | solution.py:15
  6.7 0.0 copy-done.6
  6.7 0.7 %broadcast_in_dim.49 = f32[7,32,256]{2,0,1:T(8,128)} broadcast(f32[7,256]{1,0:T(8,128)S(1)} %pad_maximum_fusion), dimensions={0,2} | broadcast | bytes 236544 | tf_op jit(solution)/shard_map/broadcast_in_dim | solution.py:33
  7.4 0.0 copy-start.8
  7.4 8.9 %all-to-all-start = ((f32[7,32,256]{2,0,1:T(8,128)}), f32[7,32,256]{2,0,1:T(8,128)S(1)}, u32[]{:S(2)}, u32[]{:S(2)}) async-start(f32[7,32,256]{2,0,1:T(8,128)} %broadcast_in_dim.49), calls=%async_computation | async-start | bytes 524288 | tf_op jit(solution)/shard_map/all_to_all | solution.py:34
  16.4 0.3 slice_reduce_fusion.1
  17.3 0.0 copy-done.8
  17.3 0.1 fusion.68
  17.5 0.1 copy.139
  17.5 0.0 collective-permute-done
  17.5 0.1 copy.138
  17.6 0.1 maximum_select_fusion.1
  17.7 1.6 %collective-permute-start.1 = (f32[6,64]{1,0:T(8,128)S(1)}, f32[6,64]{1,0:T(8,128)S(1)}, u32[]{:S(2)}, u32[]{:S(2)}) collective-permute-start(f32[6,64]{1,0:T(8,128)S(1)} %maximum_select_fusion.1), channel_id=1, source_target_pairs={{0,64},{32,96},{64,0},{96,32},{128,192},{160,224},{192,128},{224,1... | collective-permute-start | bytes 4616 | tf_op jit(solution)/shard_map/ppermute | solution.py:15
  19.3 2.0 %collective-permute-done.1 = f32[6,64]{1,0:T(8,128)S(1)} collective-permute-done((f32[6,64]{1,0:T(8,128)S(1)}, f32[6,64]{1,0:T(8,128)S(1)}, u32[]{:S(2)}, u32[]{:S(2)}) %collective-permute-start.1) | collective-permute-done | bytes 1568 | tf_op jit(solution)/shard_map/ppermute | solution.py:15
  21.3 0.1 maximum_select_fusion.2
  21.4 3.2 %collective-permute-start.2 = (f32[6,128]{1,0:T(8,128)S(1)}, f32[6,128]{1,0:T(8,128)S(1)}, u32[]{:S(2)}, u32[]{:S(2)}) collective-permute-start(f32[6,128]{1,0:T(8,128)S(1)} %maximum_select_fusion.2), channel_id=1, source_target_pairs={{0,128},{32,160},{64,192},{96,224},{128,0},{160,32},{192,64},{224,... | collective-permute-start | bytes 9224 | tf_op jit(solution)/shard_map/ppermute | solution.py:15
  24.6 0.1 copy.142
  24.8 0.1 copy.144
  24.9 0.6 %gather_fusion.2 = f32[32,3]{1,0:T(8,128)S(1)} fusion(f32[3,256]{0,1:T(8,128)S(1)} %copy.142, s32[1024]{0:T(1024)S(1)} %pad_clamp_fusion), kind=kCustom, calls=%fused_computation.clone | custom fusion | bytes 896 | tf_op jit(solution)/shard_map/jit(_take)/gather | solution.py:147
  25.5 0.1 copy.143
  25.6 0.6 %gather_fusion.3 = f32[32,3]{1,0:T(8,128)S(1)} fusion(f32[3,256]{0,1:T(8,128)S(1)} %copy.144, s32[1024]{0:T(1024)S(1)} %pad_clamp_fusion), kind=kCustom, calls=%fused_computation.1.clone | custom fusion | bytes 896 | tf_op jit(solution)/shard_map/jit(_take)/gather | solution.py:148
  26.2 0.1 copy.145
  26.2 0.3 collective-permute-done.2
  26.5 0.1 constant_dynamic-slice_fusion
  26.6 0.1 constant_dynamic-slice_fusion.1
  26.7 0.1 constant_dynamic-slice_fusion.2
  26.8 1.7 %all-to-all-done = f32[7,32,256]{2,0,1:T(8,128)S(1)} async-done(((f32[7,32,256]{2,0,1:T(8,128)}), f32[7,32,256]{2,0,1:T(8,128)S(1)}, u32[]{:S(2)}, u32[]{:S(2)}) %all-to-all-start) | async-done | bytes 229408 | tf_op jit(solution)/shard_map/all_to_all | solution.py:34
  28.4 0.2 fusion.75
  28.6 7.2 %fusion.5 = (f32[128]{0:T(128)S(1)}, f32[128]{0:T(128)S(1)}, f32[128]{0:T(128)S(1)}, f32[128]{0:T(128)S(1)}, f32[128]{0:T(128)S(1)}, /*index=5*/f32[128]{0:T(128)S(1)}) fusion(f32[128]{0:T(128)S(1)} %get-tuple-element.76, f32[8192]{0:T(1024)S(1)} %bitcast.111, f32[128]{0:T(128)S(1)} %get-tuple-element.78, f32[8192]{0:T(1024)S(1)} %bitcast.119, ...), kind=kLoop, calls=%fused_computation.37 | loop fusion | flops 41942272 | bytes 235520 | tf_op jit(solution)/shard_map/reduce_sum | solution.py:63
  35.9 3.3 %collective-permute-start.3 = (f32[6,128]{1,0:T(8,128)S(1)}, f32[6,128]{1,0:T(8,128)S(1)}, u32[]{:S(2)}, u32[]{:S(2)}) collective-permute-start(f32[6,128]{1,0:T(8,128)S(1)} %stack.122), channel_id=1, source_target_pairs={{0,128},{32,160},{64,192},{96,224},{128,0},{160,32},{192,64},{224,... | collective-permute-start | bytes 9224 | tf_op jit(solution)/shard_map/ppermute | solution.py:15
  39.1 0.1 fusion.66
  39.2 3.4 %fusion.22 = (f32[64]{0:T(128)S(1)}, f32[64]{0:T(128)S(1)}, f32[64]{0:T(128)S(1)}, f32[64]{0:T(128)S(1)}, f32[64]{0:T(128)S(1)}, /*index=5*/f32[64]{0:T(128)S(1)}) fusion(f32[64]{0:T(128)S(1)} %get-tuple-element.82, f32[8192]{0:T(1024)S(1)} %bitcast.112, f32[64]{0:T(128)S(1)} %get-tuple-element.84, f32[8192]{0:T(1024)S(1)} %bitcast.120, ...), kind=kLoop, calls=%fused_computation.85 | loop fusion | flops 20971136 | bytes 232448 | tf_op jit(solution)/shard_map/reduce_sum | solution.py:63
  42.7 2.7 %multiply_reduce_fusion = (f32[32]{0:T(128)S(1)}, f32[32]{0:T(128)S(1)}, f32[32]{0:T(128)S(1)}, f32[32]{0:T(128)S(1)}, f32[32]{0:T(128)S(1)}, /*index=5*/f32[32]...) fusion(f32[32]{0:T(128)S(1)} %get-tuple-element.50, ...), kind=kLoop, calls=%fused_computation.135 | loop fusion | flops 13893248 | bytes 264448 | tf_op jit(solution)/shard_map/reduce_sum | solution.py:71
  45.4 0.0 collective-permute-done.3
  45.4 0.1 dynamic-slice_add_fusion.1
  45.4 0.9 %collective-permute-start.4 = (f32[6,64]{1,0:T(8,128)S(1)}, f32[6,64]{1,0:T(8,128)S(1)}, u32[]{:S(2)}, u32[]{:S(2)}) collective-permute-start(f32[6,64]{1,0:T(8,128)S(1)} %dynamic-slice_add_fusion.1), channel_id=1, source_target_pairs={{0,64},{32,96},{64,0},{96,32},{128,192},{160,224},{192,128},{224,1... | collective-permute-start | bytes 4616 | tf_op jit(solution)/shard_map/ppermute | solution.py:15
  46.3 2.0 %fusion.39 = (f32[32]{0:T(128)S(1)}, f32[32]{0:T(128)S(1)}, f32[32]{0:T(128)S(1)}, f32[32]{0:T(128)S(1)}, f32[32]{0:T(128)S(1)}, /*index=5*/f32[32]{0:T(128)S(1)}) fusion(f32[32]{0:T(128)S(1)} %get-tuple-element.70, f32[32]{0:T(128)S(1)} %get-tuple-element.72, f32[8192]{0:T(1024)S(1)} %bitcast.114, f32[8192]{0:T(1024)S(1)} %bitcast.122, ...), kind=kLoop, calls=%fused_computation.110 | loop fusion | flops 10485568 | bytes 230912 | tf_op jit(solution)/shard_map/reduce_sum | solution.py:63
  48.3 0.9 %collective-permute-done.4 = f32[6,64]{1,0:T(8,128)S(1)} collective-permute-done((f32[6,64]{1,0:T(8,128)S(1)}, f32[6,64]{1,0:T(8,128)S(1)}, u32[]{:S(2)}, u32[]{:S(2)}) %collective-permute-start.4) | collective-permute-done | bytes 1568 | tf_op jit(solution)/shard_map/ppermute | solution.py:15
  49.3 0.1 dynamic-slice_add_fusion
  49.3 2.0 %collective-permute-start.5 = (f32[6,32]{1,0:T(8,128)S(1)}, f32[6,32]{1,0:T(8,128)S(1)}, u32[]{:S(2)}, u32[]{:S(2)}) collective-permute-start(f32[6,32]{1,0:T(8,128)S(1)} %dynamic-slice_add_fusion), channel_id=1, source_target_pairs={{0,32},{32,0},{64,96},{96,64},{128,160},{160,128},{192,224},{224,1... | collective-permute-start | bytes 2312 | tf_op jit(solution)/shard_map/ppermute | solution.py:15
  51.4 0.6 %stack.143 = f32[6,32]{1,0:T(8,128)} concatenate(f32[1,32]{1,0:T(1,128)S(1)} %bitcast.146, f32[1,32]{1,0:T(1,128)S(1)} %bitcast.140, f32[1,32]{1,0:T(1,128)S(1)} %bitcast.143, f32[1,32]{1,0:T(1,128)S(1)} %bitcast.134, f32[1,32]{1,0:T(1,128)S(1)} %bitcast.137, f32[1,32]{1,0:T(1,128)S(1)} %bitcast.131), dimensions={0} | concatenate | bytes 1536 | tf_op jit(solution)/shard_map/stack | solution.py:71
  52.0 2.5 %collective-permute-done.5 = f32[6,32]{1,0:T(8,128)S(1)} collective-permute-done((f32[6,32]{1,0:T(8,128)S(1)}, f32[6,32]{1,0:T(8,128)S(1)}, u32[]{:S(2)}, u32[]{:S(2)}) %collective-permute-start.5) | collective-permute-done | bytes 800 | tf_op jit(solution)/shard_map/ppermute | solution.py:15
  54.5 0.1 add_add_fusion
  54.6 0.6 %pad_maximum_fusion.2 = f32[6,32]{1,0:T(8,128)} fusion(f32[3,32]{1,0:T(4,128)S(1)} %fusion.74, f32[3,32]{1,0:T(4,128)S(1)} %fusion.72), kind=kLoop, calls=%fused_computation.162 | loop fusion | flops 192 | bytes 1536 | tf_op jit(solution)/shard_map/concatenate | solution.py:152
  55.2 0.0 copy-done.1
  (18 shorter events, 0.2 us)
Async XLA Ops:
  0.6 1.4 %copy-start = (f32[256]{0:T(256)S(1)}, f32[256]{0:T(256)}, u32[]{:S(2)}) copy-start(f32[256]{0:T(256)} %param.15) | copy-start | bytes 3076
  2.0 0.8 %copy-start.7 = (s32[32]{0:T(128)S(1)}, s32[32]{0:T(128)}, u32[]{:S(2)}) copy-start(s32[32]{0:T(128)} %param.17) | copy-start | bytes 388
  2.0 0.8 %copy-start.2 = (f32[3,256]{1,0:T(4,128)S(1)}, f32[3,256]{1,0:T(4,128)}, u32[]{:S(2)}) copy-start(f32[3,256]{1,0:T(4,128)} %param.13) | copy-start | bytes 9220
  2.0 0.8 %copy-start.3 = (f32[3,256]{1,0:T(4,128)S(1)}, f32[3,256]{1,0:T(4,128)}, u32[]{:S(2)}) copy-start(f32[3,256]{1,0:T(4,128)} %param.14) | copy-start | bytes 9220
  2.0 0.8 %copy-start.4 = (f32[3,256]{1,0:T(4,128)S(1)}, f32[3,256]{1,0:T(4,128)}, u32[]{:S(2)}) copy-start(f32[3,256]{1,0:T(4,128)} %param.11) | copy-start | bytes 9220
  2.0 0.8 %copy-start.5 = (f32[3,256]{1,0:T(4,128)S(1)}, f32[3,256]{1,0:T(4,128)}, u32[]{:S(2)}) copy-start(f32[3,256]{1,0:T(4,128)} %param.12) | copy-start | bytes 9220
  2.8 3.9 %copy-start.6 = (f32[256]{0:T(256)S(1)}, f32[256]{0:T(256)}, u32[]{:S(2)}) copy-start(f32[256]{0:T(256)} %param.16) | copy-start | bytes 3076
  3.7 13.9 %collective-permute-start = (f32[6,32]{0,1:T(8,128)S(1)}, f32[6,32]{0,1:T(8,128)S(1)}, u32[]{:S(2)}, u32[]{:S(2)}) collective-permute-start(f32[6,32]{0,1:T(8,128)S(1)} %select_bitcast_fusion), channel_id=1, source_target_pairs={{0,32},{32,0},{64,96},{96,64},{128,160},{160,128},{192,224},{224,1... | collective-permute-start | bytes 2312 | tf_op jit(solution)/shard_map/ppermute | solution.py:15
  7.4 9.9 %copy-start.8 = (s32[1,64]{1,0:T(1,128)S(1)}, s32[1,64]{1,0:T(1,128)}, u32[]{:S(2)}) copy-start(s32[1,64]{1,0:T(1,128)} %param.18) | copy-start | bytes 772
  7.4 21.0 %all-to-all-start = ((f32[7,32,256]{2,0,1:T(8,128)}), f32[7,32,256]{2,0,1:T(8,128)S(1)}, u32[]{:S(2)}, u32[]{:S(2)}) async-start(f32[7,32,256]{2,0,1:T(8,128)} %broadcast_in_dim.49), calls=%async_computation | async-start | bytes 524288 | tf_op jit(solution)/shard_map/all_to_all | solution.py:34
  17.7 3.6 %collective-permute-start.1 = (f32[6,64]{1,0:T(8,128)S(1)}, f32[6,64]{1,0:T(8,128)S(1)}, u32[]{:S(2)}, u32[]{:S(2)}) collective-permute-start(f32[6,64]{1,0:T(8,128)S(1)} %maximum_select_fusion.1), channel_id=1, source_target_pairs={{0,64},{32,96},{64,0},{96,32},{128,192},{160,224},{192,128},{224,1... | collective-permute-start | bytes 4616 | tf_op jit(solution)/shard_map/ppermute | solution.py:15
  21.4 5.1 %collective-permute-start.2 = (f32[6,128]{1,0:T(8,128)S(1)}, f32[6,128]{1,0:T(8,128)S(1)}, u32[]{:S(2)}, u32[]{:S(2)}) collective-permute-start(f32[6,128]{1,0:T(8,128)S(1)} %maximum_select_fusion.2), channel_id=1, source_target_pairs={{0,128},{32,160},{64,192},{96,224},{128,0},{160,32},{192,64},{224,... | collective-permute-start | bytes 9224 | tf_op jit(solution)/shard_map/ppermute | solution.py:15
  35.9 9.5 %collective-permute-start.3 = (f32[6,128]{1,0:T(8,128)S(1)}, f32[6,128]{1,0:T(8,128)S(1)}, u32[]{:S(2)}, u32[]{:S(2)}) collective-permute-start(f32[6,128]{1,0:T(8,128)S(1)} %stack.122), channel_id=1, source_target_pairs={{0,128},{32,160},{64,192},{96,224},{128,0},{160,32},{192,64},{224,... | collective-permute-start | bytes 9224 | tf_op jit(solution)/shard_map/ppermute | solution.py:15
  45.4 3.8 %collective-permute-start.4 = (f32[6,64]{1,0:T(8,128)S(1)}, f32[6,64]{1,0:T(8,128)S(1)}, u32[]{:S(2)}, u32[]{:S(2)}) collective-permute-start(f32[6,64]{1,0:T(8,128)S(1)} %dynamic-slice_add_fusion.1), channel_id=1, source_target_pairs={{0,64},{32,96},{64,0},{96,32},{128,192},{160,224},{192,128},{224,1... | collective-permute-start | bytes 4616 | tf_op jit(solution)/shard_map/ppermute | solution.py:15
  49.3 5.1 %collective-permute-start.5 = (f32[6,32]{1,0:T(8,128)S(1)}, f32[6,32]{1,0:T(8,128)S(1)}, u32[]{:S(2)}, u32[]{:S(2)}) collective-permute-start(f32[6,32]{1,0:T(8,128)S(1)} %dynamic-slice_add_fusion), channel_id=1, source_target_pairs={{0,32},{32,0},{64,96},{96,64},{128,160},{160,128},{192,224},{224,1... | collective-permute-start | bytes 2312 | tf_op jit(solution)/shard_map/ppermute | solution.py:15
  54.5 0.6 %copy-start.1 = (f32[6,32]{1,0:T(8,128)}, f32[6,32]{1,0:T(8,128)S(1)}, u32[]{:S(2)}) copy-start(f32[6,32]{1,0:T(8,128)S(1)} %add_add_fusion) | copy-start | bytes 2308

commit v9 on v8

--- a/solution.py
+++ b/solution.py
@@ -88,7 +88,8 @@
     )
     turned = velocity + elapsed * (accel_old + 0.5 * elapsed * jerk_old)
     sources = jnp.concatenate([moved_pos, turned], axis=0)
-    own_set = jnp.take(sources, active_stars, axis=1)
+    picks = (active_stars[None, :] == jnp.arange(sources.shape[1])[:, None]).astype(jnp.float32)
+    own_set = jnp.dot(sources, picks, precision=lax.Precision.HIGHEST)
     act_dev = active_stars.shape[0]
     block_data = jnp.concatenate([sources, masses[None, :]], axis=0)
     targets = gather_doubling(own_set, "blk")
@@ -143,9 +144,9 @@
     )
     accel_now = regular[:3] + irregular[:3]
     jerk_now = regular[3:] + irregular[3:]
-    step_time = jnp.take(elapsed, active_stars)
-    start_accel = jnp.take(accel_old, active_stars, axis=1)
-    start_jerk = jnp.take(jerk_old, active_stars, axis=1)
+    step_time = elapsed.at[active_stars].get(mode="promise_in_bounds")
+    start_accel = accel_old.at[:, active_stars].get(mode="promise_in_bounds")
+    start_jerk = jerk_old.at[:, active_stars].get(mode="promise_in_bounds")
     change = start_accel - accel_now
     snap_term = -6.0 * change - step_time * (4.0 * start_jerk + 2.0 * jerk_now)
     crackle_term = 12.0 * change + 6.0 * step_time * (start_jerk + jerk_now)

time: 55.7 us -> 55.4 us (level)
  waiting for transfers between devices: 7.39 us -> 5.74 us
  starting transfers between devices: 23 us -> 24.3 us
  local copies, waits for them, and re-layouts: 5.28 us -> 4.13 us
  other arithmetic: 18 us -> 18.9 us
    all_to_all x1, waiting for transfers between devices: 1.66 us -> 0.01 us  [gather_all_to_all(): got = lax.all_to_all(spread, axis, 1, 1, tiled=True)]
    all_to_all x1, starting transfers between devices: 8.89 us -> 9.78 us  [gather_all_to_all(): got = lax.all_to_all(spread, axis, 1, 1, tiled=True)]
    add x1, other arithmetic: 0.01 us -> 0.75 us  [per_device(): position + elapsed * (velocity + elapsed * (0.5 * accel_old + elapsed * j...]
    select_n x2 -> x1, other arithmetic: 0.74 us -> 0.01 us  [per_device(): start_accel = accel_old.at[:, active_stars].get(mode='promise_in_bounds')]
    concatenate x1, other arithmetic: 0.01 us -> 0.69 us  [per_device(): block_data = jnp.concatenate([sources, masses[None, :]], axis=0)]
    gather x6 -> x5, local copies, waits for them, and re-layouts: 2.59 us -> 2.02 us  [the longest x1 0.71 us: per_device(): step_time = elapsed.at[active_stars].get(mode='promise_in_bounds')]
where the time goes in v9:
time: 55.4 us; the launch traced here: 54.7 us
  starting transfers between devices  24.3 us (44%)
  other arithmetic  18.9 us (34%)
  waiting for transfers between devices  5.74 us (10%)
  local copies, waits for them, and re-layouts  4.13 us (7%)
  between operations  1.5 us (3%)
    ppermute x6, starting transfers between devices, exchange(): return lax.ppermute(block, axis, [(i, i ^ bit) for i in range(size)])  14.5 us
    reduce_sum x3, other arithmetic, pair_sums(): return jnp.stack([jnp.sum(scaled * term, axis=1) for term in term_list])  12.8 us
    all_to_all x1, starting transfers between devices, gather_all_to_all(): got = lax.all_to_all(spread, axis, 1, 1, tiled=True)  9.78 us
    ppermute x6, waiting for transfers between devices, exchange(): return lax.ppermute(block, axis, [(i, i ^ bit) for i in range(size)])  5.74 us
    reduce_sum x1, other arithmetic, pair_sums_split(): jnp.sum(near_scaled * term, axis=1)  2.71 us
  transfers between devices with their start and end apart: 7, of which 5 were waited for; matrix products, arithmetic and copies ran while one was open for 22% of the time, Pallas kernels for 0%

profile of v9, /device:TPU:32, one launch (start us, length us, event | category | flops | bytes accessed | tf_op | source)
XLA Modules:
  0.0 54.7 jit_solution(10304963717842223477)
XLA Ops:
  0.6 0.7 %broadcast_multiply_fusion = f32[256]{0:T(256)S(1)} fusion(f32[256]{0:T(256)} %param.13), kind=kLoop, calls=%fused_computation.204 | loop fusion | flops 256 | bytes 2048 | tf_op jit(solution)/shard_map/mul | solution.py:89
  1.3 0.8 %multiply_add_fusion.1 = (f32[3,256]{1,0:T(4,128)S(1)}, f32[3,256]{1,0:T(4,128)S(1)}) fusion(f32[3,256]{1,0:T(4,128)} %param.9, f32[3,256]{1,0:T(4,128)} %param.10, f32[3,256]{1,0:T(4,128)} %param.12, f32[3,256]{1,0:T(4,128)} %param.11, f32[256]{0:T(256)} %param.13, f32[256]{0:T(256)S(1)} %broadcast_multiply_fusion), kind=kLoop, calls=%fused_computation.164 | loop fusion | flops 9216 | bytes 20480 | tf_op jit(solution)/shard_map/add | solution.py:86
  2.1 0.7 %pad_maximum_fusion = f32[7,256]{1,0:T(8,128)S(1)} fusion(f32[1,256]{1,0:T(1,128)} %bitcast.159, f32[3,256]{1,0:T(4,128)S(1)} %get-tuple-element.58, f32[3,256]{1,0:T(4,128)S(1)} %get-tuple-element.57), kind=kLoop, calls=%fused_computation.151 | loop fusion | flops 3584 | bytes 14336 | tf_op jit(solution)/shard_map/concatenate | solution.py:94
  2.8 0.7 %broadcast_in_dim.9 = f32[7,32,256]{2,0,1:T(8,128)} broadcast(f32[7,256]{1,0:T(8,128)S(1)} %pad_maximum_fusion), dimensions={0,2} | broadcast | bytes 236544 | tf_op jit(solution)/shard_map/broadcast_in_dim | solution.py:33
  3.5 0.0 copy-start.4
  3.5 0.0 copy-start
  3.5 9.8 %all-to-all-start = ((f32[7,32,256]{2,0,1:T(8,128)}), f32[7,32,256]{2,0,1:T(8,128)S(1)}, u32[]{:S(2)}, u32[]{:S(2)}) async-start(f32[7,32,256]{2,0,1:T(8,128)} %broadcast_in_dim.9), calls=%async_computation | async-start | bytes 524288 | tf_op jit(solution)/shard_map/all_to_all | solution.py:34
  13.3 0.0 copy-done.4
  13.3 0.2 fusion.66
  13.4 2.7 %collective-permute-start = (f32[6,32]{1,0:T(8,128)S(1)}, f32[6,32]{1,0:T(8,128)S(1)}, u32[]{:S(2)}, u32[]{:S(2)}) collective-permute-start(f32[6,32]{1,0:T(8,128)S(1)} %fusion.66), channel_id=1, source_target_pairs={{0,32},{32,0},{64,96},{96,64},{128,160},{160,128},{192,224},{224,1... | collective-permute-start | bytes 2312 | tf_op jit(solution)/shard_map/ppermute | solution.py:15
  16.9 0.0 copy-done
  16.9 0.0 copy-start.5
  16.9 0.0 copy-start.2
  16.9 0.7 %gather_fusion.1 = f32[32]{0:T(128)S(1)} fusion(f32[256]{0:T(256)S(1)} %copy-done, s32[1024]{0:T(1024)S(1)} %pad_clamp_fusion), kind=kCustom, calls=%fused_computation.1 | custom fusion | bytes 384 | tf_op jit(solution)/shard_map/gather | solution.py:147
  17.6 0.0 copy-start.3
  17.6 0.0 copy-done.5
  17.6 0.1 fusion.70
  17.8 0.8 %collective-permute-done = f32[6,32]{1,0:T(8,128)S(1)} collective-permute-done((f32[6,32]{1,0:T(8,128)S(1)}, f32[6,32]{1,0:T(8,128)S(1)}, u32[]{:S(2)}, u32[]{:S(2)}) %collective-permute-start) | collective-permute-done | bytes 800 | tf_op jit(solution)/shard_map/ppermute | solution.py:15
  18.6 0.1 maximum_select_fusion.1
  18.6 1.6 %collective-permute-start.1 = (f32[6,64]{1,0:T(8,128)S(1)}, f32[6,64]{1,0:T(8,128)S(1)}, u32[]{:S(2)}, u32[]{:S(2)}) collective-permute-start(f32[6,64]{1,0:T(8,128)S(1)} %maximum_select_fusion.1), channel_id=1, source_target_pairs={{0,64},{32,96},{64,0},{96,32},{128,192},{160,224},{192,128},{224,1... | collective-permute-start | bytes 4616 | tf_op jit(solution)/shard_map/ppermute | solution.py:15
  20.2 2.0 %collective-permute-done.1 = f32[6,64]{1,0:T(8,128)S(1)} collective-permute-done((f32[6,64]{1,0:T(8,128)S(1)}, f32[6,64]{1,0:T(8,128)S(1)}, u32[]{:S(2)}, u32[]{:S(2)}) %collective-permute-start.1) | collective-permute-done | bytes 1568 | tf_op jit(solution)/shard_map/ppermute | solution.py:15
  22.3 0.1 maximum_select_fusion.2
  22.3 3.2 %collective-permute-start.2 = (f32[6,128]{1,0:T(8,128)S(1)}, f32[6,128]{1,0:T(8,128)S(1)}, u32[]{:S(2)}, u32[]{:S(2)}) collective-permute-start(f32[6,128]{1,0:T(8,128)S(1)} %maximum_select_fusion.2), channel_id=1, source_target_pairs={{0,128},{32,160},{64,192},{96,224},{128,0},{160,32},{192,64},{224,... | collective-permute-start | bytes 9224 | tf_op jit(solution)/shard_map/ppermute | solution.py:15
  25.6 0.0 copy-done.2
  25.6 0.1 copy.102
  25.7 0.0 copy-done.3
  25.7 0.1 copy.104
  25.9 0.6 %gather_fusion = f32[32,3]{1,0:T(8,128)S(1)} fusion(f32[3,256]{0,1:T(8,128)S(1)} %copy.102, s32[1024]{0:T(1024)S(1)} %pad_clamp_fusion), kind=kCustom, calls=%fused_computation | custom fusion | bytes 896 | tf_op jit(solution)/shard_map/gather | solution.py:148
  26.5 0.1 copy.103
  26.5 0.6 %gather_fusion.2 = f32[32,3]{1,0:T(8,128)S(1)} fusion(f32[3,256]{0,1:T(8,128)S(1)} %copy.104, s32[1024]{0:T(1024)S(1)} %pad_clamp_fusion), kind=kCustom, calls=%fused_computation.2 | custom fusion | bytes 896 | tf_op jit(solution)/shard_map/gather | solution.py:149
  27.1 0.1 copy.105
  27.2 0.3 collective-permute-done.2
  27.5 0.1 constant_dynamic-slice_fusion
  27.6 0.1 constant_dynamic-slice_fusion.2
  27.6 0.1 constant_dynamic-slice_fusion.1
  27.7 0.0 all-to-all-done
  27.7 0.2 fusion.81
  27.9 0.1 fusion.68
  28.0 7.3 %fusion.5 = (f32[128]{0:T(128)S(1)}, f32[128]{0:T(128)S(1)}, f32[128]{0:T(128)S(1)}, f32[128]{0:T(128)S(1)}, f32[128]{0:T(128)S(1)}, /*index=5*/f32[128]{0:T(128)S(1)}) fusion(f32[128]{0:T(128)S(1)} %get-tuple-element.72, f32[8192]{0:T(1024)S(1)} %bitcast.121, f32[128]{0:T(128)S(1)} %get-tuple-element.74, f32[8192]{0:T(1024)S(1)} %bitcast.129, ...), kind=kLoop, calls=%fused_computation.36 | loop fusion | flops 41942272 | bytes 235520 | tf_op jit(solution)/shard_map/reduce_sum | solution.py:63
  35.3 3.3 %collective-permute-start.3 = (f32[6,128]{1,0:T(8,128)S(1)}, f32[6,128]{1,0:T(8,128)S(1)}, u32[]{:S(2)}, u32[]{:S(2)}) collective-permute-start(f32[6,128]{1,0:T(8,128)S(1)} %stack.122), channel_id=1, source_target_pairs={{0,128},{32,160},{64,192},{96,224},{128,0},{160,32},{192,64},{224,... | collective-permute-start | bytes 9224 | tf_op jit(solution)/shard_map/ppermute | solution.py:15
  38.6 3.5 %fusion.22 = (f32[64]{0:T(128)S(1)}, f32[64]{0:T(128)S(1)}, f32[64]{0:T(128)S(1)}, f32[64]{0:T(128)S(1)}, f32[64]{0:T(128)S(1)}, /*index=5*/f32[64]{0:T(128)S(1)}) fusion(f32[64]{0:T(128)S(1)} %get-tuple-element.78, f32[8192]{0:T(1024)S(1)} %bitcast.122, f32[64]{0:T(128)S(1)} %get-tuple-element.80, f32[8192]{0:T(1024)S(1)} %bitcast.130, ...), kind=kLoop, calls=%fused_computation.84 | loop fusion | flops 20971136 | bytes 232448 | tf_op jit(solution)/shard_map/reduce_sum | solution.py:63
  42.1 2.7 %multiply_reduce_fusion = (f32[32]{0:T(128)S(1)}, f32[32]{0:T(128)S(1)}, f32[32]{0:T(128)S(1)}, f32[32]{0:T(128)S(1)}, f32[32]{0:T(128)S(1)}, /*index=5*/f32[32]...) fusion(f32[32]{0:T(128)S(1)} %get-tuple-element.60, ...), kind=kLoop, calls=%fused_computation.134 | loop fusion | flops 13893248 | bytes 264448 | tf_op jit(solution)/shard_map/reduce_sum | solution.py:71
  44.9 0.0 collective-permute-done.3
  44.9 0.1 dynamic-slice_add_fusion.1
  44.9 0.9 %collective-permute-start.4 = (f32[6,64]{1,0:T(8,128)S(1)}, f32[6,64]{1,0:T(8,128)S(1)}, u32[]{:S(2)}, u32[]{:S(2)}) collective-permute-start(f32[6,64]{1,0:T(8,128)S(1)} %dynamic-slice_add_fusion.1), channel_id=1, source_target_pairs={{0,64},{32,96},{64,0},{96,32},{128,192},{160,224},{192,128},{224,1... | collective-permute-start | bytes 4616 | tf_op jit(solution)/shard_map/ppermute | solution.py:15
  45.9 2.0 %fusion.39 = (f32[32]{0:T(128)S(1)}, f32[32]{0:T(128)S(1)}, f32[32]{0:T(128)S(1)}, f32[32]{0:T(128)S(1)}, f32[32]{0:T(128)S(1)}, /*index=5*/f32[32]{0:T(128)S(1)}) fusion(f32[32]{0:T(128)S(1)} %get-tuple-element.66, f32[32]{0:T(128)S(1)} %get-tuple-element.68, f32[8192]{0:T(1024)S(1)} %bitcast.124, f32[8192]{0:T(1024)S(1)} %bitcast.132, ...), kind=kLoop, calls=%fused_computation.109 | loop fusion | flops 10485568 | bytes 230912 | tf_op jit(solution)/shard_map/reduce_sum | solution.py:63
  47.9 0.9 %collective-permute-done.4 = f32[6,64]{1,0:T(8,128)S(1)} collective-permute-done((f32[6,64]{1,0:T(8,128)S(1)}, f32[6,64]{1,0:T(8,128)S(1)}, u32[]{:S(2)}, u32[]{:S(2)}) %collective-permute-start.4) | collective-permute-done | bytes 1568 | tf_op jit(solution)/shard_map/ppermute | solution.py:15
  48.8 0.1 dynamic-slice_add_fusion
  48.8 2.8 %collective-permute-start.5 = (f32[6,32]{1,0:T(8,128)S(1)}, f32[6,32]{1,0:T(8,128)S(1)}, u32[]{:S(2)}, u32[]{:S(2)}) collective-permute-start(f32[6,32]{1,0:T(8,128)S(1)} %dynamic-slice_add_fusion), channel_id=1, source_target_pairs={{0,32},{32,0},{64,96},{96,64},{128,160},{160,128},{192,224},{224,1... | collective-permute-start | bytes 2312 | tf_op jit(solution)/shard_map/ppermute | solution.py:15
  51.6 0.6 %stack.143 = f32[6,32]{1,0:T(8,128)} concatenate(f32[1,32]{1,0:T(1,128)S(1)} %bitcast.156, f32[1,32]{1,0:T(1,128)S(1)} %bitcast.150, f32[1,32]{1,0:T(1,128)S(1)} %bitcast.153, f32[1,32]{1,0:T(1,128)S(1)} %bitcast.144, f32[1,32]{1,0:T(1,128)S(1)} %bitcast.147, f32[1,32]{1,0:T(1,128)S(1)} %bitcast.141), dimensions={0} | concatenate | bytes 1536 | tf_op jit(solution)/shard_map/stack | solution.py:71
  52.2 1.7 %collective-permute-done.5 = f32[6,32]{1,0:T(8,128)S(1)} collective-permute-done((f32[6,32]{1,0:T(8,128)S(1)}, f32[6,32]{1,0:T(8,128)S(1)}, u32[]{:S(2)}, u32[]{:S(2)}) %collective-permute-start.5) | collective-permute-done | bytes 800 | tf_op jit(solution)/shard_map/ppermute | solution.py:15
  54.0 0.1 add_add_fusion
  54.0 0.0 copy-start.1
  54.1 0.6 %pad_maximum_fusion.1 = f32[6,32]{1,0:T(8,128)} fusion(f32[3,32]{1,0:T(4,128)S(1)} %fusion.76, f32[3,32]{1,0:T(4,128)S(1)} %fusion.79), kind=kLoop, calls=%fused_computation.159 | loop fusion | flops 192 | bytes 1536 | tf_op jit(solution)/shard_map/concatenate | solution.py:153
  54.7 0.0 copy-done.1
  (16 shorter events, 0.2 us)
Async XLA Ops:
  3.5 9.8 %copy-start.4 = (s32[32]{0:T(128)S(1)}, s32[32]{0:T(128)}, u32[]{:S(2)}) copy-start(s32[32]{0:T(128)} %param.15) | copy-start | bytes 388
  3.5 13.4 %copy-start = (f32[256]{0:T(256)S(1)}, f32[256]{0:T(256)}, u32[]{:S(2)}) copy-start(f32[256]{0:T(256)} %param.13) | copy-start | bytes 3076
  3.5 24.3 %all-to-all-start = ((f32[7,32,256]{2,0,1:T(8,128)}), f32[7,32,256]{2,0,1:T(8,128)S(1)}, u32[]{:S(2)}, u32[]{:S(2)}) async-start(f32[7,32,256]{2,0,1:T(8,128)} %broadcast_in_dim.9), calls=%async_computation | async-start | bytes 524288 | tf_op jit(solution)/shard_map/all_to_all | solution.py:34
  13.4 5.1 %collective-permute-start = (f32[6,32]{1,0:T(8,128)S(1)}, f32[6,32]{1,0:T(8,128)S(1)}, u32[]{:S(2)}, u32[]{:S(2)}) collective-permute-start(f32[6,32]{1,0:T(8,128)S(1)} %fusion.66), channel_id=1, source_target_pairs={{0,32},{32,0},{64,96},{96,64},{128,160},{160,128},{192,224},{224,1... | collective-permute-start | bytes 2312 | tf_op jit(solution)/shard_map/ppermute | solution.py:15
  16.9 0.7 %copy-start.5 = (s32[1,64]{1,0:T(1,128)S(1)}, s32[1,64]{1,0:T(1,128)}, u32[]{:S(2)}) copy-start(s32[1,64]{1,0:T(1,128)} %param.16) | copy-start | bytes 772
  16.9 8.7 %copy-start.2 = (f32[3,256]{1,0:T(4,128)S(1)}, f32[3,256]{1,0:T(4,128)}, u32[]{:S(2)}) copy-start(f32[3,256]{1,0:T(4,128)} %param.11) | copy-start | bytes 9220
  17.6 8.1 %copy-start.3 = (f32[3,256]{1,0:T(4,128)S(1)}, f32[3,256]{1,0:T(4,128)}, u32[]{:S(2)}) copy-start(f32[3,256]{1,0:T(4,128)} %param.12) | copy-start | bytes 9220
  18.6 3.6 %collective-permute-start.1 = (f32[6,64]{1,0:T(8,128)S(1)}, f32[6,64]{1,0:T(8,128)S(1)}, u32[]{:S(2)}, u32[]{:S(2)}) collective-permute-start(f32[6,64]{1,0:T(8,128)S(1)} %maximum_select_fusion.1), channel_id=1, source_target_pairs={{0,64},{32,96},{64,0},{96,32},{128,192},{160,224},{192,128},{224,1... | collective-permute-start | bytes 4616 | tf_op jit(solution)/shard_map/ppermute | solution.py:15
  22.3 5.1 %collective-permute-start.2 = (f32[6,128]{1,0:T(8,128)S(1)}, f32[6,128]{1,0:T(8,128)S(1)}, u32[]{:S(2)}, u32[]{:S(2)}) collective-permute-start(f32[6,128]{1,0:T(8,128)S(1)} %maximum_select_fusion.2), channel_id=1, source_target_pairs={{0,128},{32,160},{64,192},{96,224},{128,0},{160,32},{192,64},{224,... | collective-permute-start | bytes 9224 | tf_op jit(solution)/shard_map/ppermute | solution.py:15
  35.3 9.5 %collective-permute-start.3 = (f32[6,128]{1,0:T(8,128)S(1)}, f32[6,128]{1,0:T(8,128)S(1)}, u32[]{:S(2)}, u32[]{:S(2)}) collective-permute-start(f32[6,128]{1,0:T(8,128)S(1)} %stack.122), channel_id=1, source_target_pairs={{0,128},{32,160},{64,192},{96,224},{128,0},{160,32},{192,64},{224,... | collective-permute-start | bytes 9224 | tf_op jit(solution)/shard_map/ppermute | solution.py:15
  44.9 3.8 %collective-permute-start.4 = (f32[6,64]{1,0:T(8,128)S(1)}, f32[6,64]{1,0:T(8,128)S(1)}, u32[]{:S(2)}, u32[]{:S(2)}) collective-permute-start(f32[6,64]{1,0:T(8,128)S(1)} %dynamic-slice_add_fusion.1), channel_id=1, source_target_pairs={{0,64},{32,96},{64,0},{96,32},{128,192},{160,224},{192,128},{224,1... | collective-permute-start | bytes 4616 | tf_op jit(solution)/shard_map/ppermute | solution.py:15
  48.8 5.1 %collective-permute-start.5 = (f32[6,32]{1,0:T(8,128)S(1)}, f32[6,32]{1,0:T(8,128)S(1)}, u32[]{:S(2)}, u32[]{:S(2)}) collective-permute-start(f32[6,32]{1,0:T(8,128)S(1)} %dynamic-slice_add_fusion), channel_id=1, source_target_pairs={{0,32},{32,0},{64,96},{96,64},{128,160},{160,128},{192,224},{224,1... | collective-permute-start | bytes 2312 | tf_op jit(solution)/shard_map/ppermute | solution.py:15
  54.0 0.6 %copy-start.1 = (f32[6,32]{1,0:T(8,128)}, f32[6,32]{1,0:T(8,128)S(1)}, u32[]{:S(2)}) copy-start(f32[6,32]{1,0:T(8,128)S(1)} %add_add_fusion) | copy-start | bytes 2308

commit v10 on v9

--- a/solution.py
+++ b/solution.py
@@ -57,18 +57,27 @@
     return inv_cube, term_list
 
 
+def two_stage_sums(scaled, term_list, groups=2):
+    rows, width = scaled.shape
+    partial = jnp.stack(
+        [
+            jnp.sum((scaled * term).reshape(rows, groups, width // groups), axis=2)
+            for term in term_list
+        ]
+    )
+    return jnp.sum(lax.optimization_barrier(partial), axis=2)
+
+
 def pair_sums(targets, sources, weight):
     inv_cube, term_list = pair_terms(targets, sources)
     scaled = weight * inv_cube
-    return jnp.stack([jnp.sum(scaled * term, axis=1) for term in term_list])
+    return two_stage_sums(scaled, term_list)
 
 
 def pair_sums_split(targets, sources, far_weight, near_weight):
     inv_cube, term_list = pair_terms(targets, sources)
-    far_scaled = far_weight * inv_cube
-    near_scaled = near_weight * inv_cube
-    far = jnp.stack([jnp.sum(far_scaled * term, axis=1) for term in term_list])
-    near = jnp.stack([jnp.sum(near_scaled * term, axis=1) for term in term_list])
+    far = two_stage_sums(far_weight * inv_cube, term_list)
+    near = two_stage_sums(near_weight * inv_cube, term_list)
     return far, near
 
 

time: 55.4 us -> 58.8 us (1.061)
  waiting for transfers between devices: 5.74 us -> 8.2 us
    ppermute x6, waiting for transfers between devices: 5.74 us -> 8.2 us  [exchange(): return lax.ppermute(block, axis, [(i, i ^ bit) for i in range(size)])]
    another operation x5 -> x4, local copies, waits for them, and re-layouts: 0.71 us -> 0.03 us  [two_stage_sums(): jnp.stack([jnp.sum((scaled * term).reshape(rows, groups, width // groups)...]
    reduce_sum x4 -> x9, other arithmetic: 15.5 us -> 16.1 us  [the longest x4 16 us: two_stage_sums(): jnp.sum((scaled * term).reshape(rows, groups, width // groups), axis=2)]
  transfers between devices with their start and end apart: 7 -> 7, of which waited for: 5 -> 5; matrix products, arithmetic and copies ran while one was open for 22% -> 13% of each run, Pallas kernels for 0% -> 0%
where the time goes in v10:
time: 58.8 us; the launch traced here: 58.1 us
  starting transfers between devices  24.3 us (41%)
  other arithmetic  19.4 us (33%)
  waiting for transfers between devices  8.2 us (14%)
  local copies, waits for them, and re-layouts  4.41 us (8%)
  between operations  1.67 us (3%)
    reduce_sum x4, other arithmetic, two_stage_sums(): jnp.sum((scaled * term).reshape(rows, groups, width // groups), axis=2)  16 us
    ppermute x6, starting transfers between devices, exchange(): return lax.ppermute(block, axis, [(i, i ^ bit) for i in range(size)])  14.5 us
    all_to_all x1, starting transfers between devices, gather_all_to_all(): got = lax.all_to_all(spread, axis, 1, 1, tiled=True)  9.79 us
    ppermute x6, waiting for transfers between devices, exchange(): return lax.ppermute(block, axis, [(i, i ^ bit) for i in range(size)])  8.2 us
  transfers between devices with their start and end apart: 7, of which 5 were waited for; matrix products, arithmetic and copies ran while one was open for 13% of the time, Pallas kernels for 0%

profile of v10, /device:TPU:32, one launch (start us, length us, event | category | flops | bytes accessed | tf_op | source)
XLA Modules:
  0.0 58.1 jit_solution(7138777769362278671)
XLA Ops:
  0.6 0.7 %broadcast_multiply_fusion = f32[256]{0:T(256)S(1)} fusion(f32[256]{0:T(256)} %param.13), kind=kLoop, calls=%fused_computation.241 | loop fusion | flops 256 | bytes 2048 | tf_op jit(solution)/shard_map/mul | solution.py:98
  1.3 0.8 %multiply_add_fusion.1 = (f32[3,256]{1,0:T(4,128)S(1)}, f32[3,256]{1,0:T(4,128)S(1)}) fusion(f32[3,256]{1,0:T(4,128)} %param.9, f32[3,256]{1,0:T(4,128)} %param.10, f32[3,256]{1,0:T(4,128)} %param.12, f32[3,256]{1,0:T(4,128)} %param.11, f32[256]{0:T(256)} %param.13, f32[256]{0:T(256)S(1)} %broadcast_multiply_fusion), kind=kLoop, calls=%fused_computation.202 | loop fusion | flops 9216 | bytes 20480 | tf_op jit(solution)/shard_map/add | solution.py:95
  2.1 0.7 %pad_maximum_fusion = f32[7,256]{1,0:T(8,128)S(1)} fusion(f32[1,256]{1,0:T(1,128)} %bitcast.138, f32[3,256]{1,0:T(4,128)S(1)} %get-tuple-element.58, f32[3,256]{1,0:T(4,128)S(1)} %get-tuple-element.57), kind=kLoop, calls=%fused_computation.189 | loop fusion | flops 3584 | bytes 14336 | tf_op jit(solution)/shard_map/concatenate | solution.py:103
  2.8 0.7 %broadcast_in_dim.11 = f32[7,32,256]{2,0,1:T(8,128)} broadcast(f32[7,256]{1,0:T(8,128)S(1)} %pad_maximum_fusion), dimensions={0,2} | broadcast | bytes 236544 | tf_op jit(solution)/shard_map/broadcast_in_dim | solution.py:33
  3.5 0.0 copy-start.5
  3.5 0.0 copy-start.6
  3.5 0.0 copy-start
  3.5 9.8 %all-to-all-start = ((f32[7,32,256]{2,0,1:T(8,128)}), f32[7,32,256]{2,0,1:T(8,128)S(1)}, u32[]{:S(2)}, u32[]{:S(2)}) async-start(f32[7,32,256]{2,0,1:T(8,128)} %broadcast_in_dim.11), calls=%async_computation | async-start | bytes 524288 | tf_op jit(solution)/shard_map/all_to_all | solution.py:34
  13.3 0.0 copy-done.5
  13.3 0.2 fusion.66
  13.4 2.7 %collective-permute-start = (f32[6,32]{1,0:T(8,128)S(1)}, f32[6,32]{1,0:T(8,128)S(1)}, u32[]{:S(2)}, u32[]{:S(2)}) collective-permute-start(f32[6,32]{1,0:T(8,128)S(1)} %fusion.66), channel_id=1, source_target_pairs={{0,32},{32,0},{64,96},{96,64},{128,160},{160,128},{192,224},{224,1... | collective-permute-start | bytes 2312 | tf_op jit(solution)/shard_map/ppermute | solution.py:15
  16.9 0.0 copy-done.6
  16.9 0.1 fusion.70
  17.0 0.1 reshape.1622
  17.1 0.1 broadcast_bitcast_fusion
  17.2 0.0 copy-done
  17.2 0.0 copy-start.2
  17.2 0.7 %gather_fusion.1 = f32[32]{0:T(128)S(1)} fusion(f32[256]{0:T(256)S(1)} %copy-done, s32[1024]{0:T(1024)S(1)} %pad_clamp_fusion), kind=kCustom, calls=%fused_computation.1 | custom fusion | bytes 384 | tf_op jit(solution)/shard_map/gather | solution.py:156
  17.9 0.0 copy-start.3
  17.9 0.6 %collective-permute-done = f32[6,32]{1,0:T(8,128)S(1)} collective-permute-done((f32[6,32]{1,0:T(8,128)S(1)}, f32[6,32]{1,0:T(8,128)S(1)}, u32[]{:S(2)}, u32[]{:S(2)}) %collective-permute-start) | collective-permute-done | bytes 800 | tf_op jit(solution)/shard_map/ppermute | solution.py:15
  18.6 0.1 maximum_select_fusion.1
  18.6 1.6 %collective-permute-start.1 = (f32[6,64]{1,0:T(8,128)S(1)}, f32[6,64]{1,0:T(8,128)S(1)}, u32[]{:S(2)}, u32[]{:S(2)}) collective-permute-start(f32[6,64]{1,0:T(8,128)S(1)} %maximum_select_fusion.1), channel_id=1, source_target_pairs={{0,64},{32,96},{64,0},{96,32},{128,192},{160,224},{192,128},{224,1... | collective-permute-start | bytes 4616 | tf_op jit(solution)/shard_map/ppermute | solution.py:15
  20.2 2.0 %collective-permute-done.1 = f32[6,64]{1,0:T(8,128)S(1)} collective-permute-done((f32[6,64]{1,0:T(8,128)S(1)}, f32[6,64]{1,0:T(8,128)S(1)}, u32[]{:S(2)}, u32[]{:S(2)}) %collective-permute-start.1) | collective-permute-done | bytes 1568 | tf_op jit(solution)/shard_map/ppermute | solution.py:15
  22.3 0.1 maximum_select_fusion.2
  22.3 3.2 %collective-permute-start.2 = (f32[6,128]{1,0:T(8,128)S(1)}, f32[6,128]{1,0:T(8,128)S(1)}, u32[]{:S(2)}, u32[]{:S(2)}) collective-permute-start(f32[6,128]{1,0:T(8,128)S(1)} %maximum_select_fusion.2), channel_id=1, source_target_pairs={{0,128},{32,160},{64,192},{96,224},{128,0},{160,32},{192,64},{224,... | collective-permute-start | bytes 9224 | tf_op jit(solution)/shard_map/ppermute | solution.py:15
  25.6 0.0 copy-done.2
  25.6 0.1 copy.47
  25.7 0.0 copy-done.3
  25.7 0.1 copy.49
  25.9 0.6 gather_fusion
  26.4 0.1 copy.48
  26.5 0.6 gather_fusion.2
  27.1 0.1 copy.50
  27.2 0.3 collective-permute-done.2
  27.5 0.1 constant_dynamic-slice_fusion
  27.6 0.1 constant_dynamic-slice_fusion.2
  27.6 0.1 constant_dynamic-slice_fusion.1
  27.7 0.0 all-to-all-done
  27.7 0.6 %slice_reduce_fusion.1 = (f32[32,256]{1,0:T(8,128)S(1)}, f32[32,256]{1,0:T(8,128)S(1)}, f32[32,256]{1,0:T(8,128)S(1)}, f32[32,256]{1,0:T(8,128)S(1)}, f32[32,256...) fusion(f32[7,32,256]{2,0,1:T(8,128)S(1)} %all-to-all-done), kind=kLoop, calls=%fused_computation.179 | loop fusion | bytes 458752 | tf_op jit(solution)/shard_map/slice | solution.py:43
  28.6 2.7 %multiply_reduce_fusion = (f32[32,2]{0,1:T(2,128)S(1)}, f32[32,2]{0,1:T(2,128)S(1)}, f32[32,2]{0,1:T(2,128)S(1)}, f32[32,2]{0,1:T(2,128)S(1)}, f32[32,2]{0,1:T(2...) fusion(f32[32]{0:T(128)S(1)} %get-tuple-element.62, ...), kind=kLoop, calls=%fused_computation.134 | loop fusion | flops 13892864 | bytes 265984 | tf_op jit(solution)/shard_map/reduce_sum | solution.py:64
  31.3 2.0 %fusion.39 = (f32[32,2]{0,1:T(2,128)S(1)}, f32[32,2]{0,1:T(2,128)S(1)}, f32[32,2]{0,1:T(2,128)S(1)}, f32[32,2]{0,1:T(2,128)S(1)}, f32[32,2]{0,1:T(2,128)S(1)}, /*index=5*/f32[32,2]{0,1:T(2,128)S(1)}) fusion(f32[32]{0:T(128)S(1)} %get-tuple-element.68, f32[32]{0:T(128)S(1)} %get-tuple-element.70, f32[2,4096]{1,0:T(2,128)S(1)} %sub.607, ...), kind=kLoop, calls=%fused_computation.109 | loop fusion | flops 10485376 | bytes 231680 | tf_op jit(solution)/shard_map/reduce_sum | solution.py:64
  33.4 7.3 %fusion.5 = (f32[128,2]{0,1:T(2,128)S(1)}, f32[128,2]{0,1:T(2,128)S(1)}, f32[128,2]{0,1:T(2,128)S(1)}, f32[128,2]{0,1:T(2,128)S(1)}, f32[128,2]{0,1:T(2,128)S(1)}, /*index=5*/f32[128,2]{0,1:T(2,128)S(1)}) fusion(f32[128]{0:T(128)S(1)} %get-tuple-element.74, f32[2,4096]{1,0:T(2,128)S(1)} %sub.607, f32[128]{0:T(128)S(1)} %get-tuple-element.76, ...), kind=kLoop, calls=%fused_computation.36 | loop fusion | flops 41941504 | bytes 238592 | tf_op jit(solution)/shard_map/reduce_sum | solution.py:64
  40.8 3.5 %collective-permute-start.3 = (f32[6,128]{1,0:T(8,128)S(1)}, f32[6,128]{1,0:T(8,128)S(1)}, u32[]{:S(2)}, u32[]{:S(2)}) collective-permute-start(f32[6,128]{1,0:T(8,128)S(1)} %reduce_sum.328), channel_id=1, source_target_pairs={{0,128},{32,160},{64,192},{96,224},{128,0},{160,32},{192,64},{224,... | collective-permute-start | bytes 9224 | tf_op jit(solution)/shard_map/ppermute | solution.py:15
  44.3 3.9 %fusion.22 = (f32[64,2]{0,1:T(2,128)S(1)}, f32[64,2]{0,1:T(2,128)S(1)}, f32[64,2]{0,1:T(2,128)S(1)}, f32[64,2]{0,1:T(2,128)S(1)}, f32[64,2]{0,1:T(2,128)S(1)}, /*index=5*/f32[64,2]{0,1:T(2,128)S(1)}) fusion(f32[64]{0:T(128)S(1)} %get-tuple-element.80, f32[2,4096]{1,0:T(2,128)S(1)} %sub.607, f32[64]{0:T(128)S(1)} %get-tuple-element.82, ...), kind=kLoop, calls=%fused_computation.84 | loop fusion | flops 20970752 | bytes 233984 | tf_op jit(solution)/shard_map/reduce_sum | solution.py:64
  48.5 0.0 collective-permute-done.3
  48.5 0.1 dynamic-slice_add_fusion.1
  48.5 0.7 %collective-permute-start.4 = (f32[6,64]{1,0:T(8,128)S(1)}, f32[6,64]{1,0:T(8,128)S(1)}, u32[]{:S(2)}, u32[]{:S(2)}) collective-permute-start(f32[6,64]{1,0:T(8,128)S(1)} %dynamic-slice_add_fusion.1), channel_id=1, source_target_pairs={{0,64},{32,96},{64,0},{96,32},{128,192},{160,224},{192,128},{224,1... | collective-permute-start | bytes 4616 | tf_op jit(solution)/shard_map/ppermute | solution.py:15
  49.3 2.9 %collective-permute-done.4 = f32[6,64]{1,0:T(8,128)S(1)} collective-permute-done((f32[6,64]{1,0:T(8,128)S(1)}, f32[6,64]{1,0:T(8,128)S(1)}, u32[]{:S(2)}, u32[]{:S(2)}) %collective-permute-start.4) | collective-permute-done | bytes 1568 | tf_op jit(solution)/shard_map/ppermute | solution.py:15
  52.2 0.1 dynamic-slice_add_fusion
  52.2 2.8 %collective-permute-start.5 = (f32[6,32]{1,0:T(8,128)S(1)}, f32[6,32]{1,0:T(8,128)S(1)}, u32[]{:S(2)}, u32[]{:S(2)}) collective-permute-start(f32[6,32]{1,0:T(8,128)S(1)} %dynamic-slice_add_fusion), channel_id=1, source_target_pairs={{0,32},{32,0},{64,96},{96,64},{128,160},{160,128},{192,224},{224,1... | collective-permute-start | bytes 2312 | tf_op jit(solution)/shard_map/ppermute | solution.py:15
  55.1 0.0 copy-start.1
  55.1 2.3 %collective-permute-done.5 = f32[6,32]{1,0:T(8,128)S(1)} collective-permute-done((f32[6,32]{1,0:T(8,128)S(1)}, f32[6,32]{1,0:T(8,128)S(1)}, u32[]{:S(2)}, u32[]{:S(2)}) %collective-permute-start.5) | collective-permute-done | bytes 800 | tf_op jit(solution)/shard_map/ppermute | solution.py:15
  57.4 0.1 add_add_fusion
  57.5 0.0 copy-start.4
  57.5 0.6 %pad_maximum_fusion.1 = f32[6,32]{1,0:T(8,128)} fusion(f32[3,32]{1,0:T(4,128)S(1)} %get-tuple-element.60, f32[3,32]{1,0:T(4,128)S(1)} %get-tuple-element.59), kind=kLoop, calls=%fused_computation.197 | loop fusion | flops 192 | bytes 1536 | tf_op jit(solution)/shard_map/concatenate | solution.py:162
  58.1 0.0 copy-done.1
  58.1 0.0 copy-done.4
  (53 shorter events, 0.6 us)
Async XLA Ops:
  3.5 9.8 %copy-start.5 = (s32[32]{0:T(128)S(1)}, s32[32]{0:T(128)}, u32[]{:S(2)}) copy-start(s32[32]{0:T(128)} %param.15) | copy-start | bytes 388
  3.5 13.4 %copy-start.6 = (s32[1,64]{1,0:T(1,128)S(1)}, s32[1,64]{1,0:T(1,128)}, u32[]{:S(2)}) copy-start(s32[1,64]{1,0:T(1,128)} %param.16) | copy-start | bytes 772
  3.5 13.7 %copy-start = (f32[256]{0:T(256)S(1)}, f32[256]{0:T(256)}, u32[]{:S(2)}) copy-start(f32[256]{0:T(256)} %param.13) | copy-start | bytes 3076
  3.5 24.3 %all-to-all-start = ((f32[7,32,256]{2,0,1:T(8,128)}), f32[7,32,256]{2,0,1:T(8,128)S(1)}, u32[]{:S(2)}, u32[]{:S(2)}) async-start(f32[7,32,256]{2,0,1:T(8,128)} %broadcast_in_dim.11), calls=%async_computation | async-start | bytes 524288 | tf_op jit(solution)/shard_map/all_to_all | solution.py:34
  13.4 5.1 %collective-permute-start = (f32[6,32]{1,0:T(8,128)S(1)}, f32[6,32]{1,0:T(8,128)S(1)}, u32[]{:S(2)}, u32[]{:S(2)}) collective-permute-start(f32[6,32]{1,0:T(8,128)S(1)} %fusion.66), channel_id=1, source_target_pairs={{0,32},{32,0},{64,96},{96,64},{128,160},{160,128},{192,224},{224,1... | collective-permute-start | bytes 2312 | tf_op jit(solution)/shard_map/ppermute | solution.py:15
  17.2 8.4 %copy-start.2 = (f32[3,256]{1,0:T(4,128)S(1)}, f32[3,256]{1,0:T(4,128)}, u32[]{:S(2)}) copy-start(f32[3,256]{1,0:T(4,128)} %param.11) | copy-start | bytes 9220
  17.9 7.8 %copy-start.3 = (f32[3,256]{1,0:T(4,128)S(1)}, f32[3,256]{1,0:T(4,128)}, u32[]{:S(2)}) copy-start(f32[3,256]{1,0:T(4,128)} %param.12) | copy-start | bytes 9220
  18.6 3.6 %collective-permute-start.1 = (f32[6,64]{1,0:T(8,128)S(1)}, f32[6,64]{1,0:T(8,128)S(1)}, u32[]{:S(2)}, u32[]{:S(2)}) collective-permute-start(f32[6,64]{1,0:T(8,128)S(1)} %maximum_select_fusion.1), channel_id=1, source_target_pairs={{0,64},{32,96},{64,0},{96,32},{128,192},{160,224},{192,128},{224,1... | collective-permute-start | bytes 4616 | tf_op jit(solution)/shard_map/ppermute | solution.py:15
  22.3 5.1 %collective-permute-start.2 = (f32[6,128]{1,0:T(8,128)S(1)}, f32[6,128]{1,0:T(8,128)S(1)}, u32[]{:S(2)}, u32[]{:S(2)}) collective-permute-start(f32[6,128]{1,0:T(8,128)S(1)} %maximum_select_fusion.2), channel_id=1, source_target_pairs={{0,128},{32,160},{64,192},{96,224},{128,0},{160,32},{192,64},{224,... | collective-permute-start | bytes 9224 | tf_op jit(solution)/shard_map/ppermute | solution.py:15
  40.8 7.6 %collective-permute-start.3 = (f32[6,128]{1,0:T(8,128)S(1)}, f32[6,128]{1,0:T(8,128)S(1)}, u32[]{:S(2)}, u32[]{:S(2)}) collective-permute-start(f32[6,128]{1,0:T(8,128)S(1)} %reduce_sum.328), channel_id=1, source_target_pairs={{0,128},{32,160},{64,192},{96,224},{128,0},{160,32},{192,64},{224,... | collective-permute-start | bytes 9224 | tf_op jit(solution)/shard_map/ppermute | solution.py:15
  48.5 3.6 %collective-permute-start.4 = (f32[6,64]{1,0:T(8,128)S(1)}, f32[6,64]{1,0:T(8,128)S(1)}, u32[]{:S(2)}, u32[]{:S(2)}) collective-permute-start(f32[6,64]{1,0:T(8,128)S(1)} %dynamic-slice_add_fusion.1), channel_id=1, source_target_pairs={{0,64},{32,96},{64,0},{96,32},{128,192},{160,224},{192,128},{224,1... | collective-permute-start | bytes 4616 | tf_op jit(solution)/shard_map/ppermute | solution.py:15
  52.2 5.1 %collective-permute-start.5 = (f32[6,32]{1,0:T(8,128)S(1)}, f32[6,32]{1,0:T(8,128)S(1)}, u32[]{:S(2)}, u32[]{:S(2)}) collective-permute-start(f32[6,32]{1,0:T(8,128)S(1)} %dynamic-slice_add_fusion), channel_id=1, source_target_pairs={{0,32},{32,0},{64,96},{96,64},{128,160},{160,128},{192,224},{224,1... | collective-permute-start | bytes 2312 | tf_op jit(solution)/shard_map/ppermute | solution.py:15
  55.1 3.0 %copy-start.1 = (f32[6,32]{1,0:T(8,128)}, f32[6,32]{1,0:T(8,128)S(1)}, u32[]{:S(2)}) copy-start(f32[6,32]{1,0:T(8,128)S(1)} %reduce_sum.349) | copy-start | bytes 2308
  57.5 0.6 %copy-start.4 = (f32[6,32]{1,0:T(8,128)}, f32[6,32]{1,0:T(8,128)S(1)}, u32[]{:S(2)}) copy-start(f32[6,32]{1,0:T(8,128)S(1)} %add_add_fusion) | copy-start | bytes 2308

commit v11 on v9

--- a/solution.py
+++ b/solution.py
@@ -15,9 +15,9 @@
     return lax.ppermute(block, axis, [(i, i ^ bit) for i in range(size)])
 
 
-def gather_doubling(block, axis):
+def gather_doubling(block, axis, first=1):
     me = lax.axis_index(axis)
-    bit = 1
+    bit = first
     while bit < lax.axis_size(axis):
         got = exchange(block, axis, bit)
         upper = (me // bit) % 2 == 1
@@ -86,13 +86,27 @@
     moved_pos = position + elapsed * (
         velocity + elapsed * (0.5 * accel_old + elapsed * jerk_old / 6.0)
     )
-    turned = velocity + elapsed * (accel_old + 0.5 * elapsed * jerk_old)
+    turned = velocity + elapsed * (accel_old + 0.5 * (elapsed * jerk_old))
     sources = jnp.concatenate([moved_pos, turned], axis=0)
-    picks = (active_stars[None, :] == jnp.arange(sources.shape[1])[:, None]).astype(jnp.float32)
-    own_set = jnp.dot(sources, picks, precision=lax.Precision.HIGHEST)
+    res_dev = sources.shape[1]
     act_dev = active_stars.shape[0]
+
+    def select(block, index):
+        picks = (index[None, :] == jnp.arange(res_dev)[:, None]).astype(jnp.float32)
+        return jnp.dot(block, picks, precision=lax.Precision.HIGHEST)
+
+    own_set = select(sources, active_stars)
     block_data = jnp.concatenate([sources, masses[None, :]], axis=0)
-    targets = gather_doubling(own_set, "blk")
+    index_row = jnp.pad(active_stars.astype(jnp.float32), (0, res_dev - act_dev))
+    got = exchange(jnp.concatenate([sources, index_row[None, :]], 0), "blk", 1)
+    other_set = select(got[:6], got[6, :act_dev].astype(jnp.int32))
+    upper = lax.axis_index("blk") % 2 == 1
+    pair = jnp.where(
+        upper,
+        jnp.concatenate([other_set, own_set], 1),
+        jnp.concatenate([own_set, other_set], 1),
+    )
+    targets = gather_doubling(pair, "blk", first=2)
     group = gather_all_to_all(block_data, "grp")
     group_src = group[:6]
     group_mass = group[6]

time: 55.4 us -> 55.6 us (level)
    select_n x1, other arithmetic: 0.01 us -> 0.74 us  [per_device(): start_accel = accel_old.at[:, active_stars].get(mode='promise_in_bounds')]
    mul x1 -> x0, other arithmetic: 0.68 us -> none  [per_device(): turned = velocity + elapsed * (accel_old + 0.5 * elapsed * jerk_old)]
where the time goes in v11:
time: 55.6 us; the launch traced here: 54.9 us
  starting transfers between devices  24.3 us (44%)
  other arithmetic  18.9 us (34%)
  waiting for transfers between devices  5.61 us (10%)
  local copies, waits for them, and re-layouts  4.13 us (7%)
  between operations  1.56 us (3%)
    ppermute x6, starting transfers between devices, exchange(): return lax.ppermute(block, axis, [(i, i ^ bit) for i in range(size)])  14.6 us
    reduce_sum x3, other arithmetic, pair_sums(): return jnp.stack([jnp.sum(scaled * term, axis=1) for term in term_list])  12.8 us
    all_to_all x1, starting transfers between devices, gather_all_to_all(): got = lax.all_to_all(spread, axis, 1, 1, tiled=True)  9.79 us
    ppermute x6, waiting for transfers between devices, exchange(): return lax.ppermute(block, axis, [(i, i ^ bit) for i in range(size)])  5.61 us
    reduce_sum x1, other arithmetic, pair_sums_split(): jnp.sum(near_scaled * term, axis=1)  2.71 us
  transfers between devices with their start and end apart: 7, of which 5 were waited for; matrix products, arithmetic and copies ran while one was open for 22% of the time, Pallas kernels for 0%

profile of v11, /device:TPU:32, one launch (start us, length us, event | category | flops | bytes accessed | tf_op | source)
XLA Modules:
  0.0 54.9 jit_solution(11107327415151602801)
XLA Ops:
  0.6 0.7 %compare_select_fusion = (s32[32]{0:T(128)S(1)}, f32[32]{0:T(128)S(1)}) fusion(s32[32]{0:T(128)} %param.15), kind=kLoop, calls=%fused_computation.171 | loop fusion | flops 128 | bytes 384 | tf_op jit(solution)/shard_map/select_n | solution.py:162
  1.4 0.8 %multiply_add_fusion.1 = (f32[3,256]{1,0:T(4,128)S(1)}, f32[3,256]{1,0:T(4,128)S(1)}) fusion(f32[3,256]{1,0:T(4,128)} %param.9, f32[3,256]{1,0:T(4,128)} %param.10, f32[3,256]{1,0:T(4,128)} %param.11, f32[3,256]{1,0:T(4,128)} %param.12, f32[256]{0:T(256)} %param.13), kind=kLoop, calls=%fused_computation.170 | loop fusion | flops 9216 | bytes 19456 | tf_op jit(solution)/shard_map/add | solution.py:86
  2.1 0.7 %pad_maximum_fusion = (f32[7,256]{1,0:T(8,128)S(1)}, f32[7,256]{1,0:T(8,128)S(1)}) fusion(f32[1,256]{1,0:T(1,128)} %bitcast.163, f32[3,256]{1,0:T(4,128)S(1)} %get-tuple-element.58, f32[3,256]{1,0:T(4,128)S(1)} %get-tuple-element.57, f32[1,256]{1,0:T(1,128)S(1)} %bitcast.162), kind=kLoop, calls=%fused_computation.155 | loop fusion | flops 5376 | bytes 22528 | tf_op jit(solution)/shard_map/concatenate | solution.py:99
  2.8 0.7 %broadcast_in_dim.11 = f32[7,32,256]{2,0,1:T(8,128)} broadcast(f32[7,256]{1,0:T(8,128)S(1)} %get-tuple-element.59), dimensions={0,2} | broadcast | bytes 236544 | tf_op jit(solution)/shard_map/broadcast_in_dim | solution.py:33
  3.5 0.0 copy-start.4
  3.5 0.0 copy-start
  3.5 9.8 %all-to-all-start = ((f32[7,32,256]{2,0,1:T(8,128)}), f32[7,32,256]{2,0,1:T(8,128)S(1)}, u32[]{:S(2)}, u32[]{:S(2)}) async-start(f32[7,32,256]{2,0,1:T(8,128)} %broadcast_in_dim.11), calls=%async_computation | async-start | bytes 524288 | tf_op jit(solution)/shard_map/all_to_all | solution.py:34
  13.3 2.8 %collective-permute-start = (f32[7,256]{1,0:T(8,128)S(1)}, f32[7,256]{1,0:T(8,128)S(1)}, u32[]{:S(2)}, u32[]{:S(2)}) collective-permute-start(f32[7,256]{1,0:T(8,128)S(1)} %get-tuple-element.60), channel_id=1, source_target_pairs={{0,32},{32,0},{64,96},{96,64},{128,160},{160,128},{192,224},{224,1... | collective-permute-start | bytes 21512 | tf_op jit(solution)/shard_map/ppermute | solution.py:15
  16.1 0.0 copy-done.4
  16.2 0.2 fusion.66
  17.0 0.0 copy-done
  17.0 0.0 copy-start.5
  17.0 0.7 %gather_fusion.1 = f32[32]{0:T(128)S(1)} fusion(f32[256]{0:T(256)S(1)} %copy-done, s32[1024]{0:T(1024)S(1)} %pad_clamp_fusion), kind=kCustom, calls=%fused_computation.1 | custom fusion | bytes 384 | tf_op jit(solution)/shard_map/gather | solution.py:161
  17.7 0.0 copy-start.2
  17.7 0.0 copy-start.3
  17.8 0.0 copy-done.5
  17.8 0.1 fusion.72
  18.0 0.6 %collective-permute-done = f32[7,256]{1,0:T(8,128)S(1)} collective-permute-done((f32[7,256]{1,0:T(8,128)S(1)}, f32[7,256]{1,0:T(8,128)S(1)}, u32[]{:S(2)}, u32[]{:S(2)}) %collective-permute-start) | collective-permute-done | bytes 7200 | tf_op jit(solution)/shard_map/ppermute | solution.py:15
  18.6 0.2 fusion.67
  18.7 0.1 maximum_select_fusion.1
  18.8 1.6 %collective-permute-start.1 = (f32[6,64]{1,0:T(8,128)S(1)}, f32[6,64]{1,0:T(8,128)S(1)}, u32[]{:S(2)}, u32[]{:S(2)}) collective-permute-start(f32[6,64]{1,0:T(8,128)S(1)} %maximum_select_fusion.1), channel_id=1, source_target_pairs={{0,64},{32,96},{64,0},{96,32},{128,192},{160,224},{192,128},{224,1... | collective-permute-start | bytes 4616 | tf_op jit(solution)/shard_map/ppermute | solution.py:15
  20.4 2.0 %collective-permute-done.1 = f32[6,64]{1,0:T(8,128)S(1)} collective-permute-done((f32[6,64]{1,0:T(8,128)S(1)}, f32[6,64]{1,0:T(8,128)S(1)}, u32[]{:S(2)}, u32[]{:S(2)}) %collective-permute-start.1) | collective-permute-done | bytes 1568 | tf_op jit(solution)/shard_map/ppermute | solution.py:15
  22.5 0.1 maximum_select_fusion.2
  22.5 3.2 %collective-permute-start.2 = (f32[6,128]{1,0:T(8,128)S(1)}, f32[6,128]{1,0:T(8,128)S(1)}, u32[]{:S(2)}, u32[]{:S(2)}) collective-permute-start(f32[6,128]{1,0:T(8,128)S(1)} %maximum_select_fusion.2), channel_id=1, source_target_pairs={{0,128},{32,160},{64,192},{96,224},{128,0},{160,32},{192,64},{224,... | collective-permute-start | bytes 9224 | tf_op jit(solution)/shard_map/ppermute | solution.py:15
  25.7 0.0 copy-done.2
  25.8 0.1 copy.102
  25.9 0.0 copy-done.3
  25.9 0.1 copy.104
  26.1 0.6 %gather_fusion = f32[32,3]{1,0:T(8,128)S(1)} fusion(f32[3,256]{0,1:T(8,128)S(1)} %copy.102, s32[1024]{0:T(1024)S(1)} %pad_clamp_fusion), kind=kCustom, calls=%fused_computation | custom fusion | bytes 896 | tf_op jit(solution)/shard_map/gather | solution.py:162
  26.6 0.1 copy.103
  26.7 0.6 %gather_fusion.2 = f32[32,3]{1,0:T(8,128)S(1)} fusion(f32[3,256]{0,1:T(8,128)S(1)} %copy.104, s32[1024]{0:T(1024)S(1)} %pad_clamp_fusion), kind=kCustom, calls=%fused_computation.2 | custom fusion | bytes 896 | tf_op jit(solution)/shard_map/gather | solution.py:163
  27.3 0.1 copy.105
  27.4 0.3 collective-permute-done.2
  27.7 0.1 constant_dynamic-slice_fusion
  27.8 0.1 constant_dynamic-slice_fusion.2
  27.8 0.1 constant_dynamic-slice_fusion.1
  27.9 0.0 all-to-all-done
  27.9 0.2 fusion.85
  28.1 0.1 fusion.70
  28.2 7.3 %fusion.5 = (f32[128]{0:T(128)S(1)}, f32[128]{0:T(128)S(1)}, f32[128]{0:T(128)S(1)}, f32[128]{0:T(128)S(1)}, f32[128]{0:T(128)S(1)}, /*index=5*/f32[128]{0:T(128)S(1)}) fusion(f32[128]{0:T(128)S(1)} %get-tuple-element.74, f32[8192]{0:T(1024)S(1)} %bitcast.124, f32[128]{0:T(128)S(1)} %get-tuple-element.76, f32[8192]{0:T(1024)S(1)} %bitcast.132, ...), kind=kLoop, calls=%fused_computation.36 | loop fusion | flops 41942272 | bytes 235520 | tf_op jit(solution)/shard_map/reduce_sum | solution.py:63
  35.5 3.3 %collective-permute-start.3 = (f32[6,128]{1,0:T(8,128)S(1)}, f32[6,128]{1,0:T(8,128)S(1)}, u32[]{:S(2)}, u32[]{:S(2)}) collective-permute-start(f32[6,128]{1,0:T(8,128)S(1)} %stack.122), channel_id=1, source_target_pairs={{0,128},{32,160},{64,192},{96,224},{128,0},{160,32},{192,64},{224,... | collective-permute-start | bytes 9224 | tf_op jit(solution)/shard_map/ppermute | solution.py:15
  38.8 3.5 %fusion.22 = (f32[64]{0:T(128)S(1)}, f32[64]{0:T(128)S(1)}, f32[64]{0:T(128)S(1)}, f32[64]{0:T(128)S(1)}, f32[64]{0:T(128)S(1)}, /*index=5*/f32[64]{0:T(128)S(1)}) fusion(f32[64]{0:T(128)S(1)} %get-tuple-element.80, f32[8192]{0:T(1024)S(1)} %bitcast.125, f32[64]{0:T(128)S(1)} %get-tuple-element.82, f32[8192]{0:T(1024)S(1)} %bitcast.133, ...), kind=kLoop, calls=%fused_computation.84 | loop fusion | flops 20971136 | bytes 232448 | tf_op jit(solution)/shard_map/reduce_sum | solution.py:63
  42.3 2.7 %multiply_reduce_fusion = (f32[32]{0:T(128)S(1)}, f32[32]{0:T(128)S(1)}, f32[32]{0:T(128)S(1)}, f32[32]{0:T(128)S(1)}, f32[32]{0:T(128)S(1)}, /*index=5*/f32[32]...) fusion(f32[32]{0:T(128)S(1)} %get-tuple-element.62, ...), kind=kLoop, calls=%fused_computation.134 | loop fusion | flops 13893248 | bytes 264448 | tf_op jit(solution)/shard_map/reduce_sum | solution.py:71
  45.0 0.0 collective-permute-done.3
  45.1 0.1 dynamic-slice_add_fusion.1
  45.1 0.9 %collective-permute-start.4 = (f32[6,64]{1,0:T(8,128)S(1)}, f32[6,64]{1,0:T(8,128)S(1)}, u32[]{:S(2)}, u32[]{:S(2)}) collective-permute-start(f32[6,64]{1,0:T(8,128)S(1)} %dynamic-slice_add_fusion.1), channel_id=1, source_target_pairs={{0,64},{32,96},{64,0},{96,32},{128,192},{160,224},{192,128},{224,1... | collective-permute-start | bytes 4616 | tf_op jit(solution)/shard_map/ppermute | solution.py:15
  46.0 2.0 %fusion.39 = (f32[32]{0:T(128)S(1)}, f32[32]{0:T(128)S(1)}, f32[32]{0:T(128)S(1)}, f32[32]{0:T(128)S(1)}, f32[32]{0:T(128)S(1)}, /*index=5*/f32[32]{0:T(128)S(1)}) fusion(f32[32]{0:T(128)S(1)} %get-tuple-element.68, f32[32]{0:T(128)S(1)} %get-tuple-element.70, f32[8192]{0:T(1024)S(1)} %bitcast.127, f32[8192]{0:T(1024)S(1)} %bitcast.135, ...), kind=kLoop, calls=%fused_computation.109 | loop fusion | flops 10485568 | bytes 230912 | tf_op jit(solution)/shard_map/reduce_sum | solution.py:63
  48.0 0.9 %collective-permute-done.4 = f32[6,64]{1,0:T(8,128)S(1)} collective-permute-done((f32[6,64]{1,0:T(8,128)S(1)}, f32[6,64]{1,0:T(8,128)S(1)}, u32[]{:S(2)}, u32[]{:S(2)}) %collective-permute-start.4) | collective-permute-done | bytes 1568 | tf_op jit(solution)/shard_map/ppermute | solution.py:15
  48.9 0.1 dynamic-slice_add_fusion
  49.0 2.8 %collective-permute-start.5 = (f32[6,32]{1,0:T(8,128)S(1)}, f32[6,32]{1,0:T(8,128)S(1)}, u32[]{:S(2)}, u32[]{:S(2)}) collective-permute-start(f32[6,32]{1,0:T(8,128)S(1)} %dynamic-slice_add_fusion), channel_id=1, source_target_pairs={{0,32},{32,0},{64,96},{96,64},{128,160},{160,128},{192,224},{224,1... | collective-permute-start | bytes 2312 | tf_op jit(solution)/shard_map/ppermute | solution.py:15
  51.8 0.6 %stack.143 = f32[6,32]{1,0:T(8,128)} concatenate(f32[1,32]{1,0:T(1,128)S(1)} %bitcast.159, f32[1,32]{1,0:T(1,128)S(1)} %bitcast.153, f32[1,32]{1,0:T(1,128)S(1)} %bitcast.156, f32[1,32]{1,0:T(1,128)S(1)} %bitcast.147, f32[1,32]{1,0:T(1,128)S(1)} %bitcast.150, f32[1,32]{1,0:T(1,128)S(1)} %bitcast.144), dimensions={0} | concatenate | bytes 1536 | tf_op jit(solution)/shard_map/stack | solution.py:71
  52.4 1.7 %collective-permute-done.5 = f32[6,32]{1,0:T(8,128)S(1)} collective-permute-done((f32[6,32]{1,0:T(8,128)S(1)}, f32[6,32]{1,0:T(8,128)S(1)}, u32[]{:S(2)}, u32[]{:S(2)}) %collective-permute-start.5) | collective-permute-done | bytes 800 | tf_op jit(solution)/shard_map/ppermute | solution.py:15
  54.2 0.1 add_add_fusion
  54.2 0.0 copy-start.1
  54.3 0.6 %pad_maximum_fusion.3 = f32[6,32]{1,0:T(8,128)} fusion(f32[3,32]{1,0:T(4,128)S(1)} %fusion.79, f32[3,32]{1,0:T(4,128)S(1)} %fusion.82), kind=kLoop, calls=%fused_computation.165 | loop fusion | flops 192 | bytes 1536 | tf_op jit(solution)/shard_map/concatenate | solution.py:167
  54.9 0.0 copy-done.1
  (17 shorter events, 0.2 us)
Async XLA Ops:
  3.5 12.6 %copy-start.4 = (s32[32]{0:T(128)S(1)}, s32[32]{0:T(128)}, u32[]{:S(2)}) copy-start(s32[32]{0:T(128)} %param.15) | copy-start | bytes 388
  3.5 13.5 %copy-start = (f32[256]{0:T(256)S(1)}, f32[256]{0:T(256)}, u32[]{:S(2)}) copy-start(f32[256]{0:T(256)} %param.13) | copy-start | bytes 3076
  3.5 24.4 %all-to-all-start = ((f32[7,32,256]{2,0,1:T(8,128)}), f32[7,32,256]{2,0,1:T(8,128)S(1)}, u32[]{:S(2)}, u32[]{:S(2)}) async-start(f32[7,32,256]{2,0,1:T(8,128)} %broadcast_in_dim.11), calls=%async_computation | async-start | bytes 524288 | tf_op jit(solution)/shard_map/all_to_all | solution.py:34
  13.3 5.2 %collective-permute-start = (f32[7,256]{1,0:T(8,128)S(1)}, f32[7,256]{1,0:T(8,128)S(1)}, u32[]{:S(2)}, u32[]{:S(2)}) collective-permute-start(f32[7,256]{1,0:T(8,128)S(1)} %get-tuple-element.60), channel_id=1, source_target_pairs={{0,32},{32,0},{64,96},{96,64},{128,160},{160,128},{192,224},{224,1... | collective-permute-start | bytes 21512 | tf_op jit(solution)/shard_map/ppermute | solution.py:15
  17.0 0.7 %copy-start.5 = (s32[1,64]{1,0:T(1,128)S(1)}, s32[1,64]{1,0:T(1,128)}, u32[]{:S(2)}) copy-start(s32[1,64]{1,0:T(1,128)} %param.16) | copy-start | bytes 772
  17.7 8.0 %copy-start.2 = (f32[3,256]{1,0:T(4,128)S(1)}, f32[3,256]{1,0:T(4,128)}, u32[]{:S(2)}) copy-start(f32[3,256]{1,0:T(4,128)} %param.11) | copy-start | bytes 9220
  17.7 8.1 %copy-start.3 = (f32[3,256]{1,0:T(4,128)S(1)}, f32[3,256]{1,0:T(4,128)}, u32[]{:S(2)}) copy-start(f32[3,256]{1,0:T(4,128)} %param.12) | copy-start | bytes 9220
  18.8 3.6 %collective-permute-start.1 = (f32[6,64]{1,0:T(8,128)S(1)}, f32[6,64]{1,0:T(8,128)S(1)}, u32[]{:S(2)}, u32[]{:S(2)}) collective-permute-start(f32[6,64]{1,0:T(8,128)S(1)} %maximum_select_fusion.1), channel_id=1, source_target_pairs={{0,64},{32,96},{64,0},{96,32},{128,192},{160,224},{192,128},{224,1... | collective-permute-start | bytes 4616 | tf_op jit(solution)/shard_map/ppermute | solution.py:15
  22.5 5.1 %collective-permute-start.2 = (f32[6,128]{1,0:T(8,128)S(1)}, f32[6,128]{1,0:T(8,128)S(1)}, u32[]{:S(2)}, u32[]{:S(2)}) collective-permute-start(f32[6,128]{1,0:T(8,128)S(1)} %maximum_select_fusion.2), channel_id=1, source_target_pairs={{0,128},{32,160},{64,192},{96,224},{128,0},{160,32},{192,64},{224,... | collective-permute-start | bytes 9224 | tf_op jit(solution)/shard_map/ppermute | solution.py:15
  35.5 9.5 %collective-permute-start.3 = (f32[6,128]{1,0:T(8,128)S(1)}, f32[6,128]{1,0:T(8,128)S(1)}, u32[]{:S(2)}, u32[]{:S(2)}) collective-permute-start(f32[6,128]{1,0:T(8,128)S(1)} %stack.122), channel_id=1, source_target_pairs={{0,128},{32,160},{64,192},{96,224},{128,0},{160,32},{192,64},{224,... | collective-permute-start | bytes 9224 | tf_op jit(solution)/shard_map/ppermute | solution.py:15
  45.1 3.8 %collective-permute-start.4 = (f32[6,64]{1,0:T(8,128)S(1)}, f32[6,64]{1,0:T(8,128)S(1)}, u32[]{:S(2)}, u32[]{:S(2)}) collective-permute-start(f32[6,64]{1,0:T(8,128)S(1)} %dynamic-slice_add_fusion.1), channel_id=1, source_target_pairs={{0,64},{32,96},{64,0},{96,32},{128,192},{160,224},{192,128},{224,1... | collective-permute-start | bytes 4616 | tf_op jit(solution)/shard_map/ppermute | solution.py:15
  49.0 5.1 %collective-permute-start.5 = (f32[6,32]{1,0:T(8,128)S(1)}, f32[6,32]{1,0:T(8,128)S(1)}, u32[]{:S(2)}, u32[]{:S(2)}) collective-permute-start(f32[6,32]{1,0:T(8,128)S(1)} %dynamic-slice_add_fusion), channel_id=1, source_target_pairs={{0,32},{32,0},{64,96},{96,64},{128,160},{160,128},{192,224},{224,1... | collective-permute-start | bytes 2312 | tf_op jit(solution)/shard_map/ppermute | solution.py:15
  54.2 0.6 %copy-start.1 = (f32[6,32]{1,0:T(8,128)}, f32[6,32]{1,0:T(8,128)S(1)}, u32[]{:S(2)}) copy-start(f32[6,32]{1,0:T(8,128)S(1)} %add_add_fusion) | copy-start | bytes 2308
